TPU v7x, 32 devices: a whole 2x2x4 slice. The times are simulated.
32 devices in a mesh: group: 2 (over x), seq: 16 (over z, y, core).
Axes of the slice: x: 2, y: 2, z: 4, core: 2. Of those that a mesh axis runs over, the one named last changes fastest.
Arguments:
- queries: bfloat16 [4, 2048, 4096], P('group', 'seq'), parts along dimension 0, may hold values from -32 to 32
- key_vectors: bfloat16 [4, 2048, 4096], P('group', 'seq'), parts along dimension 0, may hold values from -24 to 24
- value_vectors: bfloat16 [4, 2048, 4096], P('group', 'seq'), parts along dimension 0, may hold values from -6 to 6
- out_grad: bfloat16 [4, 2048, 4096], P('group', 'seq'), parts along dimension 0, may hold values from -6 to 6
Outputs:
- grad_queries: bfloat16 [4, 2048, 4096], P('group', 'seq'), parts along dimension 0
- grad_keys: bfloat16 [4, 2048, 4096], P('group', 'seq'), parts along dimension 0
- grad_values: bfloat16 [4, 2048, 4096], P('group', 'seq'), parts along dimension 0
There are 2 independent parts, one for each index of `group`. A program takes and returns all parts, laid end to end along the dimension named above; each array names one. Nothing has to cross between parts.
All inputs are finite; a program needn't handle non-finite values.
Results may differ from a plain program's by a relative error of at most 0.0052.
Values may be sent and summed in bfloat16 or wider, within the bound.
No kernel may reach another device: no remote copies, remote signals or barrier semaphores. Data moves between devices by JAX's collectives and lax.ppermute only.
A program may use at most 128 MiB of HBM per device.

v0:
```python
import jax
import jax.numpy as jnp
from jax import lax
from jax.sharding import PartitionSpec as P

HEADS = 32


def shortened(array):
    return jax.tree.map(lambda a: a.astype(jnp.bfloat16) if a.dtype == jnp.float32 else a, array)


def item_gradients(operands):
    queries, key_vectors, value_vectors, out_grad = operands
    tokens_all, head_width = queries.shape
    score_scale = head_width ** (-0.5)
    block_rows = min(512, tokens_all)
    grad_keys = jnp.zeros((tokens_all, head_width), jnp.float32)
    grad_values = jnp.zeros((tokens_all, head_width), jnp.float32)
    query_parts = []
    for block_index in range(tokens_all // block_rows):
        row_start = block_index * block_rows
        row_stop = row_start + block_rows
        query_block = queries[row_start:row_stop]
        grad_block = out_grad[row_start:row_stop]
        key_prefix = key_vectors[:row_stop]
        value_prefix = value_vectors[:row_stop]
        scores = (
            jnp.dot(query_block, key_prefix.T, preferred_element_type=jnp.float32) * score_scale
        )
        row_ids = row_start + lax.broadcasted_iota(jnp.int32, (block_rows, row_stop), 0)
        col_ids = lax.broadcasted_iota(jnp.int32, (block_rows, row_stop), 1)
        scores = jnp.where(row_ids >= col_ids, scores, -jnp.inf)
        row_top = jnp.max(scores, axis=1, keepdims=True)
        weights = jnp.exp(scores - row_top)
        softmax_rows = weights / jnp.sum(weights, axis=1, keepdims=True)
        probs_low = softmax_rows.astype(jnp.bfloat16)
        dprobs = jnp.dot(grad_block, value_prefix.T, preferred_element_type=jnp.float32)
        row_delta = jnp.sum(softmax_rows * dprobs, axis=1, keepdims=True)
        dscores = (softmax_rows * (dprobs - row_delta)).astype(jnp.bfloat16)
        value_terms = jnp.dot(probs_low.T, grad_block, preferred_element_type=jnp.float32)
        grad_values = grad_values.at[:row_stop].add(value_terms)
        key_terms = (
            jnp.dot(dscores.T, query_block, preferred_element_type=jnp.float32) * score_scale
        )
        grad_keys = grad_keys.at[:row_stop].add(key_terms)
        query_terms = jnp.dot(dscores, key_prefix, preferred_element_type=jnp.float32) * score_scale
        query_parts.append(query_terms.astype(jnp.bfloat16))
    grad_queries = jnp.concatenate(query_parts, axis=0)
    return (grad_queries, grad_keys.astype(jnp.bfloat16), grad_values.astype(jnp.bfloat16))


def head_gradients(queries, key_vectors, value_vectors, out_grad):
    page_count, tokens_all, local_heads, head_width = queries.shape

    def to_items(operand):
        return jnp.moveaxis(operand, 2, 1).reshape(page_count * local_heads, tokens_all, head_width)

    def from_items(operand):
        return jnp.moveaxis(operand.reshape(page_count, local_heads, tokens_all, head_width), 1, 2)

    results = lax.map(
        item_gradients,
        (to_items(queries), to_items(key_vectors), to_items(value_vectors), to_items(out_grad)),
    )
    return (from_items(results[0]), from_items(results[1]), from_items(results[2]))


def body(queries, key_vectors, value_vectors, out_grad):
    page_count, tok_rows, feature_width = queries.shape
    head_width = feature_width // HEADS
    query_heads = queries.reshape(page_count, tok_rows, HEADS, head_width)
    key_heads = key_vectors.reshape(page_count, tok_rows, HEADS, head_width)
    value_heads = value_vectors.reshape(page_count, tok_rows, HEADS, head_width)
    grad_heads = out_grad.reshape(page_count, tok_rows, HEADS, head_width)
    arrived = (
        lax.all_to_all(query_heads, "seq", split_axis=2, concat_axis=1, tiled=True),
        lax.all_to_all(key_heads, "seq", split_axis=2, concat_axis=1, tiled=True),
        lax.all_to_all(value_heads, "seq", split_axis=2, concat_axis=1, tiled=True),
        lax.all_to_all(grad_heads, "seq", split_axis=2, concat_axis=1, tiled=True),
    )
    results = head_gradients(arrived[0], arrived[1], arrived[2], arrived[3])
    returned = (
        lax.all_to_all(shortened(results[0]), "seq", split_axis=1, concat_axis=2, tiled=True),
        lax.all_to_all(results[1], "seq", split_axis=1, concat_axis=2, tiled=True),
        lax.all_to_all(results[2], "seq", split_axis=1, concat_axis=2, tiled=True),
    )
    return (
        returned[0].reshape(page_count, tok_rows, feature_width),
        returned[1].reshape(page_count, tok_rows, feature_width),
        returned[2].reshape(page_count, tok_rows, feature_width),
    )


def solution(mesh):
    placed = (
        P("group", "seq", None),
        P("group", "seq", None),
        P("group", "seq", None),
        P("group", "seq", None),
    )
    return jax.shard_map(
        body,
        mesh=mesh,
        in_specs=placed,
        out_specs=(P("group", "seq", None), P("group", "seq", None), P("group", "seq", None)),
        check_vma=False,
    )
```

profile of v0, /device:TPU:13, one launch (start us, length us, event | category | flops | bytes accessed | tf_op | source)
XLA Modules:
  0.0 511.8 jit_solution(13454407848001196836)
XLA Ops:
  0.6 3.1 copy.57
  3.8 2.7 copy.58
  6.5 6.5 %all-to-all-start = ((bf16[2,128,32,128]{3,1,0,2:T(8,128)(2,1)}), bf16[2,128,32,128]{3,1,0,2:T(8,128)(2,1)S(1)}, u32[]{:S(2)}, u32[]{:S(2)}) async-start(bf16[2,128,32,128]{3,1,0,2:T(8,128)(2,1)} %copy.58), calls=%async_computation | async-start | bytes 4194304 | tf_op jit(solution)/shard_map/all_to_all | solution.py:77
  13.0 4.1 copy.61
  17.1 4.1 copy.62
  21.2 39.3 %all-to-all-done = bf16[2,128,32,128]{3,1,0,2:T(8,128)(2,1)S(1)} async-done(((bf16[2,128,32,128]{3,1,0,2:T(8,128)(2,1)}), bf16[2,128,32,128]{3,1,0,2:T(8,128)(2,1)S(1)}, u32[]{:S(2)}, u32[]{:S(2)}) %all-to-all-start) | async-done | bytes 2097184 | tf_op jit(solution)/shard_map/all_to_all | solution.py:77
  60.4 4.8 all-to-all-start.1
  65.2 4.1 copy.69
  69.3 4.1 copy.70
  73.4 39.4 %all-to-all-done.1 = bf16[2,128,32,128]{3,1,0,2:T(8,128)(2,1)} async-done(((bf16[2,128,32,128]{3,1,0,2:T(8,128)(2,1)}), bf16[2,128,32,128]{3,1,0,2:T(8,128)(2,1)}, u32[]{:S(2)}, u32[]{:S(2)}) %all-to-all-start.1) | async-done | bytes 2097184 | tf_op jit(solution)/shard_map/all_to_all | solution.py:78
  112.7 4.8 all-to-all-start.3
  117.5 4.1 copy.65
  121.6 4.1 copy.66
  125.7 39.4 %all-to-all-done.3 = bf16[2,128,32,128]{3,1,0,2:T(8,128)(2,1)} async-done(((bf16[2,128,32,128]{3,1,0,2:T(8,128)(2,1)}), bf16[2,128,32,128]{3,1,0,2:T(8,128)(2,1)}, u32[]{:S(2)}, u32[]{:S(2)}) %all-to-all-start.3) | async-done | bytes 2097184 | tf_op jit(solution)/shard_map/all_to_all | solution.py:79
  165.0 4.8 all-to-all-start.2
  173.3 3.1 copy.72
  176.4 40.9 %all-to-all-done.2 = bf16[2,128,32,128]{3,1,0,2:T(8,128)(2,1)} async-done(((bf16[2,128,32,128]{3,1,0,2:T(8,128)(2,1)}), bf16[2,128,32,128]{3,1,0,2:T(8,128)(2,1)}, u32[]{:S(2)}, u32[]{:S(2)}) %all-to-all-start.2) | async-done | bytes 2097184 | tf_op jit(solution)/shard_map/all_to_all | solution.py:80
  217.4 3.2 copy.68
  220.5 121.2 %while.27 = (s32[]{:T(128)}, bf16[4,2048,128]{2,1,0:T(8,128)(2,1)}, bf16[4,2048,128]{2,1,0:T(8,128)(2,1)}, bf16[4,2048,128]{2,1,0:T(8,128)(2,1)}, bf16[4,2048,12...) while((s32[]{:T(128)}, bf16[4,2048,128]{2,1,0:T(8,128)(2,1)}, ...), condition=%wide.region_13.14_spmd, body=%wide.region_0.13_spmd.sunk | while | flops 3407605248 | bytes 125159704 | solution.py:62
  239.3 1.9 fusion.125
  241.9 2.3 fusion.144
  247.5 2.5 fusion.140
  269.6 1.9 fusion.125
  272.2 2.3 fusion.144
  277.8 2.5 fusion.140
  299.9 1.9 fusion.125
  302.5 2.3 fusion.144
  308.1 2.5 fusion.140
  330.2 1.9 fusion.125
  332.8 2.3 fusion.144
  338.4 2.5 fusion.140
  341.7 4.7 copy.79
  346.4 4.8 all-to-all-start.6
  351.2 4.6 copy.73
  355.9 42.8 %all-to-all-done.6 = bf16[2,2048,2,128]{3,2,0,1:T(2,128)(2,1)S(1)} async-done(((bf16[2,2048,2,128]{3,2,0,1:T(2,128)(2,1)}), bf16[2,2048,2,128]{3,2,0,1:T(2,128)(2,1)S(1)}, u32[]{:S(2)}, u32[]{:S(2)}) %all-to-all-start.6) | async-done | bytes 2097184 | tf_op jit(solution)/shard_map/all_to_all | solution.py:86
  398.6 4.8 all-to-all-start.4
  403.4 4.7 copy.76
  408.1 42.8 %all-to-all-done.4 = bf16[2,2048,2,128]{3,2,0,1:T(2,128)(2,1)} async-done(((bf16[2,2048,2,128]{3,2,0,1:T(2,128)(2,1)}), bf16[2,2048,2,128]{3,2,0,1:T(2,128)(2,1)}, u32[]{:S(2)}, u32[]{:S(2)}) %all-to-all-start.4) | async-done | bytes 2097184 | tf_op jit(solution)/shard_map/all_to_all | solution.py:84
  450.9 4.8 all-to-all-start.5
  457.3 3.0 copy.81
  460.4 2.7 copy.84
  463.1 1.9 copy.74
  464.9 2.6 copy.75
  467.5 4.1 copy.82
  471.6 31.6 %all-to-all-done.5 = bf16[2,2048,2,128]{3,2,0,1:T(2,128)(2,1)} async-done(((bf16[2,2048,2,128]{3,2,0,1:T(2,128)(2,1)}), bf16[2,2048,2,128]{3,2,0,1:T(2,128)(2,1)}, u32[]{:S(2)}, u32[]{:S(2)}) %all-to-all-start.5) | async-done | bytes 2097184 | tf_op jit(solution)/shard_map/all_to_all | solution.py:85
  503.2 1.9 copy.77
  505.1 2.6 copy.78
  507.7 4.1 copy.83
  (146 shorter events, 99.3 us)
Async XLA Ops:
  6.5 53.9 %all-to-all-start = ((bf16[2,128,32,128]{3,1,0,2:T(8,128)(2,1)}), bf16[2,128,32,128]{3,1,0,2:T(8,128)(2,1)S(1)}, u32[]{:S(2)}, u32[]{:S(2)}) async-start(bf16[2,128,32,128]{3,1,0,2:T(8,128)(2,1)} %copy.58), calls=%async_computation | async-start | bytes 4194304 | tf_op jit(solution)/shard_map/all_to_all | solution.py:77
  60.4 52.3 %all-to-all-start.1 = ((bf16[2,128,32,128]{3,1,0,2:T(8,128)(2,1)}), bf16[2,128,32,128]{3,1,0,2:T(8,128)(2,1)}, u32[]{:S(2)}, u32[]{:S(2)}) async-start(bf16[2,128,32,128]{3,1,0,2:T(8,128)(2,1)} %copy.62), calls=%async_computation.1 | async-start | bytes 4194304 | tf_op jit(solution)/shard_map/all_to_all | solution.py:78
  112.7 52.3 %all-to-all-start.3 = ((bf16[2,128,32,128]{3,1,0,2:T(8,128)(2,1)}), bf16[2,128,32,128]{3,1,0,2:T(8,128)(2,1)}, u32[]{:S(2)}, u32[]{:S(2)}) async-start(bf16[2,128,32,128]{3,1,0,2:T(8,128)(2,1)} %copy.70), calls=%async_computation.3 | async-start | bytes 4194304 | tf_op jit(solution)/shard_map/all_to_all | solution.py:79
  165.0 52.3 %all-to-all-start.2 = ((bf16[2,128,32,128]{3,1,0,2:T(8,128)(2,1)}), bf16[2,128,32,128]{3,1,0,2:T(8,128)(2,1)}, u32[]{:S(2)}, u32[]{:S(2)}) async-start(bf16[2,128,32,128]{3,1,0,2:T(8,128)(2,1)} %copy.66), calls=%async_computation.2 | async-start | bytes 4194304 | tf_op jit(solution)/shard_map/all_to_all | solution.py:80
  220.5 1.7 copy-start.1
  222.2 1.6 copy-start
  250.8 1.7 copy-start.1
  252.5 1.6 copy-start
  281.1 1.7 copy-start.1
  282.8 1.6 copy-start
  311.4 1.7 copy-start.1
  313.1 1.6 copy-start
  346.4 52.2 %all-to-all-start.6 = ((bf16[2,2048,2,128]{3,2,0,1:T(2,128)(2,1)}), bf16[2,2048,2,128]{3,2,0,1:T(2,128)(2,1)S(1)}, u32[]{:S(2)}, u32[]{:S(2)}) async-start(bf16[2,2048,2,128]{3,2,0,1:T(2,128)(2,1)} %bitcast.253), calls=%async_computation.6 | async-start | bytes 4194304 | tf_op jit(solution)/shard_map/all_to_all | solution.py:86
  398.6 52.3 %all-to-all-start.4 = ((bf16[2,2048,2,128]{3,2,0,1:T(2,128)(2,1)}), bf16[2,2048,2,128]{3,2,0,1:T(2,128)(2,1)}, u32[]{:S(2)}, u32[]{:S(2)}) async-start(bf16[2,2048,2,128]{3,2,0,1:T(2,128)(2,1)} %bitcast.252), calls=%async_computation.4 | async-start | bytes 4194304 | tf_op jit(solution)/shard_map/all_to_all | solution.py:84
  450.9 52.3 %all-to-all-start.5 = ((bf16[2,2048,2,128]{3,2,0,1:T(2,128)(2,1)}), bf16[2,2048,2,128]{3,2,0,1:T(2,128)(2,1)}, u32[]{:S(2)}, u32[]{:S(2)}) async-start(bf16[2,2048,2,128]{3,2,0,1:T(2,128)(2,1)} %bitcast.251), calls=%async_computation.5 | async-start | bytes 4194304 | tf_op jit(solution)/shard_map/all_to_all | solution.py:85
where the time goes:
time: 514 us; the launch traced here: 512 us
  waiting for transfers between devices  276 us (54%)
  matrix products  91.7 us (18%)
  local copies, waits for them, and re-layouts  84.1 us (16%)
  starting transfers between devices  35.2 us (7%)
  other arithmetic  23.4 us (5%)
    all_to_all x1, waiting for transfers between devices, body(): lax.all_to_all(shortened(results[0]), 'seq', split_axis=1, concat_axis=2,...  42.8 us
    all_to_all x1, waiting for transfers between devices, body(): lax.all_to_all(results[2], 'seq', split_axis=1, concat_axis=2, tiled=True)  42.8 us
    all_to_all x1, waiting for transfers between devices, body(): lax.all_to_all(grad_heads, 'seq', split_axis=2, concat_axis=1, tiled=True)  40.9 us
    all_to_all x1, waiting for transfers between devices, body(): lax.all_to_all(value_heads, 'seq', split_axis=2, concat_axis=1, tiled=True)  39.4 us
    all_to_all x1, waiting for transfers between devices, body(): lax.all_to_all(key_heads, 'seq', split_axis=2, concat_axis=1, tiled=True)  39.4 us
    all_to_all x1, waiting for transfers between devices, body(): lax.all_to_all(query_heads, 'seq', split_axis=2, concat_axis=1, tiled=True)  39.3 us
    all_to_all x1, waiting for transfers between devices, body(): lax.all_to_all(results[1], 'seq', split_axis=1, concat_axis=2, tiled=True)  31.6 us
    dot_general x16, matrix products, item_gradients(): jnp.dot(dscores.T, query_block, preferred_element_type=jnp.float32)  27 us
  transfers between devices with their start and end apart: 7, of which 7 were waited for; matrix products, arithmetic and copies ran while one was open for 11% of the time, Pallas kernels for 0%

commit v1 on v0

v1 whole, which is shorter than its diff:
```python
import jax
import jax.numpy as jnp
from jax import lax
from jax.sharding import PartitionSpec as P

HEADS = 32


def item_gradients(queries, key_vectors, value_vectors, out_grad):
    tokens_all, head_width = queries.shape
    score_scale = head_width ** (-0.5)
    block_rows = min(512, tokens_all)
    grad_keys = jnp.zeros((tokens_all, head_width), jnp.float32)
    grad_values = jnp.zeros((tokens_all, head_width), jnp.float32)
    query_parts = []
    for block_index in range(tokens_all // block_rows):
        row_start = block_index * block_rows
        row_stop = row_start + block_rows
        query_block = queries[row_start:row_stop]
        grad_block = out_grad[row_start:row_stop]
        key_prefix = key_vectors[:row_stop]
        value_prefix = value_vectors[:row_stop]
        scores = (
            jnp.dot(query_block, key_prefix.T, preferred_element_type=jnp.float32) * score_scale
        )
        row_ids = row_start + lax.broadcasted_iota(jnp.int32, (block_rows, row_stop), 0)
        col_ids = lax.broadcasted_iota(jnp.int32, (block_rows, row_stop), 1)
        scores = jnp.where(row_ids >= col_ids, scores, -jnp.inf)
        row_top = jnp.max(scores, axis=1, keepdims=True)
        weights = jnp.exp(scores - row_top)
        softmax_rows = weights / jnp.sum(weights, axis=1, keepdims=True)
        probs_low = softmax_rows.astype(jnp.bfloat16)
        dprobs = jnp.dot(grad_block, value_prefix.T, preferred_element_type=jnp.float32)
        row_delta = jnp.sum(softmax_rows * dprobs, axis=1, keepdims=True)
        dscores = (softmax_rows * (dprobs - row_delta)).astype(jnp.bfloat16)
        value_terms = jnp.dot(probs_low.T, grad_block, preferred_element_type=jnp.float32)
        grad_values = grad_values.at[:row_stop].add(value_terms)
        key_terms = (
            jnp.dot(dscores.T, query_block, preferred_element_type=jnp.float32) * score_scale
        )
        grad_keys = grad_keys.at[:row_stop].add(key_terms)
        query_terms = jnp.dot(dscores, key_prefix, preferred_element_type=jnp.float32) * score_scale
        query_parts.append(query_terms.astype(jnp.bfloat16))
    grad_queries = jnp.concatenate(query_parts, axis=0)
    return grad_queries, grad_keys.astype(jnp.bfloat16), grad_values.astype(jnp.bfloat16)


def body(queries, key_vectors, value_vectors, out_grad):
    page_count, tok_rows, feature_width = queries.shape
    seq_size = lax.psum(1, "seq")
    head_width = feature_width // HEADS
    per_dev = HEADS // seq_size
    stacked = jnp.stack([queries, key_vectors, value_vectors, out_grad]).reshape(
        4, page_count, tok_rows, seq_size, per_dev, head_width
    )
    chunk_out = {}
    for page in range(page_count):
        for head in range(per_dev):
            part = stacked[:, page, :, :, head, :]
            arrived = lax.all_to_all(part, "seq", split_axis=2, concat_axis=1, tiled=True)
            arrived = arrived.reshape(4, seq_size * tok_rows, head_width)
            grads = item_gradients(arrived[0], arrived[1], arrived[2], arrived[3])
            grads = jnp.stack(grads).reshape(3, seq_size, tok_rows, 1, head_width)
            returned = lax.all_to_all(grads, "seq", split_axis=1, concat_axis=3, tiled=True)
            chunk_out[(page, head)] = returned.reshape(3, tok_rows, seq_size, head_width)
    pages = []
    for page in range(page_count):
        pages.append(jnp.stack([chunk_out[(page, head)] for head in range(per_dev)], axis=3))
    result = jnp.stack(pages, axis=1).reshape(3, page_count, tok_rows, feature_width)
    return result[0], result[1], result[2]


def solution(mesh):
    placed = P("group", "seq", None)
    return jax.shard_map(
        body,
        mesh=mesh,
        in_specs=(placed, placed, placed, placed),
        out_specs=(placed, placed, placed),
        check_vma=False,
    )
```

time: 514 us -> 470 us (0.914)
  waiting for transfers between devices: 276 us -> 228 us
  matrix products: 91.7 us -> 68.1 us
  other arithmetic: 23.4 us -> 35.5 us
  starting transfers between devices: 35.2 us -> 42.8 us
    all_to_all x7 -> x8, waiting for transfers between devices: 276 us -> 228 us  [the longest x4 151 us: body(): lax.all_to_all(part, 'seq', split_axis=2, concat_axis=1, tiled=True)]
    while x19 -> x0, local copies, waits for them, and re-layouts: 19.1 us -> none  [the longest x3 14.1 us: head_gradients(): lax.map(item_gradients, (to_items(queries), to_items(key_vectors), to_ite...]
    squeeze x0 -> x5, local copies, waits for them, and re-layouts: none -> 17.2 us  [body(): part = stacked[:, page, :, :, head, :]]
    dot_general x16, matrix products: 27 us -> 11.9 us  [item_gradients(): jnp.dot(dscores.T, query_block, preferred_element_type=jnp.float32)]
    dot_general x16, matrix products: 25.5 us -> 10.4 us  [item_gradients(): jnp.dot(query_block, key_prefix.T, preferred_element_type=jnp.float32)]
    reshape x4 -> x0, local copies, waits for them, and re-layouts: 14.9 us -> none  [the longest x1 4.07 us: body(): grad_heads = out_grad.reshape(page_count, tok_rows, HEADS, head_width)]
    slice x0 -> x16, local copies, waits for them, and re-layouts: none -> 14.9 us  [the longest x12 10.6 us: item_gradients(): value_prefix = value_vectors[:row_stop]]
    another operation x3 -> x7, other arithmetic: 0.01 us -> 14 us  [the longest x4 5.25 us: body(): grads = jnp.stack(grads).reshape(3, seq_size, tok_rows, 1, head_width)]
  transfers between devices with their start and end apart: 7 -> 8, of which waited for: 7 -> 7; matrix products, arithmetic and copies ran while one was open for 11% -> 25% of each run, Pallas kernels for 0% -> 0%
where the time goes in v1:
time: 470 us; the launch traced here: 465 us
  waiting for transfers between devices  228 us (49%)
  local copies, waits for them, and re-layouts  88 us (19%)
  matrix products  68.1 us (14%)
  starting transfers between devices  42.8 us (9%)
  other arithmetic  35.5 us (8%)
    all_to_all x4, waiting for transfers between devices, body(): lax.all_to_all(part, 'seq', split_axis=2, concat_axis=1, tiled=True)  151 us
    all_to_all x4, waiting for transfers between devices, body(): lax.all_to_all(grads, 'seq', split_axis=1, concat_axis=3, tiled=True)  77 us
    unnamed x169, local copies, waits for them, and re-layouts  37.7 us
    all_to_all x4, starting transfers between devices, body(): lax.all_to_all(grads, 'seq', split_axis=1, concat_axis=3, tiled=True)  21.8 us
    all_to_all x4, starting transfers between devices, body(): lax.all_to_all(part, 'seq', split_axis=2, concat_axis=1, tiled=True)  21 us
    dot_general x16, matrix products, item_gradients(): jnp.dot(probs_low.T, grad_block, preferred_element_type=jnp.float32)  17.4 us
    squeeze x5, local copies, waits for them, and re-layouts, body(): part = stacked[:, page, :, :, head, :]  17.2 us
    dot_general x16, matrix products, item_gradients(): jnp.dot(grad_block, value_prefix.T, preferred_element_type=jnp.float32)  14.5 us
  transfers between devices with their start and end apart: 8, of which 7 were waited for; matrix products, arithmetic and copies ran while one was open for 25% of the time, Pallas kernels for 0%

profile of v1, /device:TPU:13, one launch (start us, length us, event | category | flops | bytes accessed | tf_op | source)
XLA Modules:
  0.0 464.6 jit_solution(4292827705189031111)
XLA Ops:
  0.6 3.1 copy.210
  3.8 4.1 copy.209
  7.9 4.1 copy.208
  11.9 4.1 copy.207
  16.0 3.8 pad_maximum_fusion
  19.8 2.8 slice_bitcast_fusion.1
  22.6 2.6 copy.219
  25.2 6.5 %all-to-all-start.2 = ((bf16[4,128,16,128]{3,1,0,2:T(8,128)(2,1)}), bf16[4,128,16,128]{3,1,0,2:T(8,128)(2,1)S(1)}, u32[]{:S(2)}, u32[]{:S(2)}) async-start(bf16[4,128,16,128]{3,1,0,2:T(8,128)(2,1)} %copy.219), calls=%async_computation.2 | async-start | bytes 4194304 | tf_op jit(solution)/shard_map/all_to_all | solution.py:60
  31.7 3.9 copy.212
  35.7 43.5 %all-to-all-done.2 = bf16[4,128,16,128]{3,1,0,2:T(8,128)(2,1)S(1)} async-done(((bf16[4,128,16,128]{3,1,0,2:T(8,128)(2,1)}), bf16[4,128,16,128]{3,1,0,2:T(8,128)(2,1)S(1)}, u32[]{:S(2)}, u32[]{:S(2)}) %all-to-all-start.2) | async-done | bytes 2097184 | tf_op jit(solution)/shard_map/all_to_all | solution.py:60
  79.2 4.8 %all-to-all-start = ((bf16[4,128,16,128]{3,1,0,2:T(8,128)(2,1)}), bf16[4,128,16,128]{3,1,0,2:T(8,128)(2,1)}, u32[]{:S(2)}, u32[]{:S(2)}) async-start(bf16[4,128,16,128]{3,1,0,2:T(8,128)(2,1)} %copy.212), calls=%async_computation | async-start | bytes 4194304 | tf_op jit(solution)/shard_map/all_to_all | solution.py:60
  83.9 3.9 copy.233
  87.9 43.6 %all-to-all-done = bf16[4,128,16,128]{3,1,0,2:T(8,128)(2,1)} async-done(((bf16[4,128,16,128]{3,1,0,2:T(8,128)(2,1)}), bf16[4,128,16,128]{3,1,0,2:T(8,128)(2,1)}, u32[]{:S(2)}, u32[]{:S(2)}) %all-to-all-start) | async-done | bytes 2097184 | tf_op jit(solution)/shard_map/all_to_all | solution.py:60
  131.5 4.8 %all-to-all-start.6 = ((bf16[4,128,16,128]{3,1,0,2:T(8,128)(2,1)}), bf16[4,128,16,128]{3,1,0,2:T(8,128)(2,1)}, u32[]{:S(2)}, u32[]{:S(2)}) async-start(bf16[4,128,16,128]{3,1,0,2:T(8,128)(2,1)} %copy.233), calls=%async_computation.6 | async-start | bytes 4194304 | tf_op jit(solution)/shard_map/all_to_all | solution.py:60
  136.2 3.9 copy.226
  140.4 2.5 copy.257
  146.4 37.4 %all-to-all-done.6 = bf16[4,128,16,128]{3,1,0,2:T(8,128)(2,1)} async-done(((bf16[4,128,16,128]{3,1,0,2:T(8,128)(2,1)}), bf16[4,128,16,128]{3,1,0,2:T(8,128)(2,1)}, u32[]{:S(2)}, u32[]{:S(2)}) %all-to-all-start.6) | async-done | bytes 2097184 | tf_op jit(solution)/shard_map/all_to_all | solution.py:60
  183.8 4.9 %all-to-all-start.4 = ((bf16[4,128,16,128]{3,1,0,2:T(8,128)(2,1)}), bf16[4,128,16,128]{3,1,0,2:T(8,128)(2,1)}, u32[]{:S(2)}, u32[]{:S(2)}) async-start(bf16[4,128,16,128]{3,1,0,2:T(8,128)(2,1)} %copy.226), calls=%async_computation.4 | async-start | bytes 4194304 | tf_op jit(solution)/shard_map/all_to_all | solution.py:60
  188.7 1.7 copy.254
  209.7 26.4 %all-to-all-done.4 = bf16[4,128,16,128]{3,1,0,2:T(8,128)(2,1)} async-done(((bf16[4,128,16,128]{3,1,0,2:T(8,128)(2,1)}), bf16[4,128,16,128]{3,1,0,2:T(8,128)(2,1)}, u32[]{:S(2)}, u32[]{:S(2)}) %all-to-all-start.4) | async-done | bytes 2097184 | tf_op jit(solution)/shard_map/all_to_all | solution.py:60
  236.1 1.7 copy.255
  253.7 1.4 fusion.39
  255.1 1.5 multiply_reduce_fusion.2
  261.0 5.3 %all-to-all-start.3 = ((bf16[3,16,128,1,128]{4,2,0,3,1:T(8,128)(2,1)}), bf16[3,16,128,1,128]{4,2,0,3,1:T(8,128)(2,1)}, u32[]{:S(2)}, u32[]{:S(2)}) async-start(bf16[3,16,128,1,128]{4,2,0,3,1:T(8,128)(2,1)} %pad_maximum_fusion.3), calls=%async_computation.3 | async-start | bytes 3145728 | tf_op jit(solution)/shard_map/all_to_all | solution.py:64
  281.1 1.4 fusion.37
  282.6 1.5 multiply_reduce_fusion.3
  284.1 1.6 multiply_convert_fusion.3
  300.9 1.4 fusion.43
  302.4 1.5 multiply_reduce_fusion
  303.9 1.6 multiply_convert_fusion
  321.8 6.6 %all-to-all-start.1 = ((bf16[3,16,128,1,128]{4,2,3,0,1:T(8,128)(2,1)}), bf16[3,16,128,1,128]{4,2,3,0,1:T(8,128)(2,1)}, u32[]{:S(2)}, u32[]{:S(2)}) async-start(bf16[3,16,128,1,128]{4,2,3,0,1:T(8,128)(2,1)} %pad_maximum_fusion.2), calls=%async_computation.1 | async-start | bytes 3145728 | tf_op jit(solution)/shard_map/all_to_all | solution.py:64
  328.4 2.0 fusion.82
  339.6 24.9 %all-to-all-done.1 = bf16[3,16,128,1,128]{4,2,3,0,1:T(8,128)(2,1)} async-done(((bf16[3,16,128,1,128]{4,2,3,0,1:T(8,128)(2,1)}), bf16[3,16,128,1,128]{4,2,3,0,1:T(8,128)(2,1)}, u32[]{:S(2)}, u32[]{:S(2)}) %all-to-all-start.1) | async-done | bytes 1572896 | tf_op jit(solution)/shard_map/all_to_all | solution.py:64
  364.5 4.8 %all-to-all-start.7 = ((bf16[3,16,128,1,128]{4,2,0,3,1:T(8,128)(2,1)}), bf16[3,16,128,1,128]{4,2,0,3,1:T(8,128)(2,1)}, u32[]{:S(2)}, u32[]{:S(2)}) async-start(bf16[3,16,128,1,128]{4,2,0,3,1:T(8,128)(2,1)} %pad_maximum_fusion.5), calls=%async_computation.7 | async-start | bytes 3145728 | tf_op jit(solution)/shard_map/all_to_all | solution.py:64
  370.3 1.8 fusion.75
  379.7 1.5 fusion.41
  382.4 23.1 %all-to-all-done.7 = bf16[3,16,128,1,128]{4,2,0,3,1:T(8,128)(2,1)} async-done(((bf16[3,16,128,1,128]{4,2,0,3,1:T(8,128)(2,1)}), bf16[3,16,128,1,128]{4,2,0,3,1:T(8,128)(2,1)}, u32[]{:S(2)}, u32[]{:S(2)}) %all-to-all-start.7) | async-done | bytes 1572896 | tf_op jit(solution)/shard_map/all_to_all | solution.py:64
  405.6 5.2 %all-to-all-start.5 = ((bf16[3,16,128,1,128]{4,2,0,3,1:T(8,128)(2,1)}), bf16[3,16,128,1,128]{4,2,0,3,1:T(8,128)(2,1)S(1)}, u32[]{:S(2)}, u32[]{:S(2)}) async-start(bf16[3,16,128,1,128]{4,2,0,3,1:T(8,128)(2,1)} %pad_maximum_fusion.4), calls=%async_computation.5 | async-start | bytes 3145728 | tf_op jit(solution)/shard_map/all_to_all | solution.py:64
  410.7 1.9 copy.224
  412.6 2.6 copy.217
  415.2 2.6 copy.238
  417.8 29.0 %all-to-all-done.5 = bf16[3,16,128,1,128]{4,2,0,3,1:T(8,128)(2,1)S(1)} async-done(((bf16[3,16,128,1,128]{4,2,0,3,1:T(8,128)(2,1)}), bf16[3,16,128,1,128]{4,2,0,3,1:T(8,128)(2,1)S(1)}, u32[]{:S(2)}, u32[]{:S(2)}) %all-to-all-start.5) | async-done | bytes 1572896 | tf_op jit(solution)/shard_map/all_to_all | solution.py:64
  446.8 1.6 copy.231
  448.4 2.6 maximum_bitcast_fusion
  451.0 2.3 pad_maximum_fusion.1
  453.3 4.1 copy.239
  457.4 4.1 copy.240
  461.4 2.7 copy.241
  (300 shorter events, 107.7 us)
Async XLA Ops:
  25.2 53.9 %all-to-all-start.2 = ((bf16[4,128,16,128]{3,1,0,2:T(8,128)(2,1)}), bf16[4,128,16,128]{3,1,0,2:T(8,128)(2,1)S(1)}, u32[]{:S(2)}, u32[]{:S(2)}) async-start(bf16[4,128,16,128]{3,1,0,2:T(8,128)(2,1)} %copy.219), calls=%async_computation.2 | async-start | bytes 4194304 | tf_op jit(solution)/shard_map/all_to_all | solution.py:60
  79.2 52.3 %all-to-all-start = ((bf16[4,128,16,128]{3,1,0,2:T(8,128)(2,1)}), bf16[4,128,16,128]{3,1,0,2:T(8,128)(2,1)}, u32[]{:S(2)}, u32[]{:S(2)}) async-start(bf16[4,128,16,128]{3,1,0,2:T(8,128)(2,1)} %copy.212), calls=%async_computation | async-start | bytes 4194304 | tf_op jit(solution)/shard_map/all_to_all | solution.py:60
  131.5 52.3 %all-to-all-start.6 = ((bf16[4,128,16,128]{3,1,0,2:T(8,128)(2,1)}), bf16[4,128,16,128]{3,1,0,2:T(8,128)(2,1)}, u32[]{:S(2)}, u32[]{:S(2)}) async-start(bf16[4,128,16,128]{3,1,0,2:T(8,128)(2,1)} %copy.233), calls=%async_computation.6 | async-start | bytes 4194304 | tf_op jit(solution)/shard_map/all_to_all | solution.py:60
  140.4 4.2 copy-start.2
  183.8 52.3 %all-to-all-start.4 = ((bf16[4,128,16,128]{3,1,0,2:T(8,128)(2,1)}), bf16[4,128,16,128]{3,1,0,2:T(8,128)(2,1)}, u32[]{:S(2)}, u32[]{:S(2)}) async-start(bf16[4,128,16,128]{3,1,0,2:T(8,128)(2,1)} %copy.226), calls=%async_computation.4 | async-start | bytes 4194304 | tf_op jit(solution)/shard_map/all_to_all | solution.py:60
  197.6 3.3 copy-start.3
  237.8 2.8 copy-start.55
  238.9 1.8 copy-start.14
  253.7 1.5 copy-start.37
  261.0 60.8 %all-to-all-start.3 = ((bf16[3,16,128,1,128]{4,2,0,3,1:T(8,128)(2,1)}), bf16[3,16,128,1,128]{4,2,0,3,1:T(8,128)(2,1)}, u32[]{:S(2)}, u32[]{:S(2)}) async-start(bf16[3,16,128,1,128]{4,2,0,3,1:T(8,128)(2,1)} %pad_maximum_fusion.3), calls=%async_computation.3 | async-start | bytes 3145728 | tf_op jit(solution)/shard_map/all_to_all | solution.py:64
  266.3 2.1 copy-start.18
  266.3 2.1 copy-start.28
  281.1 1.5 copy-start.35
  300.9 1.5 copy-start.33
  307.9 1.4 copy-start.70
  311.2 5.8 %copy-start.7 = (f32[512,1024]{1,0:T(8,128)}, f32[512,1024]{1,0:T(8,128)S(1)}, u32[]{:S(2)}) copy-start(f32[512,1024]{1,0:T(8,128)S(1)} %get-tuple-element.544) | copy-start | bytes 6291460
  312.0 9.0 %copy-start.4 = (f32[512,1536]{1,0:T(8,128)}, f32[512,1536]{1,0:T(8,128)S(1)}, u32[]{:S(2)}) copy-start(f32[512,1536]{1,0:T(8,128)S(1)} %get-tuple-element.546) | copy-start | bytes 9437188
  312.0 9.0 %copy-start.77 = (f32[512]{0:T(512)}, f32[512]{0:T(512)S(1)}, u32[]{:S(2)}) copy-start(f32[512]{0:T(512)S(1)} %get-tuple-element.545) | copy-start | bytes 6148
  313.1 7.9 %copy-start.79 = (f32[512]{0:T(512)}, f32[512]{0:T(512)S(1)}, u32[]{:S(2)}) copy-start(f32[512]{0:T(512)S(1)} %fusion.17) | copy-start | bytes 6148
  314.5 1.9 copy-start.56
  314.5 1.8 copy-start.64
  317.5 3.4 copy-start.6
  317.6 2.2 copy-start.50
  317.6 2.2 copy-start.62
  321.8 6.6 %copy-start.12 = (bf16[512,512]{0,1:T(8,128)(2,1)S(1)}, bf16[512,512]{0,1:T(8,128)(2,1)}, u32[]{:S(2)}) copy-start(bf16[512,512]{0,1:T(8,128)(2,1)} %copy-done.11) | copy-start | bytes 1572868
  321.8 42.7 %all-to-all-start.1 = ((bf16[3,16,128,1,128]{4,2,3,0,1:T(8,128)(2,1)}), bf16[3,16,128,1,128]{4,2,3,0,1:T(8,128)(2,1)}, u32[]{:S(2)}, u32[]{:S(2)}) async-start(bf16[3,16,128,1,128]{4,2,3,0,1:T(8,128)(2,1)} %pad_maximum_fusion.2), calls=%async_computation.1 | async-start | bytes 3145728 | tf_op jit(solution)/shard_map/all_to_all | solution.py:64
  328.4 3.2 copy-start.38
  328.4 3.2 copy-start.45
  332.6 2.9 copy-start
  332.6 1.4 copy-start.39
  332.6 1.5 copy-start.60
  339.6 29.7 %copy-start.40 = (bf16[512,128]{1,0:T(8,128)(2,1)S(1)}, bf16[512,128]{1,0:T(8,128)(2,1)}, u32[]{:S(2)}) copy-start(bf16[512,128]{1,0:T(8,128)(2,1)} %fusion.88) | copy-start | bytes 393220
  339.6 29.7 %copy-start.44 = (bf16[512,128]{1,0:T(8,128)(2,1)S(1)}, bf16[512,128]{1,0:T(8,128)(2,1)}, u32[]{:S(2)}) copy-start(bf16[512,128]{1,0:T(8,128)(2,1)} %fusion.82) | copy-start | bytes 393220
  339.6 30.7 %copy-start.23 = (bf16[1,4,128,1,128]{4,2,1,3,0:T(8,128)(2,1)S(1)}, bf16[1,4,128,1,128]{4,2,1,3,0:T(8,128)(2,1)}, u32[]{:S(2)}) copy-start(bf16[1,4,128,1,128]{4,2,1,3,0:T(8,128)(2,1)} %get-tuple-element.473) | copy-start | bytes 393220
  364.5 41.0 %all-to-all-start.7 = ((bf16[3,16,128,1,128]{4,2,0,3,1:T(8,128)(2,1)}), bf16[3,16,128,1,128]{4,2,0,3,1:T(8,128)(2,1)}, u32[]{:S(2)}, u32[]{:S(2)}) async-start(bf16[3,16,128,1,128]{4,2,0,3,1:T(8,128)(2,1)} %pad_maximum_fusion.5), calls=%async_computation.7 | async-start | bytes 3145728 | tf_op jit(solution)/shard_map/all_to_all | solution.py:64
  369.3 2.8 copy-start.21
  372.1 1.6 copy-start.10
  372.1 1.6 copy-start.46
  373.7 1.6 copy-start.8
  373.7 1.9 copy-start.15
  373.7 1.9 copy-start.65
  375.6 1.9 copy-start.5
  375.6 1.9 copy-start.63
  375.6 1.9 copy-start.78
  375.6 1.9 copy-start.80
  377.5 2.2 copy-start.1
  377.5 2.2 copy-start.61
  405.6 41.2 %all-to-all-start.5 = ((bf16[3,16,128,1,128]{4,2,0,3,1:T(8,128)(2,1)}), bf16[3,16,128,1,128]{4,2,0,3,1:T(8,128)(2,1)S(1)}, u32[]{:S(2)}, u32[]{:S(2)}) async-start(bf16[3,16,128,1,128]{4,2,0,3,1:T(8,128)(2,1)} %pad_maximum_fusion.4), calls=%async_computation.5 | async-start | bytes 3145728 | tf_op jit(solution)/shard_map/all_to_all | solution.py:64
  (41 other events, 42.1 us)

commit v2 on v1

--- a/solution.py
+++ b/solution.py
@@ -50,23 +50,49 @@
     seq_size = lax.psum(1, "seq")
     head_width = feature_width // HEADS
     per_dev = HEADS // seq_size
+    chunks = page_count * per_dev
+    tokens_all = seq_size * tok_rows
     stacked = jnp.stack([queries, key_vectors, value_vectors, out_grad]).reshape(
         4, page_count, tok_rows, seq_size, per_dev, head_width
     )
-    chunk_out = {}
-    for page in range(page_count):
-        for head in range(per_dev):
-            part = stacked[:, page, :, :, head, :]
-            arrived = lax.all_to_all(part, "seq", split_axis=2, concat_axis=1, tiled=True)
-            arrived = arrived.reshape(4, seq_size * tok_rows, head_width)
-            grads = item_gradients(arrived[0], arrived[1], arrived[2], arrived[3])
-            grads = jnp.stack(grads).reshape(3, seq_size, tok_rows, 1, head_width)
-            returned = lax.all_to_all(grads, "seq", split_axis=1, concat_axis=3, tiled=True)
-            chunk_out[(page, head)] = returned.reshape(3, tok_rows, seq_size, head_width)
-    pages = []
-    for page in range(page_count):
-        pages.append(jnp.stack([chunk_out[(page, head)] for head in range(per_dev)], axis=3))
-    result = jnp.stack(pages, axis=1).reshape(3, page_count, tok_rows, feature_width)
+    stacked = stacked.transpose(1, 4, 0, 2, 3, 5).reshape(chunks, 4, tok_rows, seq_size, head_width)
+
+    def fetch(chunk):
+        part = lax.dynamic_index_in_dim(stacked, chunk, 0, keepdims=False)
+        arrived = lax.all_to_all(part, "seq", split_axis=2, concat_axis=1, tiled=True)
+        return arrived.reshape(4, tokens_all, head_width)
+
+    def compute(arrived):
+        grads = item_gradients(arrived[0], arrived[1], arrived[2], arrived[3])
+        return jnp.stack(grads).reshape(3, seq_size, tok_rows, 1, head_width)
+
+    def send(grads, out_buf, chunk):
+        returned = lax.all_to_all(grads, "seq", split_axis=1, concat_axis=3, tiled=True)
+        returned = returned.reshape(1, 3, tok_rows, seq_size, head_width)
+        return lax.dynamic_update_index_in_dim(out_buf, returned[0], chunk, 0)
+
+    out_buf = jnp.zeros((chunks, 3, tok_rows, seq_size, head_width), jnp.bfloat16)
+    current = fetch(0)
+    if chunks > 1:
+        upcoming = fetch(1)
+        prev = compute(current)
+        current = upcoming
+
+        def loop_body(chunk, carry):
+            current, prev, out_buf = carry
+            upcoming = fetch(chunk + 1)
+            grads = compute(current)
+            out_buf = send(prev, out_buf, chunk - 1)
+            return upcoming, grads, out_buf
+
+        current, prev, out_buf = lax.fori_loop(1, chunks - 1, loop_body, (current, prev, out_buf))
+        last = compute(current)
+        out_buf = send(prev, out_buf, chunks - 2)
+        out_buf = send(last, out_buf, chunks - 1)
+    else:
+        out_buf = send(compute(current), out_buf, 0)
+    result = out_buf.reshape(page_count, per_dev, 3, tok_rows, seq_size, head_width)
+    result = result.transpose(2, 0, 3, 4, 1, 5).reshape(3, page_count, tok_rows, feature_width)
     return result[0], result[1], result[2]
 
 

time: 470 us -> 492 us (1.047)
  waiting for transfers between devices: 228 us -> 199 us
  matrix products: 68.1 us -> 95.2 us
  local copies, waits for them, and re-layouts: 88 us -> 109 us
    all_to_all x8, waiting for transfers between devices: 228 us -> 199 us  [the longest x4 133 us: fetch(): lax.all_to_all(part, 'seq', split_axis=2, concat_axis=1, tiled=True)]
    unnamed x169 -> x76, local copies, waits for them, and re-layouts: 37.7 us -> 12.2 us
    another operation x0 -> x10, local copies, waits for them, and re-layouts: none -> 22.7 us  [the longest x8 20.1 us: body(): jnp.stack([queries, key_vectors, value_vectors, out_grad])]
    dot_general x16, matrix products: 10.4 us -> 21.9 us  [item_gradients(): jnp.dot(query_block, key_prefix.T, preferred_element_type=jnp.float32)]
    reshape x0 -> x1, local copies, waits for them, and re-layouts: none -> 11.2 us  [body(): out_buf.reshape(page_count, per_dev, 3, tok_rows, seq_size, head_width)]
    slice x12 -> x3, local copies, waits for them, and re-layouts: 10.6 us -> 0.2 us  [item_gradients(): value_prefix = value_vectors[:row_stop]]
    dynamic_update_slice x0 -> x4, local copies, waits for them, and re-layouts: none -> 9.59 us  [send(): return lax.dynamic_update_index_in_dim(out_buf, returned[0], chunk, 0)]
    another operation x6 -> x4, other arithmetic: 10.2 us -> 1.83 us  [compute(): return jnp.stack(grads).reshape(3, seq_size, tok_rows, 1, head_width)]
  transfers between devices with their start and end apart: 8 -> 8, of which waited for: 7 -> 8; matrix products, arithmetic and copies ran while one was open for 25% -> 25% of each run, Pallas kernels for 0% -> 0%
where the time goes in v2:
time: 492 us; the launch traced here: 485 us
  waiting for transfers between devices  199 us (40%)
  local copies, waits for them, and re-layouts  109 us (22%)
  matrix products  95.2 us (19%)
  starting transfers between devices  41.1 us (8%)
  other arithmetic  38.3 us (8%)
    all_to_all x4, waiting for transfers between devices, fetch(): lax.all_to_all(part, 'seq', split_axis=2, concat_axis=1, tiled=True)  133 us
    all_to_all x4, waiting for transfers between devices, send(): lax.all_to_all(grads, 'seq', split_axis=1, concat_axis=3, tiled=True)  65.6 us
    dot_general x16, matrix products, item_gradients(): jnp.dot(probs_low.T, grad_block, preferred_element_type=jnp.float32)  23.8 us
    all_to_all x4, starting transfers between devices, fetch(): lax.all_to_all(part, 'seq', split_axis=2, concat_axis=1, tiled=True)  21.9 us
    dot_general x16, matrix products, item_gradients(): jnp.dot(query_block, key_prefix.T, preferred_element_type=jnp.float32)  21.9 us
    another operation x8, local copies, waits for them, and re-layouts, body(): jnp.stack([queries, key_vectors, value_vectors, out_grad])  20.1 us
    convert_element_type x16, other arithmetic, item_gradients(): dscores = (softmax_rows * (dprobs - row_delta)).astype(jnp.bfloat16)  19.4 us
    all_to_all x4, starting transfers between devices, send(): lax.all_to_all(grads, 'seq', split_axis=1, concat_axis=3, tiled=True)  19.2 us
  transfers between devices with their start and end apart: 8, of which 8 were waited for; matrix products, arithmetic and copies ran while one was open for 25% of the time, Pallas kernels for 0%

profile of v2, /device:TPU:13, one launch (start us, length us, event | category | flops | bytes accessed | tf_op | source)
XLA Modules:
  0.0 485.3 jit_solution(7641232779658555559)
XLA Ops:
  0.6 3.2 stack.59
  6.0 3.2 stack.60
  11.4 3.2 stack.61
  16.8 3.2 stack.62
  22.2 2.9 pad_maximum_fusion.2
  25.2 3.2 copy-done.9
  28.4 2.5 slice_bitcast_fusion
  30.9 6.9 %all-to-all-start.3 = ((bf16[4,128,16,128]{3,1,0,2:T(8,128)(2,1)}), bf16[4,128,16,128]{3,1,0,2:T(8,128)(2,1)S(1)}, u32[]{:S(2)}, u32[]{:S(2)}) async-start(bf16[4,128,16,128]{3,1,0,2:T(8,128)(2,1)} %get-tuple-element.753), calls=%async_computation.3 | async-start | bytes 4194304 | tf_op jit(solution)/shard_map/all_to_all | solution.py:62
  37.9 47.2 %all-to-all-done.3 = bf16[4,128,16,128]{3,1,0,2:T(8,128)(2,1)S(1)} async-done(((bf16[4,128,16,128]{3,1,0,2:T(8,128)(2,1)}), bf16[4,128,16,128]{3,1,0,2:T(8,128)(2,1)S(1)}, u32[]{:S(2)}, u32[]{:S(2)}) %all-to-all-start.3) | async-done | bytes 2097184 | tf_op jit(solution)/shard_map/all_to_all | solution.py:62
  100.0 3.6 multiply_reduce_fusion.5
  103.7 5.5 %all-to-all-start.2 = ((bf16[4,128,16,128]{3,1,0,2:T(8,128)(2,1)}), bf16[4,128,16,128]{3,1,0,2:T(8,128)(2,1)}, u32[]{:S(2)}, u32[]{:S(2)}) async-start(bf16[4,128,16,128]{3,1,0,2:T(8,128)(2,1)} %get-tuple-element.754), calls=%async_computation.2 | async-start | bytes 4194304 | tf_op jit(solution)/shard_map/all_to_all | solution.py:62
  109.1 4.2 multiply_convert_fusion.5
  123.7 32.8 %all-to-all-done.2 = bf16[4,128,16,128]{3,1,0,2:T(8,128)(2,1)} async-done(((bf16[4,128,16,128]{3,1,0,2:T(8,128)(2,1)}), bf16[4,128,16,128]{3,1,0,2:T(8,128)(2,1)}, u32[]{:S(2)}, u32[]{:S(2)}) %all-to-all-start.2) | async-done | bytes 2097184 | tf_op jit(solution)/shard_map/all_to_all | solution.py:62
  156.5 3.2 copy.47
  159.6 4.3 broadcast_in_dim.175
  163.9 196.1 %while.81 = (s32[]{:T(128)}, bf16[4,2048,128]{2,1,0:T(8,128)(2,1)}, bf16[3,16,128,1,128]{4,2,1,3,0:T(8,128)(2,1)S(1)}, bf16[4,3,128,16,128]{4,2,1,3,0:T(8,128)(2...) while((s32[]{:T(128)}, bf16[4,2048,128]{2,1,0:T(8,128)(2,1)}, ...), condition=%wide.region_29.30_spmd, body=%wide.region_12.29_spmd.sunk | while | flops 3409178112 | bytes 230036160 | solution.py:88
  165.4 4.8 all-to-all-start.1
  181.1 2.8 fusion.361
  184.5 2.9 fusion.362
  187.4 3.3 dynamic-slice_bitcast_fusion.2
  198.5 7.9 %all-to-all-done.1 = bf16[3,16,128,1,128]{4,2,0,3,1:T(8,128)(2,1)} async-done(((bf16[3,16,128,1,128]{4,2,0,3,1:T(8,128)(2,1)}), bf16[3,16,128,1,128]{4,2,0,3,1:T(8,128)(2,1)}, u32[]{:S(2)}, u32[]{:S(2)}) %all-to-all-start.1) | async-done | bytes 1572896 | tf_op jit(solution)/shard_map/while/body/eval_jaxpr/all_to_all | solution.py:70
  206.4 4.8 all-to-all-start
  226.7 2.4 fusion.363
  229.2 2.8 bitcast_dynamic-update-slice_fusion.4
  232.1 26.7 %all-to-all-done = bf16[4,128,16,128]{3,1,0,2:T(8,128)(2,1)} async-done(((bf16[4,128,16,128]{3,1,0,2:T(8,128)(2,1)}), bf16[4,128,16,128]{3,1,0,2:T(8,128)(2,1)}, u32[]{:S(2)}, u32[]{:S(2)}) %all-to-all-start) | async-done | bytes 2097184 | tf_op jit(solution)/shard_map/while/body/eval_jaxpr/all_to_all | solution.py:62
  258.7 3.2 copy.63
  263.2 4.8 all-to-all-start.1
  278.9 2.8 fusion.361
  282.3 2.9 fusion.362
  285.2 3.3 dynamic-slice_bitcast_fusion.2
  296.3 7.9 %all-to-all-done.1 = bf16[3,16,128,1,128]{4,2,0,3,1:T(8,128)(2,1)} async-done(((bf16[3,16,128,1,128]{4,2,0,3,1:T(8,128)(2,1)}), bf16[3,16,128,1,128]{4,2,0,3,1:T(8,128)(2,1)}, u32[]{:S(2)}, u32[]{:S(2)}) %all-to-all-start.1) | async-done | bytes 1572896 | tf_op jit(solution)/shard_map/while/body/eval_jaxpr/all_to_all | solution.py:70
  304.2 4.8 all-to-all-start
  324.4 2.4 fusion.363
  327.0 2.7 bitcast_dynamic-update-slice_fusion.4
  329.8 26.8 %all-to-all-done = bf16[4,128,16,128]{3,1,0,2:T(8,128)(2,1)} async-done(((bf16[4,128,16,128]{3,1,0,2:T(8,128)(2,1)}), bf16[4,128,16,128]{3,1,0,2:T(8,128)(2,1)}, u32[]{:S(2)}, u32[]{:S(2)}) %all-to-all-start) | async-done | bytes 2097184 | tf_op jit(solution)/shard_map/while/body/eval_jaxpr/all_to_all | solution.py:62
  356.5 3.2 copy.63
  365.2 2.3 fusion.231
  367.6 2.8 fusion.232
  372.7 4.9 %all-to-all-start.4 = ((bf16[3,16,128,1,128]{4,2,0,3,1:T(8,128)(2,1)}), bf16[3,16,128,1,128]{4,2,0,3,1:T(8,128)(2,1)}, u32[]{:S(2)}, u32[]{:S(2)}) async-start(bf16[3,16,128,1,128]{4,2,0,3,1:T(8,128)(2,1)} %copy.50), calls=%async_computation.4 | async-start | bytes 3145728 | tf_op jit(solution)/shard_map/all_to_all | solution.py:70
  397.6 16.3 %all-to-all-done.4 = bf16[3,16,128,1,128]{4,2,0,3,1:T(8,128)(2,1)} async-done(((bf16[3,16,128,1,128]{4,2,0,3,1:T(8,128)(2,1)}), bf16[3,16,128,1,128]{4,2,0,3,1:T(8,128)(2,1)}, u32[]{:S(2)}, u32[]{:S(2)}) %all-to-all-start.4) | async-done | bytes 1572896 | tf_op jit(solution)/shard_map/all_to_all | solution.py:70
  413.9 4.8 all-to-all-start.5
  418.7 2.8 bitcast_dynamic-update-slice_fusion.2
  421.5 33.4 %all-to-all-done.5 = bf16[3,16,128,1,128]{4,2,0,3,1:T(8,128)(2,1)S(1)} async-done(((bf16[3,16,128,1,128]{4,2,0,3,1:T(8,128)(2,1)}), bf16[3,16,128,1,128]{4,2,0,3,1:T(8,128)(2,1)S(1)}, u32[]{:S(2)}, u32[]{:S(2)}) %all-to-all-start.5) | async-done | bytes 1572896 | tf_op jit(solution)/shard_map/all_to_all | solution.py:70
  456.1 11.2 %copy.59 = bf16[2,2,3,128,16,128]{5,1,4,3,0,2:T(2,128)(2,1)S(1)} copy(bf16[2,2,3,128,16,128]{5,3,2,4,1,0:T(8,128)(2,1)} %bitcast.84) | data formatting | bytes 12582912 | tf_op jit(solution)/shard_map/reshape | solution.py:94
  467.3 6.1 %fusion.220 = (bf16[1,2,128,16,2,128]{5,4,3,2,1,0:T(2,128)(2,1)}, bf16[1,2,128,16,2,128]{5,4,3,2,1,0:T(2,128)(2,1)}, bf16[1,2,128,16,2,128]{5,4,3,2,1,0:T(2,128)(2,1)S(1)}) fusion(bf16[3,2,128,16,2,128]{5,4,3,2,1,0:T(2,128)(2,1)S(1)} %bitcast.426), kind=kLoop, calls=%fused_computation.318 | loop fusion | bytes 12582912 | tf_op jit(solution)/shard_map/slice | solution.py:96
  473.4 4.5 squeeze.95
  477.9 4.5 squeeze.94
  482.3 2.8 squeeze.93
  (279 shorter events, 134.0 us)
Async XLA Ops:
  20.0 2.2 copy-start.26
  25.2 3.2 copy-start.9
  30.9 54.2 %all-to-all-start.3 = ((bf16[4,128,16,128]{3,1,0,2:T(8,128)(2,1)}), bf16[4,128,16,128]{3,1,0,2:T(8,128)(2,1)S(1)}, u32[]{:S(2)}, u32[]{:S(2)}) async-start(bf16[4,128,16,128]{3,1,0,2:T(8,128)(2,1)} %get-tuple-element.753), calls=%async_computation.3 | async-start | bytes 4194304 | tf_op jit(solution)/shard_map/all_to_all | solution.py:62
  37.8 51.7 %copy-start.52 = (s32[512]{0:T(512)}, s32[512]{0:T(512)S(1)}, u32[]{:S(2)}) copy-start(s32[512]{0:T(512)S(1)} %iota_add_fusion.5) | copy-start | bytes 6148
  37.9 55.2 %copy-start.50 = (s32[512]{0:T(512)}, s32[512]{0:T(512)S(1)}, u32[]{:S(2)}) copy-start(s32[512]{0:T(512)S(1)} %iota_add_fusion.4) | copy-start | bytes 6148
  37.9 59.2 %copy-start.48 = (s32[512]{0:T(512)}, s32[512]{0:T(512)S(1)}, u32[]{:S(2)}) copy-start(s32[512]{0:T(512)S(1)} %iota_add_fusion.3) | copy-start | bytes 6148
  85.6 5.0 %copy-start.42 = (bf16[1,4,128,1,128]{4,2,1,3,0:T(8,128)(2,1)}, bf16[1,4,128,1,128]{4,2,1,3,0:T(8,128)(2,1)S(1)}, u32[]{:S(2)}) copy-start(bf16[1,4,128,1,128]{4,2,1,3,0:T(8,128)(2,1)S(1)} %get-tuple-element.769) | copy-start | bytes 393220
  85.6 8.8 %copy-start.40 = (bf16[1,4,128,1,128]{4,2,1,3,0:T(8,128)(2,1)}, bf16[1,4,128,1,128]{4,2,1,3,0:T(8,128)(2,1)S(1)}, u32[]{:S(2)}) copy-start(bf16[1,4,128,1,128]{4,2,1,3,0:T(8,128)(2,1)S(1)} %get-tuple-element.767) | copy-start | bytes 393220
  85.6 11.4 %copy-start.32 = (bf16[1,4,128,1,128]{4,2,1,3,0:T(8,128)(2,1)}, bf16[1,4,128,1,128]{4,2,1,3,0:T(8,128)(2,1)S(1)}, u32[]{:S(2)}) copy-start(bf16[1,4,128,1,128]{4,2,1,3,0:T(8,128)(2,1)S(1)} %get-tuple-element.766) | copy-start | bytes 393220
  85.6 13.1 %copy-start.38 = (bf16[1,4,128,1,128]{4,2,1,3,0:T(8,128)(2,1)}, bf16[1,4,128,1,128]{4,2,1,3,0:T(8,128)(2,1)S(1)}, u32[]{:S(2)}) copy-start(bf16[1,4,128,1,128]{4,2,1,3,0:T(8,128)(2,1)S(1)} %get-tuple-element.765) | copy-start | bytes 393220
  92.0 1.9 copy-start.20
  98.1 2.0 copy-start.15
  103.7 52.8 %all-to-all-start.2 = ((bf16[4,128,16,128]{3,1,0,2:T(8,128)(2,1)}), bf16[4,128,16,128]{3,1,0,2:T(8,128)(2,1)}, u32[]{:S(2)}, u32[]{:S(2)}) async-start(bf16[4,128,16,128]{3,1,0,2:T(8,128)(2,1)} %get-tuple-element.754), calls=%async_computation.2 | async-start | bytes 4194304 | tf_op jit(solution)/shard_map/all_to_all | solution.py:62
  116.1 1.9 copy-start.43
  118.0 1.9 copy-start.19
  118.0 1.9 copy-start.41
  118.0 1.9 copy-start.45
  118.0 1.9 copy-start.47
  119.9 2.2 copy-start.16
  119.9 2.2 copy-start.39
  165.4 41.1 %all-to-all-start.1 = ((bf16[3,16,128,1,128]{4,2,0,3,1:T(8,128)(2,1)}), bf16[3,16,128,1,128]{4,2,0,3,1:T(8,128)(2,1)}, u32[]{:S(2)}, u32[]{:S(2)}) async-start(bf16[3,16,128,1,128]{4,2,0,3,1:T(8,128)(2,1)} %copy.64), calls=%async_computation.1 | async-start | bytes 3145728 | tf_op jit(solution)/shard_map/while/body/eval_jaxpr/all_to_all | solution.py:70
  181.1 13.0 %copy-start.34 = (f32[512]{0:T(512)}, f32[512]{0:T(512)S(1)}, u32[]{:S(2)}) copy-start(f32[512]{0:T(512)S(1)} %get-tuple-element.858) | copy-start | bytes 6148 | tf_op jit(solution)/shard_map/while
  184.5 9.6 %copy-start.36 = (f32[512]{0:T(512)}, f32[512]{0:T(512)S(1)}, u32[]{:S(2)}) copy-start(f32[512]{0:T(512)S(1)} %fusion.359) | copy-start | bytes 6148 | tf_op jit(solution)/shard_map/while
  187.4 3.3 copy-start.11
  190.7 2.2 copy-start
  206.4 52.3 %all-to-all-start = ((bf16[4,128,16,128]{3,1,0,2:T(8,128)(2,1)}), bf16[4,128,16,128]{3,1,0,2:T(8,128)(2,1)}, u32[]{:S(2)}, u32[]{:S(2)}) async-start(bf16[4,128,16,128]{3,1,0,2:T(8,128)(2,1)} %dynamic-slice_bitcast_fusion.2), calls=%async_computation | async-start | bytes 4194304 | tf_op jit(solution)/shard_map/while/body/eval_jaxpr/all_to_all | solution.py:62
  213.8 2.1 copy-start.4
  214.1 3.6 copy-start.27
  215.9 1.9 copy-start.8
  224.4 2.3 copy-start.1
  263.2 41.1 %all-to-all-start.1 = ((bf16[3,16,128,1,128]{4,2,0,3,1:T(8,128)(2,1)}), bf16[3,16,128,1,128]{4,2,0,3,1:T(8,128)(2,1)}, u32[]{:S(2)}, u32[]{:S(2)}) async-start(bf16[3,16,128,1,128]{4,2,0,3,1:T(8,128)(2,1)} %copy.64), calls=%async_computation.1 | async-start | bytes 3145728 | tf_op jit(solution)/shard_map/while/body/eval_jaxpr/all_to_all | solution.py:70
  278.9 13.0 %copy-start.34 = (f32[512]{0:T(512)}, f32[512]{0:T(512)S(1)}, u32[]{:S(2)}) copy-start(f32[512]{0:T(512)S(1)} %get-tuple-element.858) | copy-start | bytes 6148 | tf_op jit(solution)/shard_map/while
  282.3 9.6 %copy-start.36 = (f32[512]{0:T(512)}, f32[512]{0:T(512)S(1)}, u32[]{:S(2)}) copy-start(f32[512]{0:T(512)S(1)} %fusion.359) | copy-start | bytes 6148 | tf_op jit(solution)/shard_map/while
  285.2 3.3 copy-start.11
  288.5 2.2 copy-start
  304.2 52.3 %all-to-all-start = ((bf16[4,128,16,128]{3,1,0,2:T(8,128)(2,1)}), bf16[4,128,16,128]{3,1,0,2:T(8,128)(2,1)}, u32[]{:S(2)}, u32[]{:S(2)}) async-start(bf16[4,128,16,128]{3,1,0,2:T(8,128)(2,1)} %dynamic-slice_bitcast_fusion.2), calls=%async_computation | async-start | bytes 4194304 | tf_op jit(solution)/shard_map/while/body/eval_jaxpr/all_to_all | solution.py:62
  311.6 2.1 copy-start.4
  311.9 3.6 copy-start.27
  313.6 1.9 copy-start.8
  322.2 2.3 copy-start.1
  363.1 2.1 copy-start.51
  365.2 2.3 copy-start.49
  372.7 7.1 %copy-start.13 = (bf16[4,2048,128]{2,1,0:T(8,128)(2,1)S(1)}, bf16[4,2048,128]{2,1,0:T(8,128)(2,1)}, u32[]{:S(2)}) copy-start(bf16[4,2048,128]{2,1,0:T(8,128)(2,1)} %get-tuple-element.705) | copy-start | bytes 6291460
  372.7 41.2 %all-to-all-start.4 = ((bf16[3,16,128,1,128]{4,2,0,3,1:T(8,128)(2,1)}), bf16[3,16,128,1,128]{4,2,0,3,1:T(8,128)(2,1)}, u32[]{:S(2)}, u32[]{:S(2)}) async-start(bf16[3,16,128,1,128]{4,2,0,3,1:T(8,128)(2,1)} %copy.50), calls=%async_computation.4 | async-start | bytes 3145728 | tf_op jit(solution)/shard_map/all_to_all | solution.py:70
  377.6 2.2 copy-start.24
  380.5 1.9 copy-start.17
  383.9 2.2 copy-start.14
  413.9 41.0 %all-to-all-start.5 = ((bf16[3,16,128,1,128]{4,2,0,3,1:T(8,128)(2,1)}), bf16[3,16,128,1,128]{4,2,0,3,1:T(8,128)(2,1)S(1)}, u32[]{:S(2)}, u32[]{:S(2)}) async-start(bf16[3,16,128,1,128]{4,2,0,3,1:T(8,128)(2,1)} %pad_maximum_fusion.4), calls=%async_computation.5 | async-start | bytes 3145728 | tf_op jit(solution)/shard_map/all_to_all | solution.py:70
  (30 other events, 45.0 us)

commit v3 on v1

v3 whole, which is shorter than its diff:
```python
import jax
import jax.numpy as jnp
from jax import lax
from jax.experimental import pallas as pl
from jax.experimental.pallas import tpu as pltpu
from jax.sharding import PartitionSpec as P

HEADS = 32
BLOCK = 256


def _kernel(q_ref, k_ref, v_ref, do_ref, dq_ref, dk_ref, dv_ref, s_scr, dp_scr, dk_acc, dv_acc):
    tokens_all, head_width = q_ref.shape
    blk = BLOCK
    scale = head_width ** (-0.5)
    dk_acc[...] = jnp.zeros_like(dk_acc)
    dv_acc[...] = jnp.zeros_like(dv_acc)
    contract_rows = (((0,), (0,)), ((), ()))
    contract_cols = (((1,), (1,)), ((), ()))

    def row_block(i, carry):
        r0 = pl.multiple_of(i * blk, blk)
        q = q_ref[pl.ds(r0, blk), :]
        do = do_ref[pl.ds(r0, blk), :]
        count = i + 1

        def scores_pass(j, top):
            c0 = pl.multiple_of(j * blk, blk)
            s = lax.dot_general(q, k_ref[pl.ds(c0, blk), :], contract_cols,
                                preferred_element_type=jnp.float32) * scale
            rows = r0 + lax.broadcasted_iota(jnp.int32, (blk, blk), 0)
            cols = c0 + lax.broadcasted_iota(jnp.int32, (blk, blk), 1)
            s = jnp.where(rows >= cols, s, -jnp.inf)
            s_scr[:, pl.ds(c0, blk)] = s
            return jnp.maximum(top, jnp.max(s, axis=1, keepdims=True))

        top = lax.fori_loop(0, count, scores_pass, jnp.full((blk, 1), -jnp.inf, jnp.float32))

        def weights_pass(j, total):
            c0 = pl.multiple_of(j * blk, blk)
            w = jnp.exp(s_scr[:, pl.ds(c0, blk)] - top)
            s_scr[:, pl.ds(c0, blk)] = w
            return total + jnp.sum(w, axis=1, keepdims=True)

        total = lax.fori_loop(0, count, weights_pass, jnp.zeros((blk, 1), jnp.float32))

        def probs_pass(j, delta):
            c0 = pl.multiple_of(j * blk, blk)
            p = s_scr[:, pl.ds(c0, blk)] / total
            dp = lax.dot_general(do, v_ref[pl.ds(c0, blk), :], contract_cols,
                                 preferred_element_type=jnp.float32)
            s_scr[:, pl.ds(c0, blk)] = p
            dp_scr[:, pl.ds(c0, blk)] = dp
            return delta + jnp.sum(p * dp, axis=1, keepdims=True)

        delta = lax.fori_loop(0, count, probs_pass, jnp.zeros((blk, 1), jnp.float32))

        def grads_pass(j, dq):
            c0 = pl.multiple_of(j * blk, blk)
            p = s_scr[:, pl.ds(c0, blk)]
            ds = (p * (dp_scr[:, pl.ds(c0, blk)] - delta)).astype(jnp.bfloat16)
            dq = dq + jnp.dot(ds, k_ref[pl.ds(c0, blk), :], preferred_element_type=jnp.float32)
            dk_acc[pl.ds(c0, blk), :] += lax.dot_general(
                ds, q, contract_rows, preferred_element_type=jnp.float32)
            dv_acc[pl.ds(c0, blk), :] += lax.dot_general(
                p.astype(jnp.bfloat16), do, contract_rows, preferred_element_type=jnp.float32)
            return dq

        dq = lax.fori_loop(0, count, grads_pass, jnp.zeros((blk, head_width), jnp.float32))
        dq_ref[pl.ds(r0, blk), :] = (dq * scale).astype(dq_ref.dtype)
        return carry

    lax.fori_loop(0, tokens_all // blk, row_block, 0)
    dk_ref[...] = (dk_acc[...] * scale).astype(dk_ref.dtype)
    dv_ref[...] = dv_acc[...].astype(dv_ref.dtype)


def item_gradients(queries, key_vectors, value_vectors, out_grad):
    tokens_all, head_width = queries.shape
    out = jax.ShapeDtypeStruct((tokens_all, head_width), jnp.bfloat16)
    return pl.pallas_call(
        _kernel,
        out_shape=(out, out, out),
        scratch_shapes=[
            pltpu.VMEM((BLOCK, tokens_all), jnp.float32),
            pltpu.VMEM((BLOCK, tokens_all), jnp.float32),
            pltpu.VMEM((tokens_all, head_width), jnp.float32),
            pltpu.VMEM((tokens_all, head_width), jnp.float32),
        ],
        compiler_params=pltpu.CompilerParams(vmem_limit_bytes=32 * 1024 * 1024),
    )(queries, key_vectors, value_vectors, out_grad)


def body(queries, key_vectors, value_vectors, out_grad):
    page_count, tok_rows, feature_width = queries.shape
    seq_size = lax.psum(1, "seq")
    head_width = feature_width // HEADS
    per_dev = HEADS // seq_size
    stacked = jnp.stack([queries, key_vectors, value_vectors, out_grad]).reshape(
        4, page_count, tok_rows, seq_size, per_dev, head_width
    )
    chunk_out = {}
    for page in range(page_count):
        for head in range(per_dev):
            part = stacked[:, page, :, :, head, :]
            arrived = lax.all_to_all(part, "seq", split_axis=2, concat_axis=1, tiled=True)
            arrived = arrived.reshape(4, seq_size * tok_rows, head_width)
            grads = item_gradients(arrived[0], arrived[1], arrived[2], arrived[3])
            grads = jnp.stack(grads).reshape(3, seq_size, tok_rows, 1, head_width)
            returned = lax.all_to_all(grads, "seq", split_axis=1, concat_axis=3, tiled=True)
            chunk_out[(page, head)] = returned.reshape(3, tok_rows, seq_size, head_width)
    pages = []
    for page in range(page_count):
        pages.append(jnp.stack([chunk_out[(page, head)] for head in range(per_dev)], axis=3))
    result = jnp.stack(pages, axis=1).reshape(3, page_count, tok_rows, feature_width)
    return result[0], result[1], result[2]


def solution(mesh):
    placed = P("group", "seq", None)
    return jax.shard_map(
        body,
        mesh=mesh,
        in_specs=(placed, placed, placed, placed),
        out_specs=(placed, placed, placed),
        check_vma=False,
    )
```

time: 470 us -> 433 us (0.921)
  Pallas kernels: 0 us -> 144 us
  matrix products: 68.1 us -> 0 us
  waiting for transfers between devices: 228 us -> 168 us
  local copies, waits for them, and re-layouts: 88 us -> 61.4 us
  other arithmetic: 35.5 us -> 14 us
    pallas_call x0 -> x4, Pallas kernels: none -> 144 us  [item_gradients(): pl.pallas_call(_kernel, out_shape=(out, out, out), scratch_shapes=[pltpu....]
    dot_general x80 -> x0, matrix products: 68.1 us -> none  [the longest x16 17.4 us: item_gradients(): jnp.dot(probs_low.T, grad_block, preferred_element_type=jnp.float32)]
    all_to_all x4, waiting for transfers between devices: 77 us -> 29.1 us  [body(): lax.all_to_all(grads, 'seq', split_axis=1, concat_axis=3, tiled=True)]
    convert_element_type x16 -> x0, other arithmetic: 12.4 us -> none  [item_gradients(): dscores = (softmax_rows * (dprobs - row_delta)).astype(jnp.bfloat16)]
    all_to_all x4, waiting for transfers between devices: 151 us -> 139 us  [body(): lax.all_to_all(part, 'seq', split_axis=2, concat_axis=1, tiled=True)]
    slice x12 -> x0, local copies, waits for them, and re-layouts: 10.6 us -> none  [item_gradients(): value_prefix = value_vectors[:row_stop]]
    reduce_sum x16 -> x0, other arithmetic: 7.94 us -> none  [item_gradients(): softmax_rows = weights / jnp.sum(weights, axis=1, keepdims=True)]
    unnamed x169 -> x13, local copies, waits for them, and re-layouts: 37.7 us -> 30.1 us
  transfers between devices with their start and end apart: 8 -> 8, of which waited for: 7 -> 5; matrix products, arithmetic and copies ran while one was open for 25% -> 7% of each run, Pallas kernels for 0% -> 33%
where the time goes in v3:
time: 433 us; the launch traced here: 432 us
  waiting for transfers between devices  168 us (39%)
  Pallas kernels  144 us (33%)
  local copies, waits for them, and re-layouts  61.4 us (14%)
  starting transfers between devices  43.7 us (10%)
  other arithmetic  14 us (3%)
    pallas_call x4, Pallas kernels, item_gradients(): pl.pallas_call(_kernel, out_shape=(out, out, out), scratch_shapes=[pltpu....  144 us
    all_to_all x4, waiting for transfers between devices, body(): lax.all_to_all(part, 'seq', split_axis=2, concat_axis=1, tiled=True)  139 us
    unnamed x13, local copies, waits for them, and re-layouts  30.1 us
    all_to_all x4, waiting for transfers between devices, body(): lax.all_to_all(grads, 'seq', split_axis=1, concat_axis=3, tiled=True)  29.1 us
    all_to_all x4, starting transfers between devices, body(): lax.all_to_all(grads, 'seq', split_axis=1, concat_axis=3, tiled=True)  22.8 us
    all_to_all x4, starting transfers between devices, body(): lax.all_to_all(part, 'seq', split_axis=2, concat_axis=1, tiled=True)  20.9 us
    squeeze x5, local copies, waits for them, and re-layouts, body(): part = stacked[:, page, :, :, head, :]  17.2 us
  transfers between devices with their start and end apart: 8, of which 5 were waited for; matrix products, arithmetic and copies ran while one was open for 7% of the time, Pallas kernels for 33%

profile of v3, /device:TPU:13, one launch (start us, length us, event | category | flops | bytes accessed | tf_op | source)
XLA Modules:
  0.0 431.7 jit_solution(12602858246267296855)
XLA Ops:
  0.6 3.1 copy.35
  3.8 4.1 copy.36
  7.9 4.1 copy.37
  11.9 4.1 copy.38
  16.0 3.8 pad_maximum_fusion
  19.8 2.8 slice_bitcast_fusion.1
  22.6 2.6 copy.49
  25.2 6.5 %all-to-all-start.4 = ((bf16[4,128,16,128]{3,1,0,2:T(8,128)(2,1)}), bf16[4,128,16,128]{3,1,0,2:T(8,128)(2,1)S(1)}, u32[]{:S(2)}, u32[]{:S(2)}) async-start(bf16[4,128,16,128]{3,1,0,2:T(8,128)(2,1)} %copy.49), calls=%async_computation.4 | async-start | bytes 4194304 | tf_op jit(solution)/shard_map/all_to_all | solution.py:106
  31.7 3.9 copy.54
  35.7 43.5 %all-to-all-done.4 = bf16[4,128,16,128]{3,1,0,2:T(8,128)(2,1)S(1)} async-done(((bf16[4,128,16,128]{3,1,0,2:T(8,128)(2,1)}), bf16[4,128,16,128]{3,1,0,2:T(8,128)(2,1)S(1)}, u32[]{:S(2)}, u32[]{:S(2)}) %all-to-all-start.4) | async-done | bytes 2097184 | tf_op jit(solution)/shard_map/all_to_all | solution.py:106
  79.2 1.3 copy-done.2
  80.5 4.8 %all-to-all-start.6 = ((bf16[4,128,16,128]{3,1,0,2:T(8,128)(2,1)}), bf16[4,128,16,128]{3,1,0,2:T(8,128)(2,1)S(1)}, u32[]{:S(2)}, u32[]{:S(2)}) async-start(bf16[4,128,16,128]{3,1,0,2:T(8,128)(2,1)} %copy.54), calls=%async_computation.6 | async-start | bytes 4194304 | tf_op jit(solution)/shard_map/all_to_all | solution.py:106
  85.2 3.9 copy.44
  89.2 43.5 %all-to-all-done.6 = bf16[4,128,16,128]{3,1,0,2:T(8,128)(2,1)S(1)} async-done(((bf16[4,128,16,128]{3,1,0,2:T(8,128)(2,1)}), bf16[4,128,16,128]{3,1,0,2:T(8,128)(2,1)S(1)}, u32[]{:S(2)}, u32[]{:S(2)}) %all-to-all-start.6) | async-done | bytes 2097184 | tf_op jit(solution)/shard_map/all_to_all | solution.py:106
  132.7 1.3 copy-done.1
  134.0 4.8 %all-to-all-start.2 = ((bf16[4,128,16,128]{3,1,0,2:T(8,128)(2,1)}), bf16[4,128,16,128]{3,1,0,2:T(8,128)(2,1)S(1)}, u32[]{:S(2)}, u32[]{:S(2)}) async-start(bf16[4,128,16,128]{3,1,0,2:T(8,128)(2,1)} %copy.44), calls=%async_computation.2 | async-start | bytes 4194304 | tf_op jit(solution)/shard_map/all_to_all | solution.py:106
  138.8 3.9 copy.39
  142.7 43.5 %all-to-all-done.2 = bf16[4,128,16,128]{3,1,0,2:T(8,128)(2,1)S(1)} async-done(((bf16[4,128,16,128]{3,1,0,2:T(8,128)(2,1)}), bf16[4,128,16,128]{3,1,0,2:T(8,128)(2,1)S(1)}, u32[]{:S(2)}, u32[]{:S(2)}) %all-to-all-start.2) | async-done | bytes 2097184 | tf_op jit(solution)/shard_map/all_to_all | solution.py:106
  186.2 1.3 copy-done
  187.5 4.8 %all-to-all-start = ((bf16[4,128,16,128]{3,1,0,2:T(8,128)(2,1)}), bf16[4,128,16,128]{3,1,0,2:T(8,128)(2,1)S(1)}, u32[]{:S(2)}, u32[]{:S(2)}) async-start(bf16[4,128,16,128]{3,1,0,2:T(8,128)(2,1)} %copy.39), calls=%async_computation | async-start | bytes 4194304 | tf_op jit(solution)/shard_map/all_to_all | solution.py:106
  192.3 1.8 fusion.2
  194.1 36.0 %shard_map.69 = (bf16[2048,128]{1,0:T(8,128)(2,1)S(1)}, bf16[2048,128]{1,0:T(8,128)(2,1)S(1)}, bf16[2048,128]{1,0:T(8,128)(2,1)S(1)}) custom-call(bf16[2048,128]{1,0:T(8,128)(2,1)S(1)} %bitcast.106, bf16[2048,128]{1,0:T(8,128)(2,1)S(1)} %bitcast.105, bf16[2048,128]{1,0:T(8,128)(2,1)S(1)} %bitcast.104, bf16[2048,128]{1,0:T(8,128)(2,1)S(1)} %bitcast.103), custom_call_target="tpu_custom_call" | custom-call | tf_op jit(solution)/shard_map/pallas_call | solution.py:81
  230.1 1.3 pad_maximum_fusion.4
  231.4 8.4 %all-to-all-done = bf16[4,128,16,128]{3,1,0,2:T(8,128)(2,1)S(1)} async-done(((bf16[4,128,16,128]{3,1,0,2:T(8,128)(2,1)}), bf16[4,128,16,128]{3,1,0,2:T(8,128)(2,1)S(1)}, u32[]{:S(2)}, u32[]{:S(2)}) %all-to-all-start) | async-done | bytes 2097184 | tf_op jit(solution)/shard_map/all_to_all | solution.py:106
  239.7 4.8 %all-to-all-start.5 = ((bf16[3,16,128,1,128]{4,2,0,3,1:T(8,128)(2,1)}), bf16[3,16,128,1,128]{4,2,0,3,1:T(8,128)(2,1)}, u32[]{:S(2)}, u32[]{:S(2)}) async-start(bf16[3,16,128,1,128]{4,2,0,3,1:T(8,128)(2,1)} %pad_maximum_fusion.4), calls=%async_computation.5 | async-start | bytes 3145728 | tf_op jit(solution)/shard_map/all_to_all | solution.py:110
  244.5 1.8 fusion.3
  246.3 36.0 %shard_map.70 = (bf16[2048,128]{1,0:T(8,128)(2,1)S(1)}, bf16[2048,128]{1,0:T(8,128)(2,1)S(1)}, bf16[2048,128]{1,0:T(8,128)(2,1)S(1)}) custom-call(bf16[2048,128]{1,0:T(8,128)(2,1)S(1)} %bitcast.110, bf16[2048,128]{1,0:T(8,128)(2,1)S(1)} %bitcast.109, bf16[2048,128]{1,0:T(8,128)(2,1)S(1)} %bitcast.108, bf16[2048,128]{1,0:T(8,128)(2,1)S(1)} %bitcast.107), custom_call_target="tpu_custom_call" | custom-call | tf_op jit(solution)/shard_map/pallas_call | solution.py:81
  282.3 1.3 pad_maximum_fusion.5
  283.6 6.0 %all-to-all-start.7 = ((bf16[3,16,128,1,128]{4,2,3,0,1:T(8,128)(2,1)}), bf16[3,16,128,1,128]{4,2,3,0,1:T(8,128)(2,1)}, u32[]{:S(2)}, u32[]{:S(2)}) async-start(bf16[3,16,128,1,128]{4,2,3,0,1:T(8,128)(2,1)} %pad_maximum_fusion.5), calls=%async_computation.7 | async-start | bytes 3145728 | tf_op jit(solution)/shard_map/all_to_all | solution.py:110
  289.6 1.8 fusion.5
  291.4 36.0 %shard_map.68 = (bf16[2048,128]{1,0:T(8,128)(2,1)S(1)}, bf16[2048,128]{1,0:T(8,128)(2,1)S(1)}, bf16[2048,128]{1,0:T(8,128)(2,1)S(1)}) custom-call(bf16[2048,128]{1,0:T(8,128)(2,1)S(1)} %bitcast.114, bf16[2048,128]{1,0:T(8,128)(2,1)S(1)} %bitcast.113, bf16[2048,128]{1,0:T(8,128)(2,1)S(1)} %bitcast.112, bf16[2048,128]{1,0:T(8,128)(2,1)S(1)} %bitcast.111), custom_call_target="tpu_custom_call" | custom-call | tf_op jit(solution)/shard_map/pallas_call | solution.py:81
  327.3 1.3 pad_maximum_fusion.3
  328.7 0.0 all-to-all-done.7
  328.7 6.0 %all-to-all-start.3 = ((bf16[3,16,128,1,128]{4,2,0,3,1:T(8,128)(2,1)}), bf16[3,16,128,1,128]{4,2,0,3,1:T(8,128)(2,1)}, u32[]{:S(2)}, u32[]{:S(2)}) async-start(bf16[3,16,128,1,128]{4,2,0,3,1:T(8,128)(2,1)} %pad_maximum_fusion.3), calls=%async_computation.3 | async-start | bytes 3145728 | tf_op jit(solution)/shard_map/all_to_all | solution.py:110
  334.7 0.1 fusion.4
  334.8 36.0 %shard_map.67 = (bf16[2048,128]{1,0:T(8,128)(2,1)S(1)}, bf16[2048,128]{1,0:T(8,128)(2,1)S(1)}, bf16[2048,128]{1,0:T(8,128)(2,1)S(1)}) custom-call(bf16[2048,128]{1,0:T(8,128)(2,1)S(1)} %bitcast.118, bf16[2048,128]{1,0:T(8,128)(2,1)S(1)} %bitcast.117, bf16[2048,128]{1,0:T(8,128)(2,1)S(1)} %bitcast.116, bf16[2048,128]{1,0:T(8,128)(2,1)S(1)} %bitcast.115), custom_call_target="tpu_custom_call" | custom-call | tf_op jit(solution)/shard_map/pallas_call | solution.py:81
  370.8 1.3 pad_maximum_fusion.2
  372.1 6.0 %all-to-all-start.1 = ((bf16[3,16,128,1,128]{4,2,0,3,1:T(8,128)(2,1)}), bf16[3,16,128,1,128]{4,2,0,3,1:T(8,128)(2,1)S(1)}, u32[]{:S(2)}, u32[]{:S(2)}) async-start(bf16[3,16,128,1,128]{4,2,0,3,1:T(8,128)(2,1)} %pad_maximum_fusion.2), calls=%async_computation.1 | async-start | bytes 3145728 | tf_op jit(solution)/shard_map/all_to_all | solution.py:110
  378.1 1.9 copy.53
  380.0 2.6 copy.58
  382.6 2.6 copy.48
  385.2 29.1 %all-to-all-done.1 = bf16[3,16,128,1,128]{4,2,0,3,1:T(8,128)(2,1)S(1)} async-done(((bf16[3,16,128,1,128]{4,2,0,3,1:T(8,128)(2,1)}), bf16[3,16,128,1,128]{4,2,0,3,1:T(8,128)(2,1)S(1)}, u32[]{:S(2)}, u32[]{:S(2)}) %all-to-all-start.1) | async-done | bytes 1572896 | tf_op jit(solution)/shard_map/all_to_all | solution.py:110
  414.3 1.6 copy.43
  415.9 2.6 maximum_bitcast_fusion
  418.5 2.3 pad_maximum_fusion.1
  420.8 4.1 copy.61
  424.9 4.1 copy.59
  429.0 2.7 copy.60
  (5 shorter events, 0.0 us)
Async XLA Ops:
  25.2 53.9 %all-to-all-start.4 = ((bf16[4,128,16,128]{3,1,0,2:T(8,128)(2,1)}), bf16[4,128,16,128]{3,1,0,2:T(8,128)(2,1)S(1)}, u32[]{:S(2)}, u32[]{:S(2)}) async-start(bf16[4,128,16,128]{3,1,0,2:T(8,128)(2,1)} %copy.49), calls=%async_computation.4 | async-start | bytes 4194304 | tf_op jit(solution)/shard_map/all_to_all | solution.py:106
  79.2 1.3 copy-start.2
  80.5 52.2 %all-to-all-start.6 = ((bf16[4,128,16,128]{3,1,0,2:T(8,128)(2,1)}), bf16[4,128,16,128]{3,1,0,2:T(8,128)(2,1)S(1)}, u32[]{:S(2)}, u32[]{:S(2)}) async-start(bf16[4,128,16,128]{3,1,0,2:T(8,128)(2,1)} %copy.54), calls=%async_computation.6 | async-start | bytes 4194304 | tf_op jit(solution)/shard_map/all_to_all | solution.py:106
  132.7 1.3 copy-start.1
  134.0 52.2 %all-to-all-start.2 = ((bf16[4,128,16,128]{3,1,0,2:T(8,128)(2,1)}), bf16[4,128,16,128]{3,1,0,2:T(8,128)(2,1)S(1)}, u32[]{:S(2)}, u32[]{:S(2)}) async-start(bf16[4,128,16,128]{3,1,0,2:T(8,128)(2,1)} %copy.44), calls=%async_computation.2 | async-start | bytes 4194304 | tf_op jit(solution)/shard_map/all_to_all | solution.py:106
  186.2 1.3 copy-start
  187.5 52.2 %all-to-all-start = ((bf16[4,128,16,128]{3,1,0,2:T(8,128)(2,1)}), bf16[4,128,16,128]{3,1,0,2:T(8,128)(2,1)S(1)}, u32[]{:S(2)}, u32[]{:S(2)}) async-start(bf16[4,128,16,128]{3,1,0,2:T(8,128)(2,1)} %copy.39), calls=%async_computation | async-start | bytes 4194304 | tf_op jit(solution)/shard_map/all_to_all | solution.py:106
  239.7 43.8 %all-to-all-start.5 = ((bf16[3,16,128,1,128]{4,2,0,3,1:T(8,128)(2,1)}), bf16[3,16,128,1,128]{4,2,0,3,1:T(8,128)(2,1)}, u32[]{:S(2)}, u32[]{:S(2)}) async-start(bf16[3,16,128,1,128]{4,2,0,3,1:T(8,128)(2,1)} %pad_maximum_fusion.4), calls=%async_computation.5 | async-start | bytes 3145728 | tf_op jit(solution)/shard_map/all_to_all | solution.py:110
  283.6 45.1 %all-to-all-start.7 = ((bf16[3,16,128,1,128]{4,2,3,0,1:T(8,128)(2,1)}), bf16[3,16,128,1,128]{4,2,3,0,1:T(8,128)(2,1)}, u32[]{:S(2)}, u32[]{:S(2)}) async-start(bf16[3,16,128,1,128]{4,2,3,0,1:T(8,128)(2,1)} %pad_maximum_fusion.5), calls=%async_computation.7 | async-start | bytes 3145728 | tf_op jit(solution)/shard_map/all_to_all | solution.py:110
  328.7 43.5 %all-to-all-start.3 = ((bf16[3,16,128,1,128]{4,2,0,3,1:T(8,128)(2,1)}), bf16[3,16,128,1,128]{4,2,0,3,1:T(8,128)(2,1)}, u32[]{:S(2)}, u32[]{:S(2)}) async-start(bf16[3,16,128,1,128]{4,2,0,3,1:T(8,128)(2,1)} %pad_maximum_fusion.3), calls=%async_computation.3 | async-start | bytes 3145728 | tf_op jit(solution)/shard_map/all_to_all | solution.py:110
  372.1 42.2 %all-to-all-start.1 = ((bf16[3,16,128,1,128]{4,2,0,3,1:T(8,128)(2,1)}), bf16[3,16,128,1,128]{4,2,0,3,1:T(8,128)(2,1)S(1)}, u32[]{:S(2)}, u32[]{:S(2)}) async-start(bf16[3,16,128,1,128]{4,2,0,3,1:T(8,128)(2,1)} %pad_maximum_fusion.2), calls=%async_computation.1 | async-start | bytes 3145728 | tf_op jit(solution)/shard_map/all_to_all | solution.py:110

commit v4 on v3

--- a/solution.py
+++ b/solution.py
@@ -96,23 +96,26 @@
     seq_size = lax.psum(1, "seq")
     head_width = feature_width // HEADS
     per_dev = HEADS // seq_size
-    stacked = jnp.stack([queries, key_vectors, value_vectors, out_grad]).reshape(
-        4, page_count, tok_rows, seq_size, per_dev, head_width
-    )
-    chunk_out = {}
+    tokens_all = seq_size * tok_rows
+    inputs = (queries, key_vectors, value_vectors, out_grad)
+    outs = []
     for page in range(page_count):
+        part = jnp.stack(
+            [x[page].reshape(tok_rows, seq_size, per_dev, head_width) for x in inputs]
+        ).transpose(2, 0, 1, 3, 4)
+        arrived = lax.all_to_all(part, "seq", split_axis=0, concat_axis=0, tiled=True)
+        arrived = arrived.reshape(seq_size, 4, tok_rows, per_dev, head_width)
+        grads = []
         for head in range(per_dev):
-            part = stacked[:, page, :, :, head, :]
-            arrived = lax.all_to_all(part, "seq", split_axis=2, concat_axis=1, tiled=True)
-            arrived = arrived.reshape(4, seq_size * tok_rows, head_width)
-            grads = item_gradients(arrived[0], arrived[1], arrived[2], arrived[3])
-            grads = jnp.stack(grads).reshape(3, seq_size, tok_rows, 1, head_width)
-            returned = lax.all_to_all(grads, "seq", split_axis=1, concat_axis=3, tiled=True)
-            chunk_out[(page, head)] = returned.reshape(3, tok_rows, seq_size, head_width)
-    pages = []
-    for page in range(page_count):
-        pages.append(jnp.stack([chunk_out[(page, head)] for head in range(per_dev)], axis=3))
-    result = jnp.stack(pages, axis=1).reshape(3, page_count, tok_rows, feature_width)
+            items = [
+                arrived[:, a, :, head, :].reshape(tokens_all, head_width) for a in range(4)
+            ]
+            grads.append(jnp.stack(item_gradients(*items)))
+        grads = jnp.stack(grads).reshape(per_dev, 3, seq_size, tok_rows, head_width)
+        grads = grads.transpose(2, 1, 0, 3, 4)
+        returned = lax.all_to_all(grads, "seq", split_axis=0, concat_axis=0, tiled=True)
+        outs.append(returned.transpose(1, 3, 0, 2, 4).reshape(3, tok_rows, feature_width))
+    result = jnp.stack(outs, axis=1)
     return result[0], result[1], result[2]
 
 

time: 433 us -> 402 us (0.928)
  starting transfers between devices: 43.7 us -> 22.1 us
  waiting for transfers between devices: 168 us -> 161 us
    all_to_all x8 -> x4, starting transfers between devices: 43.7 us -> 22.1 us  [the longest x2 11.3 us: body(): lax.all_to_all(part, 'seq', split_axis=0, concat_axis=0, tiled=True)]
    squeeze x5 -> x0, local copies, waits for them, and re-layouts: 17.2 us -> none  [body(): part = stacked[:, page, :, :, head, :]]
    another operation x7 -> x0, other arithmetic: 14 us -> none  [the longest x4 5.23 us: body(): grads = jnp.stack(grads).reshape(3, seq_size, tok_rows, 1, head_width)]
    transpose x0 -> x2, local copies, waits for them, and re-layouts: none -> 12.8 us  [body(): part = jnp.stack([x[page].reshape(tok_rows, seq_size, per_dev, head_width...]
    transpose x0 -> x4, other arithmetic: none -> 10.8 us  [the longest x2 7.15 us: body(): part = jnp.stack([x[page].reshape(tok_rows, seq_size, per_dev, head_width...]
    slice x4 -> x6, local copies, waits for them, and re-layouts: 5.42 us -> 14.6 us  [the longest x4 9.12 us: body(): x[page].reshape(tok_rows, seq_size, per_dev, head_width)]
    unnamed x13 -> x19, local copies, waits for them, and re-layouts: 30.1 us -> 22.8 us
    all_to_all x8 -> x4, waiting for transfers between devices: 168 us -> 161 us  [the longest x2 94 us: body(): lax.all_to_all(part, 'seq', split_axis=0, concat_axis=0, tiled=True)]
  transfers between devices with their start and end apart: 8 -> 4, of which waited for: 5 -> 3; matrix products, arithmetic and copies ran while one was open for 7% -> 7% of each run, Pallas kernels for 33% -> 36%
where the time goes in v4:
time: 402 us; the launch traced here: 401 us
  waiting for transfers between devices  161 us (40%)
  Pallas kernels  144 us (36%)
  local copies, waits for them, and re-layouts  57.6 us (14%)
  starting transfers between devices  22.1 us (5%)
  other arithmetic  15.1 us (4%)
    pallas_call x4, Pallas kernels, item_gradients(): pl.pallas_call(_kernel, out_shape=(out, out, out), scratch_shapes=[pltpu....  144 us
    all_to_all x2, waiting for transfers between devices, body(): lax.all_to_all(part, 'seq', split_axis=0, concat_axis=0, tiled=True)  94 us
    all_to_all x2, waiting for transfers between devices, body(): lax.all_to_all(grads, 'seq', split_axis=0, concat_axis=0, tiled=True)  67.2 us
    unnamed x19, local copies, waits for them, and re-layouts  22.8 us
    transpose x2, local copies, waits for them, and re-layouts, body(): part = jnp.stack([x[page].reshape(tok_rows, seq_size, per_dev, head_width...  12.8 us
    all_to_all x2, starting transfers between devices, body(): lax.all_to_all(part, 'seq', split_axis=0, concat_axis=0, tiled=True)  11.3 us
    all_to_all x2, starting transfers between devices, body(): lax.all_to_all(grads, 'seq', split_axis=0, concat_axis=0, tiled=True)  10.8 us
    slice x4, local copies, waits for them, and re-layouts, body(): x[page].reshape(tok_rows, seq_size, per_dev, head_width)  9.12 us
  transfers between devices with their start and end apart: 4, of which 3 were waited for; matrix products, arithmetic and copies ran while one was open for 7% of the time, Pallas kernels for 36%

profile of v4, /device:TPU:13, one launch (start us, length us, event | category | flops | bytes accessed | tf_op | source)
XLA Modules:
  0.0 400.6 jit_solution(17694267121243131861)
XLA Ops:
  0.6 1.7 fusion.7
  2.3 1.3 copy.60
  3.6 1.7 fusion.8
  5.3 1.3 copy.61
  6.6 2.7 fusion.9
  9.3 2.3 copy.62
  11.6 3.1 fusion.10
  14.6 2.3 copy.63
  16.9 3.7 maximum_bitcast_fusion.1
  20.6 6.5 %copy.45 = bf16[16,4,128,2,128]{4,2,3,1,0:T(8,128)(2,1)} copy(bf16[16,4,128,2,128]{2,4,3,0,1:T(8,128)(2,1)} %maximum_bitcast_fusion.1) | data formatting | bytes 8388608 | tf_op jit(solution)/shard_map/transpose | solution.py:105
  27.1 6.5 %all-to-all-start.2 = ((bf16[16,4,128,2,128]{4,2,3,1,0:T(8,128)(2,1)}), bf16[16,4,128,2,128]{4,2,3,1,0:T(8,128)(2,1)}, u32[]{:S(2)}, u32[]{:S(2)}) async-start(bf16[16,4,128,2,128]{4,2,3,1,0:T(8,128)(2,1)} %copy.45), calls=%async_computation.2 | async-start | bytes 8388608 | tf_op jit(solution)/shard_map/all_to_all | solution.py:106
  33.6 1.4 copy.56
  34.9 0.0 copy-start.2
  35.0 1.3 copy.57
  36.2 0.0 copy-start.3
  36.3 1.3 copy.58
  37.6 0.0 copy-done.2
  37.6 0.7 copy.59
  38.2 0.0 copy-done.3
  38.2 3.4 maximum_bitcast_fusion
  41.7 6.3 %copy.33 = bf16[16,4,128,2,128]{4,2,3,1,0:T(8,128)(2,1)} copy(bf16[16,4,128,2,128]{2,4,3,0,1:T(8,128)(2,1)} %maximum_bitcast_fusion) | data formatting | bytes 8388608 | tf_op jit(solution)/shard_map/transpose | solution.py:105
  48.0 78.1 %all-to-all-done.2 = bf16[16,4,128,2,128]{4,2,3,1,0:T(8,128)(2,1)} async-done(((bf16[16,4,128,2,128]{4,2,3,1,0:T(8,128)(2,1)}), bf16[16,4,128,2,128]{4,2,3,1,0:T(8,128)(2,1)}, u32[]{:S(2)}, u32[]{:S(2)}) %all-to-all-start.2) | async-done | bytes 4194336 | tf_op jit(solution)/shard_map/all_to_all | solution.py:106
  126.1 4.8 %all-to-all-start = ((bf16[16,4,128,2,128]{4,2,3,1,0:T(8,128)(2,1)}), bf16[16,4,128,2,128]{4,2,3,1,0:T(8,128)(2,1)}, u32[]{:S(2)}, u32[]{:S(2)}) async-start(bf16[16,4,128,2,128]{4,2,3,1,0:T(8,128)(2,1)} %copy.33), calls=%async_computation | async-start | bytes 8388608 | tf_op jit(solution)/shard_map/all_to_all | solution.py:106
  130.8 2.7 fusion.5
  133.6 36.0 %shard_map.69 = (bf16[2048,128]{1,0:T(8,128)(2,1)S(1)}, bf16[2048,128]{1,0:T(8,128)(2,1)S(1)}, bf16[2048,128]{1,0:T(8,128)(2,1)S(1)}) custom-call(bf16[2048,128]{1,0:T(8,128)(2,1)S(1)} %bitcast.91, bf16[2048,128]{1,0:T(8,128)(2,1)S(1)} %bitcast.90, bf16[2048,128]{1,0:T(8,128)(2,1)S(1)} %bitcast.89, bf16[2048,128]{1,0:T(8,128)(2,1)S(1)} %bitcast.88), custom_call_target="tpu_custom_call" | custom-call | tf_op jit(solution)/shard_map/pallas_call | solution.py:81
  169.6 36.0 %shard_map.70 = (bf16[2048,128]{1,0:T(8,128)(2,1)S(1)}, bf16[2048,128]{1,0:T(8,128)(2,1)S(1)}, bf16[2048,128]{1,0:T(8,128)(2,1)S(1)}) custom-call(bf16[2048,128]{1,0:T(8,128)(2,1)S(1)} %bitcast.83, bf16[2048,128]{1,0:T(8,128)(2,1)S(1)} %bitcast.82, bf16[2048,128]{1,0:T(8,128)(2,1)S(1)} %bitcast.81, bf16[2048,128]{1,0:T(8,128)(2,1)S(1)} %bitcast.80), custom_call_target="tpu_custom_call" | custom-call | tf_op jit(solution)/shard_map/pallas_call | solution.py:81
  205.6 1.8 maximum_bitcast_fusion.3
  207.4 15.9 %all-to-all-done = bf16[16,4,128,2,128]{4,2,3,1,0:T(8,128)(2,1)} async-done(((bf16[16,4,128,2,128]{4,2,3,1,0:T(8,128)(2,1)}), bf16[16,4,128,2,128]{4,2,3,1,0:T(8,128)(2,1)}, u32[]{:S(2)}, u32[]{:S(2)}) %all-to-all-start) | async-done | bytes 4194336 | tf_op jit(solution)/shard_map/all_to_all | solution.py:106
  223.3 4.8 %all-to-all-start.3 = ((bf16[16,3,2,128,128]{4,3,1,2,0:T(8,128)(2,1)}), bf16[16,3,2,128,128]{4,3,1,2,0:T(8,128)(2,1)S(1)}, u32[]{:S(2)}, u32[]{:S(2)}) async-start(bf16[16,3,2,128,128]{4,3,1,2,0:T(8,128)(2,1)} %maximum_bitcast_fusion.3), calls=%async_computation.3 | async-start | bytes 6291456 | tf_op jit(solution)/shard_map/all_to_all | solution.py:116
  228.1 2.7 fusion.6
  230.8 36.0 %shard_map.67 = (bf16[2048,128]{1,0:T(8,128)(2,1)S(1)}, bf16[2048,128]{1,0:T(8,128)(2,1)S(1)}, bf16[2048,128]{1,0:T(8,128)(2,1)S(1)}) custom-call(bf16[2048,128]{1,0:T(8,128)(2,1)S(1)} %bitcast.95, bf16[2048,128]{1,0:T(8,128)(2,1)S(1)} %bitcast.94, bf16[2048,128]{1,0:T(8,128)(2,1)S(1)} %bitcast.93, bf16[2048,128]{1,0:T(8,128)(2,1)S(1)} %bitcast.92), custom_call_target="tpu_custom_call" | custom-call | tf_op jit(solution)/shard_map/pallas_call | solution.py:81
  266.8 36.0 %shard_map.68 = (bf16[2048,128]{1,0:T(8,128)(2,1)S(1)}, bf16[2048,128]{1,0:T(8,128)(2,1)S(1)}, bf16[2048,128]{1,0:T(8,128)(2,1)S(1)}) custom-call(bf16[2048,128]{1,0:T(8,128)(2,1)S(1)} %bitcast.87, bf16[2048,128]{1,0:T(8,128)(2,1)S(1)} %bitcast.86, bf16[2048,128]{1,0:T(8,128)(2,1)S(1)} %bitcast.85, bf16[2048,128]{1,0:T(8,128)(2,1)S(1)} %bitcast.84), custom_call_target="tpu_custom_call" | custom-call | tf_op jit(solution)/shard_map/pallas_call | solution.py:81
  302.8 1.9 maximum_bitcast_fusion.2
  304.7 0.0 all-to-all-done.3
  304.7 6.0 %all-to-all-start.1 = ((bf16[16,3,2,128,128]{4,3,1,2,0:T(8,128)(2,1)}), bf16[16,3,2,128,128]{4,3,1,2,0:T(8,128)(2,1)}, u32[]{:S(2)}, u32[]{:S(2)}) async-start(bf16[16,3,2,128,128]{4,3,1,2,0:T(8,128)(2,1)} %maximum_bitcast_fusion.2), calls=%async_computation.1 | async-start | bytes 6291456 | tf_op jit(solution)/shard_map/all_to_all | solution.py:116
  310.7 2.8 copy.52
  313.5 0.0 copy-start
  313.5 67.2 %all-to-all-done.1 = bf16[16,3,2,128,128]{4,3,1,2,0:T(8,128)(2,1)} async-done(((bf16[16,3,2,128,128]{4,3,1,2,0:T(8,128)(2,1)}), bf16[16,3,2,128,128]{4,3,1,2,0:T(8,128)(2,1)}, u32[]{:S(2)}, u32[]{:S(2)}) %all-to-all-start.1) | async-done | bytes 3145760 | tf_op jit(solution)/shard_map/all_to_all | solution.py:116
  380.7 4.6 %copy.40 = bf16[16,3,2,128,128]{3,4,2,0,1:T(8,128)(2,1)} copy(bf16[16,3,2,128,128]{4,3,1,2,0:T(8,128)(2,1)} %all-to-all-done.1) | data formatting | bytes 6291456 | tf_op jit(solution)/shard_map/all_to_all | solution.py:116
  385.3 0.0 copy-done
  385.3 4.3 %fusion.4 = (bf16[2,128,4096]{1,2,0:T(8,128)(2,1)}, bf16[2,128,4096]{1,2,0:T(8,128)(2,1)}, bf16[2,128,4096]{1,2,0:T(8,128)(2,1)}) fusion(bf16[3,1,128,4096]{2,3,0,1:T(8,128)(2,1)S(1)} %bitcast.108, bf16[3,1,128,4096]{2,3,0,1:T(8,128)(2,1)} %bitcast.109), kind=kLoop, calls=%fused_computation.13 | loop fusion | flops 3145728 | bytes 12582912 | tf_op jit(solution)/shard_map/squeeze | solution.py:119
  389.6 4.1 %copy.55 = bf16[2,128,4096]{2,1,0:T(8,128)(2,1)} copy(bf16[2,128,4096]{1,2,0:T(8,128)(2,1)} %get-tuple-element.30) | data formatting | bytes 4194304
  393.7 0.0 copy-start.1
  393.7 4.2 %copy.53 = bf16[2,128,4096]{2,1,0:T(8,128)(2,1)} copy(bf16[2,128,4096]{1,2,0:T(8,128)(2,1)} %get-tuple-element.31) | data formatting | bytes 4194304
  397.9 0.0 copy-done.1
  397.9 2.7 copy.54
Async XLA Ops:
  27.1 99.0 %all-to-all-start.2 = ((bf16[16,4,128,2,128]{4,2,3,1,0:T(8,128)(2,1)}), bf16[16,4,128,2,128]{4,2,3,1,0:T(8,128)(2,1)}, u32[]{:S(2)}, u32[]{:S(2)}) async-start(bf16[16,4,128,2,128]{4,2,3,1,0:T(8,128)(2,1)} %copy.45), calls=%async_computation.2 | async-start | bytes 8388608 | tf_op jit(solution)/shard_map/all_to_all | solution.py:106
  34.9 2.6 copy-start.2
  36.2 2.0 copy-start.3
  126.1 97.2 %all-to-all-start = ((bf16[16,4,128,2,128]{4,2,3,1,0:T(8,128)(2,1)}), bf16[16,4,128,2,128]{4,2,3,1,0:T(8,128)(2,1)}, u32[]{:S(2)}, u32[]{:S(2)}) async-start(bf16[16,4,128,2,128]{4,2,3,1,0:T(8,128)(2,1)} %copy.33), calls=%async_computation | async-start | bytes 8388608 | tf_op jit(solution)/shard_map/all_to_all | solution.py:106
  223.3 81.4 %all-to-all-start.3 = ((bf16[16,3,2,128,128]{4,3,1,2,0:T(8,128)(2,1)}), bf16[16,3,2,128,128]{4,3,1,2,0:T(8,128)(2,1)S(1)}, u32[]{:S(2)}, u32[]{:S(2)}) async-start(bf16[16,3,2,128,128]{4,3,1,2,0:T(8,128)(2,1)} %maximum_bitcast_fusion.3), calls=%async_computation.3 | async-start | bytes 6291456 | tf_op jit(solution)/shard_map/all_to_all | solution.py:116
  304.7 76.0 %all-to-all-start.1 = ((bf16[16,3,2,128,128]{4,3,1,2,0:T(8,128)(2,1)}), bf16[16,3,2,128,128]{4,3,1,2,0:T(8,128)(2,1)}, u32[]{:S(2)}, u32[]{:S(2)}) async-start(bf16[16,3,2,128,128]{4,3,1,2,0:T(8,128)(2,1)} %maximum_bitcast_fusion.2), calls=%async_computation.1 | async-start | bytes 6291456 | tf_op jit(solution)/shard_map/all_to_all | solution.py:116
  313.5 71.9 %copy-start = (bf16[16,3,2,128,128]{3,4,2,0,1:T(8,128)(2,1)S(1)}, bf16[16,3,2,128,128]{3,4,2,0,1:T(8,128)(2,1)}, u32[]{:S(2)}) copy-start(bf16[16,3,2,128,128]{3,4,2,0,1:T(8,128)(2,1)} %copy.52) | copy-start | bytes 9437188
  393.7 4.2 %copy-start.1 = (bf16[2,128,4096]{1,2,0:T(8,128)(2,1)S(1)}, bf16[2,128,4096]{1,2,0:T(8,128)(2,1)}, u32[]{:S(2)}) copy-start(bf16[2,128,4096]{1,2,0:T(8,128)(2,1)} %get-tuple-element.32) | copy-start | bytes 6291460

commit v5 on v4

--- a/solution.py
+++ b/solution.py
@@ -17,47 +17,47 @@
     dv_acc[...] = jnp.zeros_like(dv_acc)
     contract_rows = (((0,), (0,)), ((), ()))
     contract_cols = (((1,), (1,)), ((), ()))
+    row_ids = lax.broadcasted_iota(jnp.int32, (blk, blk), 0)
+    col_ids = lax.broadcasted_iota(jnp.int32, (blk, blk), 1)
 
     def row_block(i, carry):
         r0 = pl.multiple_of(i * blk, blk)
         q = q_ref[pl.ds(r0, blk), :]
         do = do_ref[pl.ds(r0, blk), :]
-        count = i + 1
 
-        def scores_pass(j, top):
+        def scores(j, masked):
             c0 = pl.multiple_of(j * blk, blk)
             s = lax.dot_general(q, k_ref[pl.ds(c0, blk), :], contract_cols,
                                 preferred_element_type=jnp.float32) * scale
-            rows = r0 + lax.broadcasted_iota(jnp.int32, (blk, blk), 0)
-            cols = c0 + lax.broadcasted_iota(jnp.int32, (blk, blk), 1)
-            s = jnp.where(rows >= cols, s, -jnp.inf)
+            if masked:
+                s = jnp.where(row_ids >= col_ids, s, -jnp.inf)
             s_scr[:, pl.ds(c0, blk)] = s
-            return jnp.maximum(top, jnp.max(s, axis=1, keepdims=True))
+            return jnp.max(s, axis=1, keepdims=True)
 
-        top = lax.fori_loop(0, count, scores_pass, jnp.full((blk, 1), -jnp.inf, jnp.float32))
+        top = lax.fori_loop(
+            0, i, lambda j, t: jnp.maximum(t, scores(j, False)),
+            jnp.full((blk, 1), -jnp.inf, jnp.float32))
+        top = jnp.maximum(top, scores(i, True))
 
-        def weights_pass(j, total):
+        def weights_pass(j, sums):
+            total, weighted = sums
             c0 = pl.multiple_of(j * blk, blk)
             w = jnp.exp(s_scr[:, pl.ds(c0, blk)] - top)
-            s_scr[:, pl.ds(c0, blk)] = w
-            return total + jnp.sum(w, axis=1, keepdims=True)
-
-        total = lax.fori_loop(0, count, weights_pass, jnp.zeros((blk, 1), jnp.float32))
-
-        def probs_pass(j, delta):
-            c0 = pl.multiple_of(j * blk, blk)
-            p = s_scr[:, pl.ds(c0, blk)] / total
             dp = lax.dot_general(do, v_ref[pl.ds(c0, blk), :], contract_cols,
                                  preferred_element_type=jnp.float32)
-            s_scr[:, pl.ds(c0, blk)] = p
+            s_scr[:, pl.ds(c0, blk)] = w
             dp_scr[:, pl.ds(c0, blk)] = dp
-            return delta + jnp.sum(p * dp, axis=1, keepdims=True)
+            return (total + jnp.sum(w, axis=1, keepdims=True),
+                    weighted + jnp.sum(w * dp, axis=1, keepdims=True))
 
-        delta = lax.fori_loop(0, count, probs_pass, jnp.zeros((blk, 1), jnp.float32))
+        zero_col = jnp.zeros((blk, 1), jnp.float32)
+        total, weighted = lax.fori_loop(0, i + 1, weights_pass, (zero_col, zero_col))
+        inv_total = 1.0 / total
+        delta = weighted * inv_total
 
         def grads_pass(j, dq):
             c0 = pl.multiple_of(j * blk, blk)
-            p = s_scr[:, pl.ds(c0, blk)]
+            p = s_scr[:, pl.ds(c0, blk)] * inv_total
             ds = (p * (dp_scr[:, pl.ds(c0, blk)] - delta)).astype(jnp.bfloat16)
             dq = dq + jnp.dot(ds, k_ref[pl.ds(c0, blk), :], preferred_element_type=jnp.float32)
             dk_acc[pl.ds(c0, blk), :] += lax.dot_general(
@@ -66,7 +66,7 @@
                 p.astype(jnp.bfloat16), do, contract_rows, preferred_element_type=jnp.float32)
             return dq
 
-        dq = lax.fori_loop(0, count, grads_pass, jnp.zeros((blk, head_width), jnp.float32))
+        dq = lax.fori_loop(0, i + 1, grads_pass, jnp.zeros((blk, head_width), jnp.float32))
         dq_ref[pl.ds(r0, blk), :] = (dq * scale).astype(dq_ref.dtype)
         return carry
 

time: 402 us -> 394 us (0.980)
  Pallas kernels: 144 us -> 128 us
  waiting for transfers between devices: 161 us -> 170 us
    pallas_call x4, Pallas kernels: 144 us -> 128 us  [item_gradients(): pl.pallas_call(_kernel, out_shape=(out, out, out), scratch_shapes=[pltpu....]
    all_to_all x2, waiting for transfers between devices: 94 us -> 102 us  [body(): lax.all_to_all(part, 'seq', split_axis=0, concat_axis=0, tiled=True)]
  transfers between devices with their start and end apart: 4 -> 4, of which waited for: 3 -> 4; matrix products, arithmetic and copies ran while one was open for 7% -> 7% of each run, Pallas kernels for 36% -> 33%
where the time goes in v5:
time: 394 us; the launch traced here: 393 us
  waiting for transfers between devices  170 us (43%)
  Pallas kernels  128 us (32%)
  local copies, waits for them, and re-layouts  57.6 us (15%)
  starting transfers between devices  21.1 us (5%)
  other arithmetic  15.1 us (4%)
    pallas_call x4, Pallas kernels, item_gradients(): pl.pallas_call(_kernel, out_shape=(out, out, out), scratch_shapes=[pltpu....  128 us
    all_to_all x2, waiting for transfers between devices, body(): lax.all_to_all(part, 'seq', split_axis=0, concat_axis=0, tiled=True)  102 us
    all_to_all x2, waiting for transfers between devices, body(): lax.all_to_all(grads, 'seq', split_axis=0, concat_axis=0, tiled=True)  68.2 us
    unnamed x19, local copies, waits for them, and re-layouts  22.8 us
    transpose x2, local copies, waits for them, and re-layouts, body(): part = jnp.stack([x[page].reshape(tok_rows, seq_size, per_dev, head_width...  12.8 us
    all_to_all x2, starting transfers between devices, body(): lax.all_to_all(part, 'seq', split_axis=0, concat_axis=0, tiled=True)  11.3 us
    all_to_all x2, starting transfers between devices, body(): lax.all_to_all(grads, 'seq', split_axis=0, concat_axis=0, tiled=True)  9.77 us
    slice x4, local copies, waits for them, and re-layouts, body(): x[page].reshape(tok_rows, seq_size, per_dev, head_width)  9.12 us
  transfers between devices with their start and end apart: 4, of which 4 were waited for; matrix products, arithmetic and copies ran while one was open for 7% of the time, Pallas kernels for 33%

profile of v5, /device:TPU:13, one launch (start us, length us, event | category | flops | bytes accessed | tf_op | source)
XLA Modules:
  0.0 392.9 jit_solution(2319830632979088431)
XLA Ops:
  0.6 1.7 fusion.7
  2.3 1.3 copy.60
  3.6 1.7 fusion.8
  5.3 1.3 copy.61
  6.6 2.7 fusion.9
  9.3 2.3 copy.62
  11.6 3.1 fusion.10
  14.6 2.3 copy.63
  16.9 3.7 maximum_bitcast_fusion.1
  20.6 6.5 %copy.45 = bf16[16,4,128,2,128]{4,2,3,1,0:T(8,128)(2,1)} copy(bf16[16,4,128,2,128]{2,4,3,0,1:T(8,128)(2,1)} %maximum_bitcast_fusion.1) | data formatting | bytes 8388608 | tf_op jit(solution)/shard_map/transpose | solution.py:105
  27.1 6.5 %all-to-all-start.2 = ((bf16[16,4,128,2,128]{4,2,3,1,0:T(8,128)(2,1)}), bf16[16,4,128,2,128]{4,2,3,1,0:T(8,128)(2,1)}, u32[]{:S(2)}, u32[]{:S(2)}) async-start(bf16[16,4,128,2,128]{4,2,3,1,0:T(8,128)(2,1)} %copy.45), calls=%async_computation.2 | async-start | bytes 8388608 | tf_op jit(solution)/shard_map/all_to_all | solution.py:106
  33.6 1.4 copy.56
  34.9 0.0 copy-start.2
  35.0 1.3 copy.57
  36.2 0.0 copy-start.3
  36.3 1.3 copy.58
  37.6 0.0 copy-done.2
  37.6 0.7 copy.59
  38.2 0.0 copy-done.3
  38.2 3.4 maximum_bitcast_fusion
  41.7 6.3 %copy.33 = bf16[16,4,128,2,128]{4,2,3,1,0:T(8,128)(2,1)} copy(bf16[16,4,128,2,128]{2,4,3,0,1:T(8,128)(2,1)} %maximum_bitcast_fusion) | data formatting | bytes 8388608 | tf_op jit(solution)/shard_map/transpose | solution.py:105
  48.0 78.1 %all-to-all-done.2 = bf16[16,4,128,2,128]{4,2,3,1,0:T(8,128)(2,1)} async-done(((bf16[16,4,128,2,128]{4,2,3,1,0:T(8,128)(2,1)}), bf16[16,4,128,2,128]{4,2,3,1,0:T(8,128)(2,1)}, u32[]{:S(2)}, u32[]{:S(2)}) %all-to-all-start.2) | async-done | bytes 4194336 | tf_op jit(solution)/shard_map/all_to_all | solution.py:106
  126.1 4.8 %all-to-all-start = ((bf16[16,4,128,2,128]{4,2,3,1,0:T(8,128)(2,1)}), bf16[16,4,128,2,128]{4,2,3,1,0:T(8,128)(2,1)}, u32[]{:S(2)}, u32[]{:S(2)}) async-start(bf16[16,4,128,2,128]{4,2,3,1,0:T(8,128)(2,1)} %copy.33), calls=%async_computation | async-start | bytes 8388608 | tf_op jit(solution)/shard_map/all_to_all | solution.py:106
  130.8 2.7 fusion.5
  133.6 32.1 %shard_map.69 = (bf16[2048,128]{1,0:T(8,128)(2,1)S(1)}, bf16[2048,128]{1,0:T(8,128)(2,1)S(1)}, bf16[2048,128]{1,0:T(8,128)(2,1)S(1)}) custom-call(bf16[2048,128]{1,0:T(8,128)(2,1)S(1)} %bitcast.91, bf16[2048,128]{1,0:T(8,128)(2,1)S(1)} %bitcast.90, bf16[2048,128]{1,0:T(8,128)(2,1)S(1)} %bitcast.89, bf16[2048,128]{1,0:T(8,128)(2,1)S(1)} %bitcast.88), custom_call_target="tpu_custom_call" | custom-call | tf_op jit(solution)/shard_map/pallas_call | solution.py:81
  165.7 32.1 %shard_map.70 = (bf16[2048,128]{1,0:T(8,128)(2,1)S(1)}, bf16[2048,128]{1,0:T(8,128)(2,1)S(1)}, bf16[2048,128]{1,0:T(8,128)(2,1)S(1)}) custom-call(bf16[2048,128]{1,0:T(8,128)(2,1)S(1)} %bitcast.83, bf16[2048,128]{1,0:T(8,128)(2,1)S(1)} %bitcast.82, bf16[2048,128]{1,0:T(8,128)(2,1)S(1)} %bitcast.81, bf16[2048,128]{1,0:T(8,128)(2,1)S(1)} %bitcast.80), custom_call_target="tpu_custom_call" | custom-call | tf_op jit(solution)/shard_map/pallas_call | solution.py:81
  197.8 1.8 maximum_bitcast_fusion.3
  199.7 23.6 %all-to-all-done = bf16[16,4,128,2,128]{4,2,3,1,0:T(8,128)(2,1)} async-done(((bf16[16,4,128,2,128]{4,2,3,1,0:T(8,128)(2,1)}), bf16[16,4,128,2,128]{4,2,3,1,0:T(8,128)(2,1)}, u32[]{:S(2)}, u32[]{:S(2)}) %all-to-all-start) | async-done | bytes 4194336 | tf_op jit(solution)/shard_map/all_to_all | solution.py:106
  223.3 4.8 %all-to-all-start.3 = ((bf16[16,3,2,128,128]{4,3,1,2,0:T(8,128)(2,1)}), bf16[16,3,2,128,128]{4,3,1,2,0:T(8,128)(2,1)S(1)}, u32[]{:S(2)}, u32[]{:S(2)}) async-start(bf16[16,3,2,128,128]{4,3,1,2,0:T(8,128)(2,1)} %maximum_bitcast_fusion.3), calls=%async_computation.3 | async-start | bytes 6291456 | tf_op jit(solution)/shard_map/all_to_all | solution.py:116
  228.1 2.7 fusion.6
  230.8 32.1 %shard_map.67 = (bf16[2048,128]{1,0:T(8,128)(2,1)S(1)}, bf16[2048,128]{1,0:T(8,128)(2,1)S(1)}, bf16[2048,128]{1,0:T(8,128)(2,1)S(1)}) custom-call(bf16[2048,128]{1,0:T(8,128)(2,1)S(1)} %bitcast.95, bf16[2048,128]{1,0:T(8,128)(2,1)S(1)} %bitcast.94, bf16[2048,128]{1,0:T(8,128)(2,1)S(1)} %bitcast.93, bf16[2048,128]{1,0:T(8,128)(2,1)S(1)} %bitcast.92), custom_call_target="tpu_custom_call" | custom-call | tf_op jit(solution)/shard_map/pallas_call | solution.py:81
  263.0 32.1 %shard_map.68 = (bf16[2048,128]{1,0:T(8,128)(2,1)S(1)}, bf16[2048,128]{1,0:T(8,128)(2,1)S(1)}, bf16[2048,128]{1,0:T(8,128)(2,1)S(1)}) custom-call(bf16[2048,128]{1,0:T(8,128)(2,1)S(1)} %bitcast.87, bf16[2048,128]{1,0:T(8,128)(2,1)S(1)} %bitcast.86, bf16[2048,128]{1,0:T(8,128)(2,1)S(1)} %bitcast.85, bf16[2048,128]{1,0:T(8,128)(2,1)S(1)} %bitcast.84), custom_call_target="tpu_custom_call" | custom-call | tf_op jit(solution)/shard_map/pallas_call | solution.py:81
  295.1 1.9 maximum_bitcast_fusion.2
  296.9 1.0 all-to-all-done.3
  298.0 5.0 %all-to-all-start.1 = ((bf16[16,3,2,128,128]{4,3,1,2,0:T(8,128)(2,1)}), bf16[16,3,2,128,128]{4,3,1,2,0:T(8,128)(2,1)}, u32[]{:S(2)}, u32[]{:S(2)}) async-start(bf16[16,3,2,128,128]{4,3,1,2,0:T(8,128)(2,1)} %maximum_bitcast_fusion.2), calls=%async_computation.1 | async-start | bytes 6291456 | tf_op jit(solution)/shard_map/all_to_all | solution.py:116
  303.0 2.8 copy.52
  305.8 0.0 copy-start
  305.8 67.2 %all-to-all-done.1 = bf16[16,3,2,128,128]{4,3,1,2,0:T(8,128)(2,1)} async-done(((bf16[16,3,2,128,128]{4,3,1,2,0:T(8,128)(2,1)}), bf16[16,3,2,128,128]{4,3,1,2,0:T(8,128)(2,1)}, u32[]{:S(2)}, u32[]{:S(2)}) %all-to-all-start.1) | async-done | bytes 3145760 | tf_op jit(solution)/shard_map/all_to_all | solution.py:116
  373.0 4.6 %copy.40 = bf16[16,3,2,128,128]{3,4,2,0,1:T(8,128)(2,1)} copy(bf16[16,3,2,128,128]{4,3,1,2,0:T(8,128)(2,1)} %all-to-all-done.1) | data formatting | bytes 6291456 | tf_op jit(solution)/shard_map/all_to_all | solution.py:116
  377.6 0.0 copy-done
  377.6 4.3 %fusion.4 = (bf16[2,128,4096]{1,2,0:T(8,128)(2,1)}, bf16[2,128,4096]{1,2,0:T(8,128)(2,1)}, bf16[2,128,4096]{1,2,0:T(8,128)(2,1)}) fusion(bf16[3,1,128,4096]{2,3,0,1:T(8,128)(2,1)S(1)} %bitcast.108, bf16[3,1,128,4096]{2,3,0,1:T(8,128)(2,1)} %bitcast.109), kind=kLoop, calls=%fused_computation.13 | loop fusion | flops 3145728 | bytes 12582912 | tf_op jit(solution)/shard_map/squeeze | solution.py:119
  381.9 4.1 %copy.55 = bf16[2,128,4096]{2,1,0:T(8,128)(2,1)} copy(bf16[2,128,4096]{1,2,0:T(8,128)(2,1)} %get-tuple-element.30) | data formatting | bytes 4194304
  386.0 0.0 copy-start.1
  386.0 4.2 %copy.53 = bf16[2,128,4096]{2,1,0:T(8,128)(2,1)} copy(bf16[2,128,4096]{1,2,0:T(8,128)(2,1)} %get-tuple-element.31) | data formatting | bytes 4194304
  390.2 0.0 copy-done.1
  390.2 2.7 copy.54
Async XLA Ops:
  27.1 99.0 %all-to-all-start.2 = ((bf16[16,4,128,2,128]{4,2,3,1,0:T(8,128)(2,1)}), bf16[16,4,128,2,128]{4,2,3,1,0:T(8,128)(2,1)}, u32[]{:S(2)}, u32[]{:S(2)}) async-start(bf16[16,4,128,2,128]{4,2,3,1,0:T(8,128)(2,1)} %copy.45), calls=%async_computation.2 | async-start | bytes 8388608 | tf_op jit(solution)/shard_map/all_to_all | solution.py:106
  34.9 2.6 copy-start.2
  36.2 2.0 copy-start.3
  126.1 97.2 %all-to-all-start = ((bf16[16,4,128,2,128]{4,2,3,1,0:T(8,128)(2,1)}), bf16[16,4,128,2,128]{4,2,3,1,0:T(8,128)(2,1)}, u32[]{:S(2)}, u32[]{:S(2)}) async-start(bf16[16,4,128,2,128]{4,2,3,1,0:T(8,128)(2,1)} %copy.33), calls=%async_computation | async-start | bytes 8388608 | tf_op jit(solution)/shard_map/all_to_all | solution.py:106
  223.3 74.7 %all-to-all-start.3 = ((bf16[16,3,2,128,128]{4,3,1,2,0:T(8,128)(2,1)}), bf16[16,3,2,128,128]{4,3,1,2,0:T(8,128)(2,1)S(1)}, u32[]{:S(2)}, u32[]{:S(2)}) async-start(bf16[16,3,2,128,128]{4,3,1,2,0:T(8,128)(2,1)} %maximum_bitcast_fusion.3), calls=%async_computation.3 | async-start | bytes 6291456 | tf_op jit(solution)/shard_map/all_to_all | solution.py:116
  298.0 75.0 %all-to-all-start.1 = ((bf16[16,3,2,128,128]{4,3,1,2,0:T(8,128)(2,1)}), bf16[16,3,2,128,128]{4,3,1,2,0:T(8,128)(2,1)}, u32[]{:S(2)}, u32[]{:S(2)}) async-start(bf16[16,3,2,128,128]{4,3,1,2,0:T(8,128)(2,1)} %maximum_bitcast_fusion.2), calls=%async_computation.1 | async-start | bytes 6291456 | tf_op jit(solution)/shard_map/all_to_all | solution.py:116
  305.8 71.9 %copy-start = (bf16[16,3,2,128,128]{3,4,2,0,1:T(8,128)(2,1)S(1)}, bf16[16,3,2,128,128]{3,4,2,0,1:T(8,128)(2,1)}, u32[]{:S(2)}) copy-start(bf16[16,3,2,128,128]{3,4,2,0,1:T(8,128)(2,1)} %copy.52) | copy-start | bytes 9437188
  386.0 4.2 %copy-start.1 = (bf16[2,128,4096]{1,2,0:T(8,128)(2,1)S(1)}, bf16[2,128,4096]{1,2,0:T(8,128)(2,1)}, u32[]{:S(2)}) copy-start(bf16[2,128,4096]{1,2,0:T(8,128)(2,1)} %get-tuple-element.32) | copy-start | bytes 6291460

commit v6 on v5

v6 whole, which is shorter than its diff:
```python
import jax
import jax.numpy as jnp
from jax import lax
from jax.experimental import pallas as pl
from jax.experimental.pallas import tpu as pltpu
from jax.sharding import PartitionSpec as P

HEADS = 32
BLOCK = 256


def _kernel(q_ref, k_ref, kt_ref, v_ref, do_ref, dqt_ref, dk_ref, dv_ref, s_scr, dp_scr, dk_acc, dv_acc):
    tokens_all, head_width = q_ref.shape
    blk = BLOCK
    scale = head_width ** (-0.5)
    dk_acc[...] = jnp.zeros_like(dk_acc)
    dv_acc[...] = jnp.zeros_like(dv_acc)
    contract_cols = (((1,), (1,)), ((), ()))
    key_ids = lax.broadcasted_iota(jnp.int32, (blk, blk), 0)
    query_ids = lax.broadcasted_iota(jnp.int32, (blk, blk), 1)

    def query_block(i, carry):
        r0 = pl.multiple_of(i * blk, blk)
        q = q_ref[pl.ds(r0, blk), :]
        do = do_ref[pl.ds(r0, blk), :]

        def scores(j, masked):
            c0 = pl.multiple_of(j * blk, blk)
            s = lax.dot_general(k_ref[pl.ds(c0, blk), :], q, contract_cols,
                                preferred_element_type=jnp.float32) * scale
            if masked:
                s = jnp.where(query_ids >= key_ids, s, -jnp.inf)
            s_scr[pl.ds(c0, blk), :] = s
            return jnp.max(s, axis=0, keepdims=True)

        top = lax.fori_loop(
            0, i, lambda j, t: jnp.maximum(t, scores(j, False)),
            jnp.full((1, blk), -jnp.inf, jnp.float32))
        top = jnp.maximum(top, scores(i, True))

        def weights_pass(j, sums):
            total, weighted = sums
            c0 = pl.multiple_of(j * blk, blk)
            w = jnp.exp(s_scr[pl.ds(c0, blk), :] - top)
            dp = lax.dot_general(v_ref[pl.ds(c0, blk), :], do, contract_cols,
                                 preferred_element_type=jnp.float32)
            s_scr[pl.ds(c0, blk), :] = w
            dp_scr[pl.ds(c0, blk), :] = dp
            return (total + jnp.sum(w, axis=0, keepdims=True),
                    weighted + jnp.sum(w * dp, axis=0, keepdims=True))

        zero_row = jnp.zeros((1, blk), jnp.float32)
        total, weighted = lax.fori_loop(0, i + 1, weights_pass, (zero_row, zero_row))
        inv_total = 1.0 / total
        delta = weighted * inv_total

        def grads_pass(j, dqt):
            c0 = pl.multiple_of(j * blk, blk)
            p = s_scr[pl.ds(c0, blk), :] * inv_total
            ds = (p * (dp_scr[pl.ds(c0, blk), :] - delta)).astype(jnp.bfloat16)
            dqt = dqt + jnp.dot(kt_ref[:, pl.ds(c0, blk)], ds, preferred_element_type=jnp.float32)
            dk_acc[pl.ds(c0, blk), :] += jnp.dot(ds, q, preferred_element_type=jnp.float32)
            dv_acc[pl.ds(c0, blk), :] += jnp.dot(
                p.astype(jnp.bfloat16), do, preferred_element_type=jnp.float32)
            return dqt

        dqt = lax.fori_loop(0, i + 1, grads_pass, jnp.zeros((head_width, blk), jnp.float32))
        dqt_ref[:, pl.ds(r0, blk)] = (dqt * scale).astype(dqt_ref.dtype)
        return carry

    lax.fori_loop(0, tokens_all // blk, query_block, 0)
    dk_ref[...] = (dk_acc[...] * scale).astype(dk_ref.dtype)
    dv_ref[...] = dv_acc[...].astype(dv_ref.dtype)


def item_gradients(queries, key_vectors, value_vectors, out_grad):
    tokens_all, head_width = queries.shape
    out = jax.ShapeDtypeStruct((tokens_all, head_width), jnp.bfloat16)
    out_t = jax.ShapeDtypeStruct((head_width, tokens_all), jnp.bfloat16)
    dqt, dk, dv = pl.pallas_call(
        _kernel,
        out_shape=(out_t, out, out),
        scratch_shapes=[
            pltpu.VMEM((tokens_all, BLOCK), jnp.float32),
            pltpu.VMEM((tokens_all, BLOCK), jnp.float32),
            pltpu.VMEM((tokens_all, head_width), jnp.float32),
            pltpu.VMEM((tokens_all, head_width), jnp.float32),
        ],
        compiler_params=pltpu.CompilerParams(vmem_limit_bytes=32 * 1024 * 1024),
    )(queries, key_vectors, key_vectors.T, value_vectors, out_grad)
    return dqt.T, dk, dv


def body(queries, key_vectors, value_vectors, out_grad):
    page_count, tok_rows, feature_width = queries.shape
    seq_size = lax.psum(1, "seq")
    head_width = feature_width // HEADS
    per_dev = HEADS // seq_size
    tokens_all = seq_size * tok_rows
    inputs = (queries, key_vectors, value_vectors, out_grad)
    outs = []
    for page in range(page_count):
        part = jnp.stack(
            [x[page].reshape(tok_rows, seq_size, per_dev, head_width) for x in inputs]
        ).transpose(2, 0, 1, 3, 4)
        arrived = lax.all_to_all(part, "seq", split_axis=0, concat_axis=0, tiled=True)
        arrived = arrived.reshape(seq_size, 4, tok_rows, per_dev, head_width)
        grads = []
        for head in range(per_dev):
            items = [
                arrived[:, a, :, head, :].reshape(tokens_all, head_width) for a in range(4)
            ]
            grads.append(jnp.stack(item_gradients(*items)))
        grads = jnp.stack(grads).reshape(per_dev, 3, seq_size, tok_rows, head_width)
        grads = grads.transpose(2, 1, 0, 3, 4)
        returned = lax.all_to_all(grads, "seq", split_axis=0, concat_axis=0, tiled=True)
        outs.append(returned.transpose(1, 3, 0, 2, 4).reshape(3, tok_rows, feature_width))
    result = jnp.stack(outs, axis=1)
    return result[0], result[1], result[2]


def solution(mesh):
    placed = P("group", "seq", None)
    return jax.shard_map(
        body,
        mesh=mesh,
        in_specs=(placed, placed, placed, placed),
        out_specs=(placed, placed, placed),
        check_vma=False,
    )
```

time: 394 us -> 393 us (level)
  Pallas kernels: 128 us -> 98.4 us
  local copies, waits for them, and re-layouts: 57.6 us -> 84.4 us
    pallas_call x4, Pallas kernels: 128 us -> 98.4 us  [item_gradients(): pl.pallas_call(_kernel, out_shape=(out_t, out, out), scratch_shapes=[pltp...]
    unnamed x19 -> x55, local copies, waits for them, and re-layouts: 22.8 us -> 38.5 us
    another operation x0 -> x8, local copies, waits for them, and re-layouts: none -> 9.27 us  [the longest x4 6.83 us: body(): grads.append(jnp.stack(item_gradients(*items)))]
  transfers between devices with their start and end apart: 4 -> 4, of which waited for: 4 -> 4; matrix products, arithmetic and copies ran while one was open for 7% -> 11% of each run, Pallas kernels for 33% -> 25%
where the time goes in v6:
time: 393 us; the launch traced here: 391 us
  waiting for transfers between devices  169 us (43%)
  Pallas kernels  98.4 us (25%)
  local copies, waits for them, and re-layouts  84.4 us (21%)
  starting transfers between devices  20.9 us (5%)
  other arithmetic  17.7 us (5%)
    all_to_all x2, waiting for transfers between devices, body(): lax.all_to_all(part, 'seq', split_axis=0, concat_axis=0, tiled=True)  102 us
    pallas_call x4, Pallas kernels, item_gradients(): pl.pallas_call(_kernel, out_shape=(out_t, out, out), scratch_shapes=[pltp...  98.4 us
    all_to_all x2, waiting for transfers between devices, body(): lax.all_to_all(grads, 'seq', split_axis=0, concat_axis=0, tiled=True)  66.7 us
    unnamed x55, local copies, waits for them, and re-layouts  38.5 us
    transpose x2, local copies, waits for them, and re-layouts, body(): part = jnp.stack([x[page].reshape(tok_rows, seq_size, per_dev, head_width...  12.9 us
    all_to_all x2, starting transfers between devices, body(): lax.all_to_all(part, 'seq', split_axis=0, concat_axis=0, tiled=True)  11.3 us
    all_to_all x2, starting transfers between devices, body(): lax.all_to_all(grads, 'seq', split_axis=0, concat_axis=0, tiled=True)  9.56 us
    slice x4, local copies, waits for them, and re-layouts, body(): x[page].reshape(tok_rows, seq_size, per_dev, head_width)  9.12 us
  transfers between devices with their start and end apart: 4, of which 4 were waited for; matrix products, arithmetic and copies ran while one was open for 11% of the time, Pallas kernels for 25%

profile of v6, /device:TPU:13, one launch (start us, length us, event | category | flops | bytes accessed | tf_op | source)
XLA Modules:
  0.0 391.0 jit_solution(17004195092276112002)
XLA Ops:
  0.6 1.7 fusion.7
  2.3 1.3 copy.96
  3.6 1.7 fusion.8
  5.3 1.3 copy.97
  6.6 2.7 fusion.9
  9.3 2.3 copy.98
  11.6 3.1 fusion.10
  14.7 2.3 copy.99
  16.9 3.8 maximum_bitcast_fusion.1
  20.7 6.5 %copy.69 = bf16[16,4,128,2,128]{4,2,3,1,0:T(8,128)(2,1)} copy(bf16[16,4,128,2,128]{2,4,3,0,1:T(8,128)(2,1)} %maximum_bitcast_fusion.1) | data formatting | bytes 8388608 | tf_op jit(solution)/shard_map/transpose | solution.py:105
  27.2 6.5 %all-to-all-start.2 = ((bf16[16,4,128,2,128]{4,2,3,1,0:T(8,128)(2,1)}), bf16[16,4,128,2,128]{4,2,3,1,0:T(8,128)(2,1)}, u32[]{:S(2)}, u32[]{:S(2)}) async-start(bf16[16,4,128,2,128]{4,2,3,1,0:T(8,128)(2,1)} %copy.69), calls=%async_computation.2 | async-start | bytes 8388608 | tf_op jit(solution)/shard_map/all_to_all | solution.py:106
  33.7 1.3 copy.92
  35.1 1.3 copy.93
  36.4 1.3 copy.94
  38.3 3.4 maximum_bitcast_fusion
  41.8 6.4 %copy.53 = bf16[16,4,128,2,128]{4,2,3,1,0:T(8,128)(2,1)} copy(bf16[16,4,128,2,128]{2,4,3,0,1:T(8,128)(2,1)} %maximum_bitcast_fusion) | data formatting | bytes 8388608 | tf_op jit(solution)/shard_map/transpose | solution.py:105
  48.2 78.0 %all-to-all-done.2 = bf16[16,4,128,2,128]{4,2,3,1,0:T(8,128)(2,1)} async-done(((bf16[16,4,128,2,128]{4,2,3,1,0:T(8,128)(2,1)}), bf16[16,4,128,2,128]{4,2,3,1,0:T(8,128)(2,1)}, u32[]{:S(2)}, u32[]{:S(2)}) %all-to-all-start.2) | async-done | bytes 4194336 | tf_op jit(solution)/shard_map/all_to_all | solution.py:106
  126.2 4.8 %all-to-all-start = ((bf16[16,4,128,2,128]{4,2,3,1,0:T(8,128)(2,1)}), bf16[16,4,128,2,128]{4,2,3,1,0:T(8,128)(2,1)}, u32[]{:S(2)}, u32[]{:S(2)}) async-start(bf16[16,4,128,2,128]{4,2,3,1,0:T(8,128)(2,1)} %copy.53), calls=%async_computation | async-start | bytes 8388608 | tf_op jit(solution)/shard_map/all_to_all | solution.py:106
  131.0 3.5 fusion.5
  134.5 1.0 copy.90
  135.5 1.0 copy-done
  136.6 1.0 copy-done.1
  137.6 1.0 copy-done.4
  138.7 24.6 %shard_map.70 = (bf16[128,2048]{1,0:T(8,128)(2,1)S(1)}, bf16[2048,128]{1,0:T(8,128)(2,1)S(1)}, bf16[2048,128]{1,0:T(8,128)(2,1)S(1)}) custom-call(bf16[2048,128]{1,0:T(8,128)(2,1)S(1)} %bitcast.96, bf16[2048,128]{1,0:T(8,128)(2,1)S(1)} %bitcast.85, bf16[128,2048]{1,0:T(8,128)(2,1)S(1)} %bitcast.102, bf16[2048,128]{1,0:T(8,128)(2,1)S(1)} %bitcast.95, ...), custom_call_target="tpu_custom_call" | custom-call | tf_op jit(solution)/shard_map/pallas_call | solution.py:80
  165.7 2.1 copy.91
  168.0 24.6 %shard_map.69 = (bf16[128,2048]{1,0:T(8,128)(2,1)S(1)}, bf16[2048,128]{1,0:T(8,128)(2,1)S(1)}, bf16[2048,128]{1,0:T(8,128)(2,1)S(1)}) custom-call(bf16[2048,128]{1,0:T(8,128)(2,1)S(1)} %bitcast.90, bf16[2048,128]{1,0:T(8,128)(2,1)S(1)} %bitcast.81, bf16[128,2048]{1,0:T(8,128)(2,1)S(1)} %bitcast.100, bf16[2048,128]{1,0:T(8,128)(2,1)S(1)} %bitcast.89, ...), custom_call_target="tpu_custom_call" | custom-call | tf_op jit(solution)/shard_map/pallas_call | solution.py:80
  195.1 1.3 copy.89
  196.4 3.0 maximum_bitcast_fusion.3
  199.4 24.1 %all-to-all-done = bf16[16,4,128,2,128]{4,2,3,1,0:T(8,128)(2,1)} async-done(((bf16[16,4,128,2,128]{4,2,3,1,0:T(8,128)(2,1)}), bf16[16,4,128,2,128]{4,2,3,1,0:T(8,128)(2,1)}, u32[]{:S(2)}, u32[]{:S(2)}) %all-to-all-start) | async-done | bytes 4194336 | tf_op jit(solution)/shard_map/all_to_all | solution.py:106
  223.5 4.8 %all-to-all-start.3 = ((bf16[16,3,2,128,128]{4,3,1,2,0:T(8,128)(2,1)}), bf16[16,3,2,128,128]{4,3,1,2,0:T(8,128)(2,1)}, u32[]{:S(2)}, u32[]{:S(2)}) async-start(bf16[16,3,2,128,128]{4,3,1,2,0:T(8,128)(2,1)} %maximum_bitcast_fusion.3), calls=%async_computation.3 | async-start | bytes 6291456 | tf_op jit(solution)/shard_map/all_to_all | solution.py:116
  228.2 3.5 fusion.6
  232.8 1.0 copy-done.2
  233.8 1.0 copy-done.3
  234.9 1.0 copy-done.5
  235.9 24.6 %shard_map.68 = (bf16[128,2048]{1,0:T(8,128)(2,1)S(1)}, bf16[2048,128]{1,0:T(8,128)(2,1)S(1)}, bf16[2048,128]{1,0:T(8,128)(2,1)S(1)}) custom-call(bf16[2048,128]{1,0:T(8,128)(2,1)S(1)} %bitcast.99, bf16[2048,128]{1,0:T(8,128)(2,1)S(1)} %bitcast.87, bf16[128,2048]{1,0:T(8,128)(2,1)S(1)} %bitcast.103, bf16[2048,128]{1,0:T(8,128)(2,1)S(1)} %bitcast.98, ...), custom_call_target="tpu_custom_call" | custom-call | tf_op jit(solution)/shard_map/pallas_call | solution.py:80
  262.9 2.1 copy.87
  265.2 24.6 %shard_map.67 = (bf16[128,2048]{1,0:T(8,128)(2,1)S(1)}, bf16[2048,128]{1,0:T(8,128)(2,1)S(1)}, bf16[2048,128]{1,0:T(8,128)(2,1)S(1)}) custom-call(bf16[2048,128]{1,0:T(8,128)(2,1)S(1)} %bitcast.93, bf16[2048,128]{1,0:T(8,128)(2,1)S(1)} %bitcast.83, bf16[128,2048]{1,0:T(8,128)(2,1)S(1)} %bitcast.101, bf16[2048,128]{1,0:T(8,128)(2,1)S(1)} %bitcast.92, ...), custom_call_target="tpu_custom_call" | custom-call | tf_op jit(solution)/shard_map/pallas_call | solution.py:80
  292.3 1.3 copy.85
  293.6 3.1 maximum_bitcast_fusion.2
  296.7 1.6 all-to-all-done.3
  298.2 4.8 %all-to-all-start.1 = ((bf16[16,3,2,128,128]{4,3,1,2,0:T(8,128)(2,1)}), bf16[16,3,2,128,128]{4,3,1,2,0:T(8,128)(2,1)S(1)}, u32[]{:S(2)}, u32[]{:S(2)}) async-start(bf16[16,3,2,128,128]{4,3,1,2,0:T(8,128)(2,1)} %maximum_bitcast_fusion.2), calls=%async_computation.1 | async-start | bytes 6291456 | tf_op jit(solution)/shard_map/all_to_all | solution.py:116
  303.0 4.7 %copy.80 = bf16[16,3,2,128,128]{3,4,2,0,1:T(8,128)(2,1)} copy(bf16[16,3,2,128,128]{4,3,1,2,0:T(8,128)(2,1)} %all-to-all-done.3) | data formatting | bytes 6291456 | tf_op jit(solution)/shard_map/all_to_all | solution.py:116
  307.7 65.2 %all-to-all-done.1 = bf16[16,3,2,128,128]{4,3,1,2,0:T(8,128)(2,1)S(1)} async-done(((bf16[16,3,2,128,128]{4,3,1,2,0:T(8,128)(2,1)}), bf16[16,3,2,128,128]{4,3,1,2,0:T(8,128)(2,1)S(1)}, u32[]{:S(2)}, u32[]{:S(2)}) %all-to-all-start.1) | async-done | bytes 3145760 | tf_op jit(solution)/shard_map/all_to_all | solution.py:116
  372.9 2.8 copy.64
  375.7 4.4 %fusion.4 = (bf16[2,128,4096]{1,2,0:T(8,128)(2,1)}, bf16[2,128,4096]{1,2,0:T(8,128)(2,1)}, bf16[2,128,4096]{1,2,0:T(8,128)(2,1)S(1)}) fusion(bf16[3,1,128,4096]{2,3,0,1:T(8,128)(2,1)} %bitcast.116, bf16[3,1,128,4096]{2,3,0,1:T(8,128)(2,1)} %bitcast.117), kind=kLoop, calls=%fused_computation.13 | loop fusion | flops 3145728 | bytes 12582912 | tf_op jit(solution)/shard_map/squeeze | solution.py:119
  380.1 4.1 %copy.83 = bf16[2,128,4096]{2,1,0:T(8,128)(2,1)} copy(bf16[2,128,4096]{1,2,0:T(8,128)(2,1)} %get-tuple-element.30) | data formatting | bytes 4194304
  384.2 4.1 %copy.81 = bf16[2,128,4096]{2,1,0:T(8,128)(2,1)} copy(bf16[2,128,4096]{1,2,0:T(8,128)(2,1)} %get-tuple-element.31) | data formatting | bytes 4194304
  388.3 2.7 copy.82
  (42 shorter events, 11.7 us)
Async XLA Ops:
  27.2 99.0 %all-to-all-start.2 = ((bf16[16,4,128,2,128]{4,2,3,1,0:T(8,128)(2,1)}), bf16[16,4,128,2,128]{4,2,3,1,0:T(8,128)(2,1)}, u32[]{:S(2)}, u32[]{:S(2)}) async-start(bf16[16,4,128,2,128]{4,2,3,1,0:T(8,128)(2,1)} %copy.69), calls=%async_computation.2 | async-start | bytes 8388608 | tf_op jit(solution)/shard_map/all_to_all | solution.py:106
  35.1 2.6 copy-start.20
  36.4 2.0 copy-start.21
  126.2 97.2 %all-to-all-start = ((bf16[16,4,128,2,128]{4,2,3,1,0:T(8,128)(2,1)}), bf16[16,4,128,2,128]{4,2,3,1,0:T(8,128)(2,1)}, u32[]{:S(2)}, u32[]{:S(2)}) async-start(bf16[16,4,128,2,128]{4,2,3,1,0:T(8,128)(2,1)} %copy.53), calls=%async_computation | async-start | bytes 8388608 | tf_op jit(solution)/shard_map/all_to_all | solution.py:106
  135.5 1.0 copy-start
  136.6 1.0 copy-start.1
  137.6 1.0 copy-start.4
  163.3 0.8 copy-start.6
  164.1 0.8 copy-start.8
  164.9 0.8 copy-start.16
  165.7 30.7 %copy-start.7 = (bf16[2048,128]{1,0:T(8,128)(2,1)S(1)}, bf16[2048,128]{1,0:T(8,128)(2,1)}, u32[]{:S(2)}) copy-start(bf16[2048,128]{1,0:T(8,128)(2,1)} %copy-done.6) | copy-start | bytes 1572868
  192.6 0.8 copy-start.12
  193.4 0.8 copy-start.13
  194.2 0.8 copy-start.17
  223.5 74.8 %all-to-all-start.3 = ((bf16[16,3,2,128,128]{4,3,1,2,0:T(8,128)(2,1)}), bf16[16,3,2,128,128]{4,3,1,2,0:T(8,128)(2,1)}, u32[]{:S(2)}, u32[]{:S(2)}) async-start(bf16[16,3,2,128,128]{4,3,1,2,0:T(8,128)(2,1)} %maximum_bitcast_fusion.3), calls=%async_computation.3 | async-start | bytes 6291456 | tf_op jit(solution)/shard_map/all_to_all | solution.py:116
  232.8 1.0 copy-start.2
  233.8 1.0 copy-start.3
  234.9 1.0 copy-start.5
  260.5 0.8 copy-start.9
  261.3 0.8 copy-start.11
  262.1 0.8 copy-start.18
  262.9 30.7 %copy-start.10 = (bf16[2048,128]{1,0:T(8,128)(2,1)S(1)}, bf16[2048,128]{1,0:T(8,128)(2,1)}, u32[]{:S(2)}) copy-start(bf16[2048,128]{1,0:T(8,128)(2,1)} %copy-done.9) | copy-start | bytes 1572868
  289.9 0.8 copy-start.14
  290.6 0.8 copy-start.15
  291.4 0.9 copy-start.19
  298.2 74.7 %all-to-all-start.1 = ((bf16[16,3,2,128,128]{4,3,1,2,0:T(8,128)(2,1)}), bf16[16,3,2,128,128]{4,3,1,2,0:T(8,128)(2,1)S(1)}, u32[]{:S(2)}, u32[]{:S(2)}) async-start(bf16[16,3,2,128,128]{4,3,1,2,0:T(8,128)(2,1)} %maximum_bitcast_fusion.2), calls=%async_computation.1 | async-start | bytes 6291456 | tf_op jit(solution)/shard_map/all_to_all | solution.py:116

commit v7 on v6

--- a/solution.py
+++ b/solution.py
@@ -1,3 +1,5 @@
+import functools
+
 import jax
 import jax.numpy as jnp
 from jax import lax
@@ -91,6 +93,61 @@
     return dqt.T, dk, dv
 
 
+def _gather_kernel(*refs, groups, per_dev, head_width):
+    in_refs, out_ref = refs[:4], refs[4]
+    for s in range(groups):
+        for a, x_ref in enumerate(in_refs):
+            for h in range(per_dev):
+                col = (s * per_dev + h) * head_width
+                out_ref[s, a, h] = x_ref[0, :, col:col + head_width]
+
+
+def to_owners(inputs, page, seq_size, per_dev, head_width):
+    page_count, tok_rows, feature_width = inputs[0].shape
+    groups = max(1, 8 // per_dev)
+    while seq_size % groups:
+        groups //= 2
+    width = groups * per_dev * head_width
+    in_spec = pl.BlockSpec((1, tok_rows, width), lambda g: (page, 0, g))
+    out_spec = pl.BlockSpec((groups, 4, per_dev, tok_rows, head_width), lambda g: (g, 0, 0, 0, 0))
+    return pl.pallas_call(
+        functools.partial(_gather_kernel, groups=groups, per_dev=per_dev, head_width=head_width),
+        grid=(seq_size // groups,),
+        in_specs=[in_spec] * 4,
+        out_specs=out_spec,
+        out_shape=jax.ShapeDtypeStruct((seq_size, 4, per_dev, tok_rows, head_width), inputs[0].dtype),
+    )(*inputs)
+
+
+def _scatter_kernel(ret_ref, a_in, b_in, c_in, a_out, b_out, c_out, *, groups, per_dev, head_width):
+    del a_in, b_in, c_in
+    for s in range(groups):
+        for a, o_ref in enumerate((a_out, b_out, c_out)):
+            for h in range(per_dev):
+                col = (s * per_dev + h) * head_width
+                o_ref[0, :, col:col + head_width] = ret_ref[s, a, h]
+
+
+def from_owners(returned, results, page, per_dev, head_width):
+    seq_size = returned.shape[0]
+    page_count, tok_rows, feature_width = results[0].shape
+    groups = max(1, 8 // per_dev)
+    while seq_size % groups:
+        groups //= 2
+    width = groups * per_dev * head_width
+    in_spec = pl.BlockSpec((groups, 3, per_dev, tok_rows, head_width), lambda g: (g, 0, 0, 0, 0))
+    res_spec = pl.BlockSpec((1, tok_rows, width), lambda g: (page, 0, g))
+    shape = jax.ShapeDtypeStruct(results[0].shape, results[0].dtype)
+    return pl.pallas_call(
+        functools.partial(_scatter_kernel, groups=groups, per_dev=per_dev, head_width=head_width),
+        grid=(seq_size // groups,),
+        in_specs=[in_spec, pl.BlockSpec(memory_space=pl.ANY)] + [pl.BlockSpec(memory_space=pl.ANY)] * 2,
+        out_specs=[res_spec] * 3,
+        out_shape=[shape] * 3,
+        input_output_aliases={1: 0, 2: 1, 3: 2},
+    )(returned, *results)
+
+
 def body(queries, key_vectors, value_vectors, out_grad):
     page_count, tok_rows, feature_width = queries.shape
     seq_size = lax.psum(1, "seq")
@@ -98,25 +155,19 @@
     per_dev = HEADS // seq_size
     tokens_all = seq_size * tok_rows
     inputs = (queries, key_vectors, value_vectors, out_grad)
-    outs = []
+    results = tuple(jnp.zeros_like(queries) for _ in range(3))
     for page in range(page_count):
-        part = jnp.stack(
-            [x[page].reshape(tok_rows, seq_size, per_dev, head_width) for x in inputs]
-        ).transpose(2, 0, 1, 3, 4)
+        part = to_owners(inputs, page, seq_size, per_dev, head_width)
         arrived = lax.all_to_all(part, "seq", split_axis=0, concat_axis=0, tiled=True)
-        arrived = arrived.reshape(seq_size, 4, tok_rows, per_dev, head_width)
         grads = []
         for head in range(per_dev):
-            items = [
-                arrived[:, a, :, head, :].reshape(tokens_all, head_width) for a in range(4)
-            ]
+            items = [arrived[:, a, head].reshape(tokens_all, head_width) for a in range(4)]
             grads.append(jnp.stack(item_gradients(*items)))
         grads = jnp.stack(grads).reshape(per_dev, 3, seq_size, tok_rows, head_width)
         grads = grads.transpose(2, 1, 0, 3, 4)
         returned = lax.all_to_all(grads, "seq", split_axis=0, concat_axis=0, tiled=True)
-        outs.append(returned.transpose(1, 3, 0, 2, 4).reshape(3, tok_rows, feature_width))
-    result = jnp.stack(outs, axis=1)
-    return result[0], result[1], result[2]
+        results = tuple(from_owners(returned, results, page, per_dev, head_width))
+    return results
 
 
 def solution(mesh):

time: 393 us -> 359 us (0.913)
  local copies, waits for them, and re-layouts: 84.4 us -> 38.5 us
  Pallas kernels: 98.4 us -> 117 us
  other arithmetic: 17.7 us -> 6.02 us
  waiting for transfers between devices: 169 us -> 174 us
    unnamed x55 -> x42, local copies, waits for them, and re-layouts: 38.5 us -> 17.5 us
    pallas_call x0 -> x4, Pallas kernels: none -> 18.8 us  [the longest x2 9.87 us: to_owners(): pl.pallas_call(functools.partial(_gather_kernel, groups=groups, per_dev=p...]
    all_to_all x2, waiting for transfers between devices: 102 us -> 112 us  [body(): lax.all_to_all(part, 'seq', split_axis=0, concat_axis=0, tiled=True)]
    slice x6 -> x2, local copies, waits for them, and re-layouts: 16.2 us -> 7.09 us  [body(): arrived[:, a, head].reshape(tokens_all, head_width)]
    all_to_all x2 -> x0, local copies, waits for them, and re-layouts: 7.53 us -> none  [body(): lax.all_to_all(grads, 'seq', split_axis=0, concat_axis=0, tiled=True)]
    transpose x2 -> x0, other arithmetic: 7.22 us -> none  [body(): part = jnp.stack([x[page].reshape(tok_rows, seq_size, per_dev, head_width...]
    transpose x2 -> x4, local copies, waits for them, and re-layouts: 12.9 us -> 6.8 us  [item_gradients(): return (dqt.T, dk, dv)]
    squeeze x1 -> x0, other arithmetic: 4.39 us -> none  [body(): return (result[0], result[1], result[2])]
  transfers between devices with their start and end apart: 4 -> 4, of which waited for: 4 -> 4; matrix products, arithmetic and copies ran while one was open for 11% -> 8% of each run, Pallas kernels for 25% -> 30%
where the time goes in v7:
time: 359 us; the launch traced here: 357 us
  waiting for transfers between devices  174 us (48%)
  Pallas kernels  117 us (33%)
  local copies, waits for them, and re-layouts  38.5 us (11%)
  starting transfers between devices  20.9 us (6%)
  other arithmetic  6.02 us (2%)
    all_to_all x2, waiting for transfers between devices, body(): lax.all_to_all(part, 'seq', split_axis=0, concat_axis=0, tiled=True)  112 us
    pallas_call x4, Pallas kernels, item_gradients(): pl.pallas_call(_kernel, out_shape=(out_t, out, out), scratch_shapes=[pltp...  98.4 us
    all_to_all x2, waiting for transfers between devices, body(): lax.all_to_all(grads, 'seq', split_axis=0, concat_axis=0, tiled=True)  62.4 us
    unnamed x42, local copies, waits for them, and re-layouts  17.5 us
    all_to_all x2, starting transfers between devices, body(): lax.all_to_all(part, 'seq', split_axis=0, concat_axis=0, tiled=True)  11.3 us
    pallas_call x2, Pallas kernels, to_owners(): pl.pallas_call(functools.partial(_gather_kernel, groups=groups, per_dev=p...  9.87 us
    all_to_all x2, starting transfers between devices, body(): lax.all_to_all(grads, 'seq', split_axis=0, concat_axis=0, tiled=True)  9.56 us
    pallas_call x2, Pallas kernels, from_owners(): pl.pallas_call(functools.partial(_scatter_kernel, groups=groups, per_dev=...  8.97 us
  transfers between devices with their start and end apart: 4, of which 4 were waited for; matrix products, arithmetic and copies ran while one was open for 8% of the time, Pallas kernels for 30%

profile of v7, /device:TPU:13, one launch (start us, length us, event | category | flops | bytes accessed | tf_op | source)
XLA Modules:
  0.0 357.3 jit_solution(18264357993636651538)
XLA Ops:
  0.6 4.9 %shard_map.70 = bf16[16,4,2,128,128]{4,3,2,1,0:T(8,128)(2,1)} custom-call(bf16[2,128,4096]{2,1,0:T(8,128)(2,1)} %refs_0_.3, bf16[2,128,4096]{2,1,0:T(8,128)(2,1)} %refs_1_.3, bf16[2,128,4096]{2,1,0:T(8,128)(2,1)} %refs_2_.3, bf16[2,128,4096]{2,1,0:T(8,128)(2,1)} %refs_3_.3), custom_call_target="tpu_custom_call" | custom-call | tf_op jit(solution)/shard_map/pallas_call | solution.py:113
  5.5 6.5 %all-to-all-start.2 = ((bf16[16,4,2,128,128]{4,3,2,1,0:T(8,128)(2,1)}), bf16[16,4,2,128,128]{4,3,2,1,0:T(8,128)(2,1)}, u32[]{:S(2)}, u32[]{:S(2)}) async-start(bf16[16,4,2,128,128]{4,3,2,1,0:T(8,128)(2,1)} %shard_map.70), calls=%async_computation.2 | async-start | bytes 8388608 | tf_op jit(solution)/shard_map/all_to_all | solution.py:161
  12.0 5.0 %shard_map.67 = bf16[16,4,2,128,128]{4,3,2,1,0:T(8,128)(2,1)} custom-call(bf16[2,128,4096]{2,1,0:T(8,128)(2,1)} %refs_0_.3, bf16[2,128,4096]{2,1,0:T(8,128)(2,1)} %refs_1_.3, bf16[2,128,4096]{2,1,0:T(8,128)(2,1)} %refs_2_.3, bf16[2,128,4096]{2,1,0:T(8,128)(2,1)} %refs_3_.3), custom_call_target="tpu_custom_call" | custom-call | tf_op jit(solution)/shard_map/pallas_call | solution.py:113
  17.0 87.5 %all-to-all-done.2 = bf16[16,4,2,128,128]{4,3,2,1,0:T(8,128)(2,1)} async-done(((bf16[16,4,2,128,128]{4,3,2,1,0:T(8,128)(2,1)}), bf16[16,4,2,128,128]{4,3,2,1,0:T(8,128)(2,1)}, u32[]{:S(2)}, u32[]{:S(2)}) %all-to-all-start.2) | async-done | bytes 4194336 | tf_op jit(solution)/shard_map/all_to_all | solution.py:161
  104.5 4.8 %all-to-all-start = ((bf16[16,4,2,128,128]{4,3,2,1,0:T(8,128)(2,1)}), bf16[16,4,2,128,128]{4,3,2,1,0:T(8,128)(2,1)}, u32[]{:S(2)}, u32[]{:S(2)}) async-start(bf16[16,4,2,128,128]{4,3,2,1,0:T(8,128)(2,1)} %shard_map.67), calls=%async_computation | async-start | bytes 8388608 | tf_op jit(solution)/shard_map/all_to_all | solution.py:161
  109.3 3.5 fusion
  112.8 1.0 copy.28
  113.8 1.0 copy-done
  114.9 1.0 copy-done.1
  115.9 1.0 copy-done.4
  117.0 24.6 %shard_map.72 = (bf16[128,2048]{1,0:T(8,128)(2,1)S(1)}, bf16[2048,128]{1,0:T(8,128)(2,1)S(1)}, bf16[2048,128]{1,0:T(8,128)(2,1)S(1)}) custom-call(bf16[2048,128]{1,0:T(8,128)(2,1)S(1)} %bitcast.56, bf16[2048,128]{1,0:T(8,128)(2,1)S(1)} %bitcast.45, bf16[128,2048]{1,0:T(8,128)(2,1)S(1)} %bitcast.62, bf16[2048,128]{1,0:T(8,128)(2,1)S(1)} %bitcast.55, ...), custom_call_target="tpu_custom_call" | custom-call | tf_op jit(solution)/shard_map/pallas_call | solution.py:82
  141.6 0.8 copy-done.6
  142.4 0.8 copy-done.8
  143.2 0.8 copy-done.16
  144.0 2.1 copy.24
  146.3 24.6 %shard_map.71 = (bf16[128,2048]{1,0:T(8,128)(2,1)S(1)}, bf16[2048,128]{1,0:T(8,128)(2,1)S(1)}, bf16[2048,128]{1,0:T(8,128)(2,1)S(1)}) custom-call(bf16[2048,128]{1,0:T(8,128)(2,1)S(1)} %bitcast.50, bf16[2048,128]{1,0:T(8,128)(2,1)S(1)} %bitcast.41, bf16[128,2048]{1,0:T(8,128)(2,1)S(1)} %bitcast.60, bf16[2048,128]{1,0:T(8,128)(2,1)S(1)} %bitcast.49, ...), custom_call_target="tpu_custom_call" | custom-call | tf_op jit(solution)/shard_map/pallas_call | solution.py:82
  170.9 0.8 copy-done.12
  171.7 0.8 copy-done.13
  172.5 0.8 copy-done.17
  173.3 1.3 copy.21
  174.7 3.0 maximum_bitcast_fusion.1
  177.7 24.1 %all-to-all-done = bf16[16,4,2,128,128]{4,3,2,1,0:T(8,128)(2,1)} async-done(((bf16[16,4,2,128,128]{4,3,2,1,0:T(8,128)(2,1)}), bf16[16,4,2,128,128]{4,3,2,1,0:T(8,128)(2,1)}, u32[]{:S(2)}, u32[]{:S(2)}) %all-to-all-start) | async-done | bytes 4194336 | tf_op jit(solution)/shard_map/all_to_all | solution.py:161
  201.8 4.8 %all-to-all-start.3 = ((bf16[16,3,2,128,128]{4,3,2,1,0:T(8,128)(2,1)}), bf16[16,3,2,128,128]{4,3,2,1,0:T(8,128)(2,1)}, u32[]{:S(2)}, u32[]{:S(2)}) async-start(bf16[16,3,2,128,128]{4,3,2,1,0:T(8,128)(2,1)} %maximum_bitcast_fusion.1), calls=%async_computation.3 | async-start | bytes 6291456 | tf_op jit(solution)/shard_map/all_to_all | solution.py:168
  206.5 3.5 fusion.1
  210.1 1.0 copy.26
  211.1 1.0 copy-done.2
  212.1 1.0 copy-done.3
  213.2 1.0 copy-done.5
  214.2 24.6 %shard_map.69 = (bf16[128,2048]{1,0:T(8,128)(2,1)S(1)}, bf16[2048,128]{1,0:T(8,128)(2,1)S(1)}, bf16[2048,128]{1,0:T(8,128)(2,1)S(1)}) custom-call(bf16[2048,128]{1,0:T(8,128)(2,1)S(1)} %bitcast.59, bf16[2048,128]{1,0:T(8,128)(2,1)S(1)} %bitcast.47, bf16[128,2048]{1,0:T(8,128)(2,1)S(1)} %bitcast.63, bf16[2048,128]{1,0:T(8,128)(2,1)S(1)} %bitcast.58, ...), custom_call_target="tpu_custom_call" | custom-call | tf_op jit(solution)/shard_map/pallas_call | solution.py:82
  238.8 0.8 copy-done.9
  239.6 0.8 copy-done.11
  240.4 0.8 copy-done.18
  241.2 2.1 copy.18
  243.5 24.6 %shard_map.68 = (bf16[128,2048]{1,0:T(8,128)(2,1)S(1)}, bf16[2048,128]{1,0:T(8,128)(2,1)S(1)}, bf16[2048,128]{1,0:T(8,128)(2,1)S(1)}) custom-call(bf16[2048,128]{1,0:T(8,128)(2,1)S(1)} %bitcast.53, bf16[2048,128]{1,0:T(8,128)(2,1)S(1)} %bitcast.43, bf16[128,2048]{1,0:T(8,128)(2,1)S(1)} %bitcast.61, bf16[2048,128]{1,0:T(8,128)(2,1)S(1)} %bitcast.52, ...), custom_call_target="tpu_custom_call" | custom-call | tf_op jit(solution)/shard_map/pallas_call | solution.py:82
  268.1 0.8 copy-done.14
  268.9 0.8 copy-done.15
  269.7 0.8 copy-done.19
  270.6 1.3 copy.15
  271.9 3.0 maximum_bitcast_fusion
  274.9 1.6 all-to-all-done.3.ret_ref
  276.5 4.8 %all-to-all-start.1 = ((bf16[16,3,2,128,128]{4,3,2,1,0:T(8,128)(2,1)}), bf16[16,3,2,128,128]{4,3,2,1,0:T(8,128)(2,1)S(1)}, u32[]{:S(2)}, u32[]{:S(2)}) async-start(bf16[16,3,2,128,128]{4,3,2,1,0:T(8,128)(2,1)} %maximum_bitcast_fusion), calls=%async_computation.1 | async-start | bytes 6291456 | tf_op jit(solution)/shard_map/all_to_all | solution.py:168
  281.3 1.6 broadcast_1_a_in_b_in_c_in.2.clone.1.c_in
  282.9 1.6 broadcast_1_a_in_b_in_c_in.2.clone.b_in
  284.4 1.6 broadcast_1_a_in_b_in_c_in.2.a_in
  286.0 4.5 %shard_map.73 = (bf16[2,128,4096]{2,1,0:T(8,128)(2,1)}, bf16[2,128,4096]{2,1,0:T(8,128)(2,1)}, bf16[2,128,4096]{2,1,0:T(8,128)(2,1)}) custom-call(bf16[16,3,2,128,128]{4,3,2,1,0:T(8,128)(2,1)} %all-to-all-done.3.ret_ref, bf16[2,128,4096]{2,1,0:T(8,128)(2,1)} %broadcast_1_a_in_b_in_c_in.2.a_in, ...), custom_call_target="tpu_custom_call", output_to_operand_aliasing={{0}: (1, {}), {1}: (2, {}), {2}: (3, {})} | custom-call | tf_op jit(solution)/shard_map/pallas_call | solution.py:141
  290.5 60.7 %all-to-all-done.1.ret_ref = bf16[16,3,2,128,128]{4,3,2,1,0:T(8,128)(2,1)S(1)} async-done(((bf16[16,3,2,128,128]{4,3,2,1,0:T(8,128)(2,1)}), bf16[16,3,2,128,128]{4,3,2,1,0:T(8,128)(2,1)S(1)}, u32[]{:S(2)}, u32[]{:S(2)}) %all-to-all-start.1) | async-done | bytes 3145760 | tf_op jit(solution)/shard_map/all_to_all | solution.py:168
  351.2 1.6 copy-done.20
  352.8 4.5 %shard_map.74 = (bf16[2,128,4096]{2,1,0:T(8,128)(2,1)}, bf16[2,128,4096]{2,1,0:T(8,128)(2,1)}, bf16[2,128,4096]{2,1,0:T(8,128)(2,1)}) custom-call(bf16[16,3,2,128,128]{4,3,2,1,0:T(8,128)(2,1)} %copy-done.20, bf16[2,128,4096]{2,1,0:T(8,128)(2,1)} %get-tuple-element.30.a_in, ...), custom_call_target="tpu_custom_call", output_to_operand_aliasing={{0}: (1, {}), {1}: (2, {}), {2}: (3, {})} | custom-call | tf_op jit(solution)/shard_map/pallas_call | solution.py:141
  (25 shorter events, 0.5 us)
Async XLA Ops:
  5.5 99.0 %all-to-all-start.2 = ((bf16[16,4,2,128,128]{4,3,2,1,0:T(8,128)(2,1)}), bf16[16,4,2,128,128]{4,3,2,1,0:T(8,128)(2,1)}, u32[]{:S(2)}, u32[]{:S(2)}) async-start(bf16[16,4,2,128,128]{4,3,2,1,0:T(8,128)(2,1)} %shard_map.70), calls=%async_computation.2 | async-start | bytes 8388608 | tf_op jit(solution)/shard_map/all_to_all | solution.py:161
  104.5 97.2 %all-to-all-start = ((bf16[16,4,2,128,128]{4,3,2,1,0:T(8,128)(2,1)}), bf16[16,4,2,128,128]{4,3,2,1,0:T(8,128)(2,1)}, u32[]{:S(2)}, u32[]{:S(2)}) async-start(bf16[16,4,2,128,128]{4,3,2,1,0:T(8,128)(2,1)} %shard_map.67), calls=%async_computation | async-start | bytes 8388608 | tf_op jit(solution)/shard_map/all_to_all | solution.py:161
  113.8 1.0 copy-start
  114.9 1.0 copy-start.1
  115.9 1.0 copy-start.4
  141.6 0.8 copy-start.6
  142.4 0.8 copy-start.8
  143.2 0.8 copy-start.16
  144.0 30.7 %copy-start.7 = (bf16[2048,128]{1,0:T(8,128)(2,1)S(1)}, bf16[2048,128]{1,0:T(8,128)(2,1)}, u32[]{:S(2)}) copy-start(bf16[2048,128]{1,0:T(8,128)(2,1)} %copy-done.6) | copy-start | bytes 1572868
  170.9 0.8 copy-start.12
  171.7 0.8 copy-start.13
  172.5 0.8 copy-start.17
  201.8 74.8 %all-to-all-start.3 = ((bf16[16,3,2,128,128]{4,3,2,1,0:T(8,128)(2,1)}), bf16[16,3,2,128,128]{4,3,2,1,0:T(8,128)(2,1)}, u32[]{:S(2)}, u32[]{:S(2)}) async-start(bf16[16,3,2,128,128]{4,3,2,1,0:T(8,128)(2,1)} %maximum_bitcast_fusion.1), calls=%async_computation.3 | async-start | bytes 6291456 | tf_op jit(solution)/shard_map/all_to_all | solution.py:168
  211.1 1.0 copy-start.2
  212.1 1.0 copy-start.3
  213.2 1.0 copy-start.5
  238.8 0.8 copy-start.9
  239.6 0.8 copy-start.11
  240.4 0.8 copy-start.18
  241.2 30.7 %copy-start.10 = (bf16[2048,128]{1,0:T(8,128)(2,1)S(1)}, bf16[2048,128]{1,0:T(8,128)(2,1)}, u32[]{:S(2)}) copy-start(bf16[2048,128]{1,0:T(8,128)(2,1)} %copy-done.9) | copy-start | bytes 1572868
  268.1 0.8 copy-start.14
  268.9 0.8 copy-start.15
  269.7 0.8 copy-start.19
  276.5 74.7 %all-to-all-start.1 = ((bf16[16,3,2,128,128]{4,3,2,1,0:T(8,128)(2,1)}), bf16[16,3,2,128,128]{4,3,2,1,0:T(8,128)(2,1)S(1)}, u32[]{:S(2)}, u32[]{:S(2)}) async-start(bf16[16,3,2,128,128]{4,3,2,1,0:T(8,128)(2,1)} %maximum_bitcast_fusion), calls=%async_computation.1 | async-start | bytes 6291456 | tf_op jit(solution)/shard_map/all_to_all | solution.py:168
  351.2 1.6 copy-start.20

commit v8 on v7

--- a/solution.py
+++ b/solution.py
@@ -8,7 +8,7 @@
 from jax.sharding import PartitionSpec as P
 
 HEADS = 32
-BLOCK = 256
+BLOCK = 512
 
 
 def _kernel(q_ref, k_ref, kt_ref, v_ref, do_ref, dqt_ref, dk_ref, dv_ref, s_scr, dp_scr, dk_acc, dv_acc):

time: 359 us -> 359 us (level)
  waiting for transfers between devices: 174 us -> 220 us
  Pallas kernels: 117 us -> 71.3 us
    pallas_call x4, Pallas kernels: 98.4 us -> 52.4 us  [item_gradients(): pl.pallas_call(_kernel, out_shape=(out_t, out, out), scratch_shapes=[pltp...]
    all_to_all x2, waiting for transfers between devices: 112 us -> 135 us  [body(): lax.all_to_all(part, 'seq', split_axis=0, concat_axis=0, tiled=True)]
    all_to_all x2, waiting for transfers between devices: 62.4 us -> 85.4 us  [body(): lax.all_to_all(grads, 'seq', split_axis=0, concat_axis=0, tiled=True)]
  transfers between devices with their start and end apart: 4 -> 4, of which waited for: 4 -> 4; matrix products, arithmetic and copies ran while one was open for 8% -> 8% of each run, Pallas kernels for 30% -> 17%
where the time goes in v8:
time: 359 us; the launch traced here: 357 us
  waiting for transfers between devices  220 us (61%)
  Pallas kernels  71.3 us (20%)
  local copies, waits for them, and re-layouts  38.5 us (11%)
  starting transfers between devices  20.9 us (6%)
  other arithmetic  6.02 us (2%)
    all_to_all x2, waiting for transfers between devices, body(): lax.all_to_all(part, 'seq', split_axis=0, concat_axis=0, tiled=True)  135 us
    all_to_all x2, waiting for transfers between devices, body(): lax.all_to_all(grads, 'seq', split_axis=0, concat_axis=0, tiled=True)  85.4 us
    pallas_call x4, Pallas kernels, item_gradients(): pl.pallas_call(_kernel, out_shape=(out_t, out, out), scratch_shapes=[pltp...  52.4 us
    unnamed x42, local copies, waits for them, and re-layouts  17.5 us
    all_to_all x2, starting transfers between devices, body(): lax.all_to_all(part, 'seq', split_axis=0, concat_axis=0, tiled=True)  11.3 us
    pallas_call x2, Pallas kernels, to_owners(): pl.pallas_call(functools.partial(_gather_kernel, groups=groups, per_dev=p...  9.87 us
    all_to_all x2, starting transfers between devices, body(): lax.all_to_all(grads, 'seq', split_axis=0, concat_axis=0, tiled=True)  9.56 us
    pallas_call x2, Pallas kernels, from_owners(): pl.pallas_call(functools.partial(_scatter_kernel, groups=groups, per_dev=...  8.97 us
  transfers between devices with their start and end apart: 4, of which 4 were waited for; matrix products, arithmetic and copies ran while one was open for 8% of the time, Pallas kernels for 17%

profile of v8, /device:TPU:13, one launch (start us, length us, event | category | flops | bytes accessed | tf_op | source)
XLA Modules:
  0.0 357.3 jit_solution(15115994087400790326)
XLA Ops:
  0.6 4.9 %shard_map.70 = bf16[16,4,2,128,128]{4,3,2,1,0:T(8,128)(2,1)} custom-call(bf16[2,128,4096]{2,1,0:T(8,128)(2,1)} %refs_0_.3, bf16[2,128,4096]{2,1,0:T(8,128)(2,1)} %refs_1_.3, bf16[2,128,4096]{2,1,0:T(8,128)(2,1)} %refs_2_.3, bf16[2,128,4096]{2,1,0:T(8,128)(2,1)} %refs_3_.3), custom_call_target="tpu_custom_call" | custom-call | tf_op jit(solution)/shard_map/pallas_call | solution.py:113
  5.5 6.5 %all-to-all-start.2 = ((bf16[16,4,2,128,128]{4,3,2,1,0:T(8,128)(2,1)}), bf16[16,4,2,128,128]{4,3,2,1,0:T(8,128)(2,1)}, u32[]{:S(2)}, u32[]{:S(2)}) async-start(bf16[16,4,2,128,128]{4,3,2,1,0:T(8,128)(2,1)} %shard_map.70), calls=%async_computation.2 | async-start | bytes 8388608 | tf_op jit(solution)/shard_map/all_to_all | solution.py:161
  12.0 5.0 %shard_map.67 = bf16[16,4,2,128,128]{4,3,2,1,0:T(8,128)(2,1)} custom-call(bf16[2,128,4096]{2,1,0:T(8,128)(2,1)} %refs_0_.3, bf16[2,128,4096]{2,1,0:T(8,128)(2,1)} %refs_1_.3, bf16[2,128,4096]{2,1,0:T(8,128)(2,1)} %refs_2_.3, bf16[2,128,4096]{2,1,0:T(8,128)(2,1)} %refs_3_.3), custom_call_target="tpu_custom_call" | custom-call | tf_op jit(solution)/shard_map/pallas_call | solution.py:113
  17.0 87.5 %all-to-all-done.2 = bf16[16,4,2,128,128]{4,3,2,1,0:T(8,128)(2,1)} async-done(((bf16[16,4,2,128,128]{4,3,2,1,0:T(8,128)(2,1)}), bf16[16,4,2,128,128]{4,3,2,1,0:T(8,128)(2,1)}, u32[]{:S(2)}, u32[]{:S(2)}) %all-to-all-start.2) | async-done | bytes 4194336 | tf_op jit(solution)/shard_map/all_to_all | solution.py:161
  104.5 4.8 %all-to-all-start = ((bf16[16,4,2,128,128]{4,3,2,1,0:T(8,128)(2,1)}), bf16[16,4,2,128,128]{4,3,2,1,0:T(8,128)(2,1)}, u32[]{:S(2)}, u32[]{:S(2)}) async-start(bf16[16,4,2,128,128]{4,3,2,1,0:T(8,128)(2,1)} %shard_map.67), calls=%async_computation | async-start | bytes 8388608 | tf_op jit(solution)/shard_map/all_to_all | solution.py:161
  109.3 3.5 fusion
  112.8 1.0 copy.28
  113.8 1.0 copy-done
  114.9 1.0 copy-done.1
  115.9 1.0 copy-done.4
  117.0 13.1 %shard_map.72 = (bf16[128,2048]{1,0:T(8,128)(2,1)S(1)}, bf16[2048,128]{1,0:T(8,128)(2,1)S(1)}, bf16[2048,128]{1,0:T(8,128)(2,1)S(1)}) custom-call(bf16[2048,128]{1,0:T(8,128)(2,1)S(1)} %bitcast.56, bf16[2048,128]{1,0:T(8,128)(2,1)S(1)} %bitcast.45, bf16[128,2048]{1,0:T(8,128)(2,1)S(1)} %bitcast.62, bf16[2048,128]{1,0:T(8,128)(2,1)S(1)} %bitcast.55, ...), custom_call_target="tpu_custom_call" | custom-call | tf_op jit(solution)/shard_map/pallas_call | solution.py:82
  130.1 0.8 copy-done.6
  130.9 0.8 copy-done.8
  131.7 0.8 copy-done.16
  132.5 2.1 copy.24
  134.8 13.1 %shard_map.71 = (bf16[128,2048]{1,0:T(8,128)(2,1)S(1)}, bf16[2048,128]{1,0:T(8,128)(2,1)S(1)}, bf16[2048,128]{1,0:T(8,128)(2,1)S(1)}) custom-call(bf16[2048,128]{1,0:T(8,128)(2,1)S(1)} %bitcast.50, bf16[2048,128]{1,0:T(8,128)(2,1)S(1)} %bitcast.41, bf16[128,2048]{1,0:T(8,128)(2,1)S(1)} %bitcast.60, bf16[2048,128]{1,0:T(8,128)(2,1)S(1)} %bitcast.49, ...), custom_call_target="tpu_custom_call" | custom-call | tf_op jit(solution)/shard_map/pallas_call | solution.py:82
  147.9 0.8 copy-done.12
  148.7 0.8 copy-done.13
  149.5 0.8 copy-done.17
  150.4 1.3 copy.21
  151.7 3.0 maximum_bitcast_fusion.1
  154.7 47.1 %all-to-all-done = bf16[16,4,2,128,128]{4,3,2,1,0:T(8,128)(2,1)} async-done(((bf16[16,4,2,128,128]{4,3,2,1,0:T(8,128)(2,1)}), bf16[16,4,2,128,128]{4,3,2,1,0:T(8,128)(2,1)}, u32[]{:S(2)}, u32[]{:S(2)}) %all-to-all-start) | async-done | bytes 4194336 | tf_op jit(solution)/shard_map/all_to_all | solution.py:161
  201.8 4.8 %all-to-all-start.3 = ((bf16[16,3,2,128,128]{4,3,2,1,0:T(8,128)(2,1)}), bf16[16,3,2,128,128]{4,3,2,1,0:T(8,128)(2,1)}, u32[]{:S(2)}, u32[]{:S(2)}) async-start(bf16[16,3,2,128,128]{4,3,2,1,0:T(8,128)(2,1)} %maximum_bitcast_fusion.1), calls=%async_computation.3 | async-start | bytes 6291456 | tf_op jit(solution)/shard_map/all_to_all | solution.py:168
  206.5 3.5 fusion.1
  210.1 1.0 copy.26
  211.1 1.0 copy-done.2
  212.1 1.0 copy-done.3
  213.2 1.0 copy-done.5
  214.2 13.1 %shard_map.69 = (bf16[128,2048]{1,0:T(8,128)(2,1)S(1)}, bf16[2048,128]{1,0:T(8,128)(2,1)S(1)}, bf16[2048,128]{1,0:T(8,128)(2,1)S(1)}) custom-call(bf16[2048,128]{1,0:T(8,128)(2,1)S(1)} %bitcast.59, bf16[2048,128]{1,0:T(8,128)(2,1)S(1)} %bitcast.47, bf16[128,2048]{1,0:T(8,128)(2,1)S(1)} %bitcast.63, bf16[2048,128]{1,0:T(8,128)(2,1)S(1)} %bitcast.58, ...), custom_call_target="tpu_custom_call" | custom-call | tf_op jit(solution)/shard_map/pallas_call | solution.py:82
  227.3 0.8 copy-done.9
  228.1 0.8 copy-done.11
  228.9 0.8 copy-done.18
  229.7 2.1 copy.18
  232.0 13.1 %shard_map.68 = (bf16[128,2048]{1,0:T(8,128)(2,1)S(1)}, bf16[2048,128]{1,0:T(8,128)(2,1)S(1)}, bf16[2048,128]{1,0:T(8,128)(2,1)S(1)}) custom-call(bf16[2048,128]{1,0:T(8,128)(2,1)S(1)} %bitcast.53, bf16[2048,128]{1,0:T(8,128)(2,1)S(1)} %bitcast.43, bf16[128,2048]{1,0:T(8,128)(2,1)S(1)} %bitcast.61, bf16[2048,128]{1,0:T(8,128)(2,1)S(1)} %bitcast.52, ...), custom_call_target="tpu_custom_call" | custom-call | tf_op jit(solution)/shard_map/pallas_call | solution.py:82
  245.2 0.8 copy-done.14
  246.0 0.8 copy-done.15
  246.8 0.8 copy-done.19
  247.6 1.3 copy.15
  248.9 3.0 maximum_bitcast_fusion
  251.9 24.6 %all-to-all-done.3.ret_ref = bf16[16,3,2,128,128]{4,3,2,1,0:T(8,128)(2,1)} async-done(((bf16[16,3,2,128,128]{4,3,2,1,0:T(8,128)(2,1)}), bf16[16,3,2,128,128]{4,3,2,1,0:T(8,128)(2,1)}, u32[]{:S(2)}, u32[]{:S(2)}) %all-to-all-start.3) | async-done | bytes 3145760 | tf_op jit(solution)/shard_map/all_to_all | solution.py:168
  276.5 4.8 %all-to-all-start.1 = ((bf16[16,3,2,128,128]{4,3,2,1,0:T(8,128)(2,1)}), bf16[16,3,2,128,128]{4,3,2,1,0:T(8,128)(2,1)S(1)}, u32[]{:S(2)}, u32[]{:S(2)}) async-start(bf16[16,3,2,128,128]{4,3,2,1,0:T(8,128)(2,1)} %maximum_bitcast_fusion), calls=%async_computation.1 | async-start | bytes 6291456 | tf_op jit(solution)/shard_map/all_to_all | solution.py:168
  281.3 1.6 broadcast_1_a_in_b_in_c_in.2.clone.1.c_in
  282.9 1.6 broadcast_1_a_in_b_in_c_in.2.clone.b_in
  284.4 1.6 broadcast_1_a_in_b_in_c_in.2.a_in
  286.0 4.5 %shard_map.73 = (bf16[2,128,4096]{2,1,0:T(8,128)(2,1)}, bf16[2,128,4096]{2,1,0:T(8,128)(2,1)}, bf16[2,128,4096]{2,1,0:T(8,128)(2,1)}) custom-call(bf16[16,3,2,128,128]{4,3,2,1,0:T(8,128)(2,1)} %all-to-all-done.3.ret_ref, bf16[2,128,4096]{2,1,0:T(8,128)(2,1)} %broadcast_1_a_in_b_in_c_in.2.a_in, ...), custom_call_target="tpu_custom_call", output_to_operand_aliasing={{0}: (1, {}), {1}: (2, {}), {2}: (3, {})} | custom-call | tf_op jit(solution)/shard_map/pallas_call | solution.py:141
  290.5 60.7 %all-to-all-done.1.ret_ref = bf16[16,3,2,128,128]{4,3,2,1,0:T(8,128)(2,1)S(1)} async-done(((bf16[16,3,2,128,128]{4,3,2,1,0:T(8,128)(2,1)}), bf16[16,3,2,128,128]{4,3,2,1,0:T(8,128)(2,1)S(1)}, u32[]{:S(2)}, u32[]{:S(2)}) %all-to-all-start.1) | async-done | bytes 3145760 | tf_op jit(solution)/shard_map/all_to_all | solution.py:168
  351.2 1.6 copy-done.20
  352.8 4.5 %shard_map.74 = (bf16[2,128,4096]{2,1,0:T(8,128)(2,1)}, bf16[2,128,4096]{2,1,0:T(8,128)(2,1)}, bf16[2,128,4096]{2,1,0:T(8,128)(2,1)}) custom-call(bf16[16,3,2,128,128]{4,3,2,1,0:T(8,128)(2,1)} %copy-done.20, bf16[2,128,4096]{2,1,0:T(8,128)(2,1)} %get-tuple-element.30.a_in, ...), custom_call_target="tpu_custom_call", output_to_operand_aliasing={{0}: (1, {}), {1}: (2, {}), {2}: (3, {})} | custom-call | tf_op jit(solution)/shard_map/pallas_call | solution.py:141
  (25 shorter events, 0.5 us)
Async XLA Ops:
  5.5 99.0 %all-to-all-start.2 = ((bf16[16,4,2,128,128]{4,3,2,1,0:T(8,128)(2,1)}), bf16[16,4,2,128,128]{4,3,2,1,0:T(8,128)(2,1)}, u32[]{:S(2)}, u32[]{:S(2)}) async-start(bf16[16,4,2,128,128]{4,3,2,1,0:T(8,128)(2,1)} %shard_map.70), calls=%async_computation.2 | async-start | bytes 8388608 | tf_op jit(solution)/shard_map/all_to_all | solution.py:161
  104.5 97.2 %all-to-all-start = ((bf16[16,4,2,128,128]{4,3,2,1,0:T(8,128)(2,1)}), bf16[16,4,2,128,128]{4,3,2,1,0:T(8,128)(2,1)}, u32[]{:S(2)}, u32[]{:S(2)}) async-start(bf16[16,4,2,128,128]{4,3,2,1,0:T(8,128)(2,1)} %shard_map.67), calls=%async_computation | async-start | bytes 8388608 | tf_op jit(solution)/shard_map/all_to_all | solution.py:161
  113.8 1.0 copy-start
  114.9 1.0 copy-start.1
  115.9 1.0 copy-start.4
  130.1 0.8 copy-start.6
  130.9 0.8 copy-start.8
  131.7 0.8 copy-start.16
  132.5 19.2 %copy-start.7 = (bf16[2048,128]{1,0:T(8,128)(2,1)S(1)}, bf16[2048,128]{1,0:T(8,128)(2,1)}, u32[]{:S(2)}) copy-start(bf16[2048,128]{1,0:T(8,128)(2,1)} %copy-done.6) | copy-start | bytes 1572868
  147.9 0.8 copy-start.12
  148.7 0.8 copy-start.13
  149.5 0.8 copy-start.17
  201.8 74.8 %all-to-all-start.3 = ((bf16[16,3,2,128,128]{4,3,2,1,0:T(8,128)(2,1)}), bf16[16,3,2,128,128]{4,3,2,1,0:T(8,128)(2,1)}, u32[]{:S(2)}, u32[]{:S(2)}) async-start(bf16[16,3,2,128,128]{4,3,2,1,0:T(8,128)(2,1)} %maximum_bitcast_fusion.1), calls=%async_computation.3 | async-start | bytes 6291456 | tf_op jit(solution)/shard_map/all_to_all | solution.py:168
  211.1 1.0 copy-start.2
  212.1 1.0 copy-start.3
  213.2 1.0 copy-start.5
  227.3 0.8 copy-start.9
  228.1 0.8 copy-start.11
  228.9 0.8 copy-start.18
  229.7 19.2 %copy-start.10 = (bf16[2048,128]{1,0:T(8,128)(2,1)S(1)}, bf16[2048,128]{1,0:T(8,128)(2,1)}, u32[]{:S(2)}) copy-start(bf16[2048,128]{1,0:T(8,128)(2,1)} %copy-done.9) | copy-start | bytes 1572868
  245.2 0.8 copy-start.14
  246.0 0.8 copy-start.15
  246.8 0.8 copy-start.19
  276.5 74.7 %all-to-all-start.1 = ((bf16[16,3,2,128,128]{4,3,2,1,0:T(8,128)(2,1)}), bf16[16,3,2,128,128]{4,3,2,1,0:T(8,128)(2,1)S(1)}, u32[]{:S(2)}, u32[]{:S(2)}) async-start(bf16[16,3,2,128,128]{4,3,2,1,0:T(8,128)(2,1)} %maximum_bitcast_fusion), calls=%async_computation.1 | async-start | bytes 6291456 | tf_op jit(solution)/shard_map/all_to_all | solution.py:168
  351.2 1.6 copy-start.20

commit v9 on v8

--- a/solution.py
+++ b/solution.py
@@ -6,6 +6,7 @@
 from jax.experimental import pallas as pl
 from jax.experimental.pallas import tpu as pltpu
 from jax.sharding import PartitionSpec as P
+
 
 HEADS = 32
 BLOCK = 512
@@ -103,7 +104,7 @@
 
 
 def to_owners(inputs, page, seq_size, per_dev, head_width):
-    page_count, tok_rows, feature_width = inputs[0].shape
+    _, tok_rows, _ = inputs[0].shape
     groups = max(1, 8 // per_dev)
     while seq_size % groups:
         groups //= 2
@@ -130,7 +131,7 @@
 
 def from_owners(returned, results, page, per_dev, head_width):
     seq_size = returned.shape[0]
-    page_count, tok_rows, feature_width = results[0].shape
+    _, tok_rows, _ = results[0].shape
     groups = max(1, 8 // per_dev)
     while seq_size % groups:
         groups //= 2
@@ -148,6 +149,17 @@
     )(returned, *results)
 
 
+def exchange(x, seq_size):
+    me = lax.axis_index("seq")
+    out = x
+    for shift in range(1, seq_size):
+        piece = lax.dynamic_index_in_dim(x, (me + shift) % seq_size, 0)
+        perm = [(i, (i + shift) % seq_size) for i in range(seq_size)]
+        got = lax.ppermute(piece, "seq", perm)
+        out = lax.dynamic_update_index_in_dim(out, got[0], (me - shift) % seq_size, 0)
+    return out
+
+
 def body(queries, key_vectors, value_vectors, out_grad):
     page_count, tok_rows, feature_width = queries.shape
     seq_size = lax.psum(1, "seq")
@@ -158,14 +170,14 @@
     results = tuple(jnp.zeros_like(queries) for _ in range(3))
     for page in range(page_count):
         part = to_owners(inputs, page, seq_size, per_dev, head_width)
-        arrived = lax.all_to_all(part, "seq", split_axis=0, concat_axis=0, tiled=True)
+        arrived = exchange(part, seq_size)
         grads = []
         for head in range(per_dev):
             items = [arrived[:, a, head].reshape(tokens_all, head_width) for a in range(4)]
             grads.append(jnp.stack(item_gradients(*items)))
         grads = jnp.stack(grads).reshape(per_dev, 3, seq_size, tok_rows, head_width)
         grads = grads.transpose(2, 1, 0, 3, 4)
-        returned = lax.all_to_all(grads, "seq", split_axis=0, concat_axis=0, tiled=True)
+        returned = exchange(grads, seq_size)
         results = tuple(from_owners(returned, results, page, per_dev, head_width))
     return results
 

time: 359 us -> 514 us (1.43)
  starting transfers between devices: 20.9 us -> 179 us
  waiting for transfers between devices: 220 us -> 168 us
  local copies, waits for them, and re-layouts: 38.5 us -> 81.1 us
    all_to_all x4 -> x0, waiting for transfers between devices: 220 us -> none  [the longest x2 135 us: body(): lax.all_to_all(part, 'seq', split_axis=0, concat_axis=0, tiled=True)]
    ppermute x0 -> x60, starting transfers between devices: none -> 179 us  [exchange(): got = lax.ppermute(piece, 'seq', perm)]
    ppermute x0 -> x60, waiting for transfers between devices: none -> 168 us  [exchange(): got = lax.ppermute(piece, 'seq', perm)]
    dynamic_update_slice x0 -> x57, local copies, waits for them, and re-layouts: none -> 28 us  [exchange(): lax.dynamic_update_index_in_dim(out, got[0], (me - shift) % seq_size, 0)]
    all_to_all x4 -> x0, starting transfers between devices: 20.9 us -> none  [the longest x2 11.3 us: body(): lax.all_to_all(part, 'seq', split_axis=0, concat_axis=0, tiled=True)]
    dynamic_slice x0 -> x6, local copies, waits for them, and re-layouts: none -> 12.5 us  [exchange(): piece = lax.dynamic_index_in_dim(x, (me + shift) % seq_size, 0)]
    unnamed x42 -> x60, local copies, waits for them, and re-layouts: 17.5 us -> 20.4 us
  transfers between devices with their start and end apart: 4 -> 60, of which waited for: 4 -> 23; matrix products, arithmetic and copies ran while one was open for 8% -> 8% of each run, Pallas kernels for 17% -> 2%
where the time goes in v9:
time: 514 us; the launch traced here: 508 us
  starting transfers between devices  179 us (35%)
  waiting for transfers between devices  168 us (33%)
  local copies, waits for them, and re-layouts  81.1 us (16%)
  Pallas kernels  71.4 us (14%)
  other arithmetic  6.56 us (1%)
    ppermute x60, starting transfers between devices, exchange(): got = lax.ppermute(piece, 'seq', perm)  179 us
    ppermute x60, waiting for transfers between devices, exchange(): got = lax.ppermute(piece, 'seq', perm)  168 us
    pallas_call x4, Pallas kernels, item_gradients(): pl.pallas_call(_kernel, out_shape=(out_t, out, out), scratch_shapes=[pltp...  52.4 us
    dynamic_update_slice x57, local copies, waits for them, and re-layouts, exchange(): lax.dynamic_update_index_in_dim(out, got[0], (me - shift) % seq_size, 0)  28 us
    unnamed x60, local copies, waits for them, and re-layouts  20.4 us
    dynamic_slice x6, local copies, waits for them, and re-layouts, exchange(): piece = lax.dynamic_index_in_dim(x, (me + shift) % seq_size, 0)  12.5 us
  transfers between devices with their start and end apart: 60, of which 23 were waited for; matrix products, arithmetic and copies ran while one was open for 8% of the time, Pallas kernels for 2%

profile of v9, /device:TPU:13, one launch (start us, length us, event | category | flops | bytes accessed | tf_op | source)
XLA Modules:
  0.0 507.5 jit_solution(4444662241974367265)
XLA Ops:
  0.6 5.0 shard_map.70
  8.4 4.9 shard_map.67
  14.6 3.9 constant_dynamic-slice_fusion
  19.9 3.9 constant_dynamic-slice_fusion.15
  32.4 3.0 collective-permute-start.35
  39.8 22.5 %collective-permute-done.2 = bf16[1,4,2,128,128]{4,3,2,1,0:T(8,128)(2,1)S(1)} collective-permute-done((bf16[1,4,2,128,128]{4,3,2,1,0:T(8,128)(2,1)}, bf16[1,4,2,128,128]{4,3,2,1,0:T(8,128)(2,1)S(1)}, u32[]{:S(2)}, u32[]{:S(2)}) %collective-permute-start.2) | collective-permute-done | bytes 262176 | tf_op jit(solution)/shard_map/ppermute | solution.py:158
  63.8 18.2 %collective-permute-done.3 = bf16[1,4,2,128,128]{4,3,2,1,0:T(8,128)(2,1)S(1)} collective-permute-done((bf16[1,4,2,128,128]{4,3,2,1,0:T(8,128)(2,1)}, bf16[1,4,2,128,128]{4,3,2,1,0:T(8,128)(2,1)S(1)}, u32[]{:S(2)}, u32[]{:S(2)}) %collective-permute-start.3) | collective-permute-done | bytes 262176 | tf_op jit(solution)/shard_map/ppermute | solution.py:158
  83.4 21.0 %collective-permute-done.4 = bf16[1,4,2,128,128]{4,3,2,1,0:T(8,128)(2,1)S(1)} collective-permute-done((bf16[1,4,2,128,128]{4,3,2,1,0:T(8,128)(2,1)}, bf16[1,4,2,128,128]{4,3,2,1,0:T(8,128)(2,1)S(1)}, u32[]{:S(2)}, u32[]{:S(2)}) %collective-permute-start.4) | collective-permute-done | bytes 262176 | tf_op jit(solution)/shard_map/ppermute | solution.py:158
  104.4 18.4 %collective-permute-start.38 = (bf16[1,4,2,128,128]{4,3,2,1,0:T(8,128)(2,1)S(1)}, bf16[1,4,2,128,128]{4,3,2,1,0:T(8,128)(2,1)S(1)}, u32[]{:S(2)}, u32[]{:S(2)}) collective-permute-start(bf16[1,4,2,128,128]{4,3,2,1,0:T(8,128)(2,1)S(1)} %get-tuple-element.47), channel_id=1, source_target_pairs={{0,9},{1,10},{2,11},{3,12},{4,13},{5,14},{6,15},{7,0},{8,1},{9,2},... | collective-permute-start | bytes 786440 | tf_op jit(solution)/shard_map/ppermute | solution.py:158
  124.3 9.3 %collective-permute-start.39 = (bf16[1,4,2,128,128]{4,3,2,1,0:T(8,128)(2,1)S(1)}, bf16[1,4,2,128,128]{4,3,2,1,0:T(8,128)(2,1)S(1)}, u32[]{:S(2)}, u32[]{:S(2)}) collective-permute-start(bf16[1,4,2,128,128]{4,3,2,1,0:T(8,128)(2,1)S(1)} %get-tuple-element.46), channel_id=1, source_target_pairs={{0,10},{1,11},{2,12},{3,13},{4,14},{5,15},{6,0},{7,1},{8,2},{9,3},... | collective-permute-start | bytes 786440 | tf_op jit(solution)/shard_map/ppermute | solution.py:158
  135.0 9.4 %collective-permute-done.6 = bf16[1,4,2,128,128]{4,3,2,1,0:T(8,128)(2,1)S(1)} collective-permute-done((bf16[1,4,2,128,128]{4,3,2,1,0:T(8,128)(2,1)S(1)}, bf16[1,4,2,128,128]{4,3,2,1,0:T(8,128)(2,1)S(1)}, u32[]{:S(2)}, u32[]{:S(2)}) %collective-permute-start.6) | collective-permute-done | bytes 262176 | tf_op jit(solution)/shard_map/ppermute | solution.py:158
  144.4 5.7 %collective-permute-start.40 = (bf16[1,4,2,128,128]{4,3,2,1,0:T(8,128)(2,1)S(1)}, bf16[1,4,2,128,128]{4,3,2,1,0:T(8,128)(2,1)S(1)}, u32[]{:S(2)}, u32[]{:S(2)}) collective-permute-start(bf16[1,4,2,128,128]{4,3,2,1,0:T(8,128)(2,1)S(1)} %get-tuple-element.45), channel_id=1, source_target_pairs={{0,11},{1,12},{2,13},{3,14},{4,15},{5,0},{6,1},{7,2},{8,3},{9,4},{... | collective-permute-start | bytes 786440 | tf_op jit(solution)/shard_map/ppermute | solution.py:158
  151.7 3.8 collective-permute-done.7
  155.5 8.2 %collective-permute-start.41 = (bf16[1,4,2,128,128]{4,3,2,1,0:T(8,128)(2,1)S(1)}, bf16[1,4,2,128,128]{4,3,2,1,0:T(8,128)(2,1)S(1)}, u32[]{:S(2)}, u32[]{:S(2)}) collective-permute-start(bf16[1,4,2,128,128]{4,3,2,1,0:T(8,128)(2,1)S(1)} %get-tuple-element.44), channel_id=1, source_target_pairs={{0,12},{1,13},{2,14},{3,15},{4,0},{5,1},{6,2},{7,3},{8,4},{9,5},{1... | collective-permute-start | bytes 786440 | tf_op jit(solution)/shard_map/ppermute | solution.py:158
  166.2 24.4 %collective-permute-start.42 = (bf16[1,4,2,128,128]{4,3,2,1,0:T(8,128)(2,1)S(1)}, bf16[1,4,2,128,128]{4,3,2,1,0:T(8,128)(2,1)S(1)}, u32[]{:S(2)}, u32[]{:S(2)}) collective-permute-start(bf16[1,4,2,128,128]{4,3,2,1,0:T(8,128)(2,1)S(1)} %get-tuple-element.43), channel_id=1, source_target_pairs={{0,13},{1,14},{2,15},{3,0},{4,1},{5,2},{6,3},{7,4},{8,5},{9,6},{10... | collective-permute-start | bytes 786440 | tf_op jit(solution)/shard_map/ppermute | solution.py:158
  192.0 4.0 collective-permute-start.43
  197.4 4.2 collective-permute-done.10
  202.4 3.0 collective-permute-start.12
  206.1 9.5 %collective-permute-start.13 = (bf16[1,4,2,128,128]{4,3,2,1,0:T(8,128)(2,1)S(1)}, bf16[1,4,2,128,128]{4,3,2,1,0:T(8,128)(2,1)S(1)}, u32[]{:S(2)}, u32[]{:S(2)}) collective-permute-start(bf16[1,4,2,128,128]{4,3,2,1,0:T(8,128)(2,1)S(1)} %get-tuple-element.65), channel_id=1, source_target_pairs={{0,14},{1,15},{2,0},{3,1},{4,2},{5,3},{6,4},{7,5},{8,6},{9,7},{10,... | collective-permute-start | bytes 786440 | tf_op jit(solution)/shard_map/ppermute | solution.py:158
  218.6 8.0 %collective-permute-done.13 = bf16[1,4,2,128,128]{4,3,2,1,0:T(8,128)(2,1)S(1)} collective-permute-done((bf16[1,4,2,128,128]{4,3,2,1,0:T(8,128)(2,1)S(1)}, bf16[1,4,2,128,128]{4,3,2,1,0:T(8,128)(2,1)S(1)}, u32[]{:S(2)}, u32[]{:S(2)}) %collective-permute-start.13) | collective-permute-done | bytes 262176 | tf_op jit(solution)/shard_map/ppermute | solution.py:158
  230.6 3.7 fusion.1
  239.5 13.1 %shard_map.69 = (bf16[128,2048]{1,0:T(8,128)(2,1)S(1)}, bf16[2048,128]{1,0:T(8,128)(2,1)S(1)}, bf16[2048,128]{1,0:T(8,128)(2,1)S(1)}) custom-call(bf16[2048,128]{1,0:T(8,128)(2,1)S(1)} %bitcast.132, bf16[2048,128]{1,0:T(8,128)(2,1)S(1)} %bitcast.105, bf16[128,2048]{1,0:T(8,128)(2,1)S(1)} %bitcast.138, bf16[2048,128]{1,0:T(8,128)(2,1)S(1)} %bitcast.131, ...), custom_call_target="tpu_custom_call" | custom-call | tf_op jit(solution)/shard_map/pallas_call | solution.py:83
  257.8 13.1 %shard_map.68 = (bf16[128,2048]{1,0:T(8,128)(2,1)S(1)}, bf16[2048,128]{1,0:T(8,128)(2,1)S(1)}, bf16[2048,128]{1,0:T(8,128)(2,1)S(1)}) custom-call(bf16[2048,128]{1,0:T(8,128)(2,1)S(1)} %bitcast.122, bf16[2048,128]{1,0:T(8,128)(2,1)S(1)} %bitcast.101, bf16[128,2048]{1,0:T(8,128)(2,1)S(1)} %bitcast.136, bf16[2048,128]{1,0:T(8,128)(2,1)S(1)} %bitcast.121, ...), custom_call_target="tpu_custom_call" | custom-call | tf_op jit(solution)/shard_map/pallas_call | solution.py:83
  286.7 13.1 %shard_map.72 = (bf16[128,2048]{1,0:T(8,128)(2,1)S(1)}, bf16[2048,128]{1,0:T(8,128)(2,1)S(1)}, bf16[2048,128]{1,0:T(8,128)(2,1)S(1)}) custom-call(bf16[2048,128]{1,0:T(8,128)(2,1)S(1)} %bitcast.135, bf16[2048,128]{1,0:T(8,128)(2,1)S(1)} %bitcast.107, bf16[128,2048]{1,0:T(8,128)(2,1)S(1)} %bitcast.139, bf16[2048,128]{1,0:T(8,128)(2,1)S(1)} %bitcast.134, ...), custom_call_target="tpu_custom_call" | custom-call | tf_op jit(solution)/shard_map/pallas_call | solution.py:83
  306.7 13.1 %shard_map.71 = (bf16[128,2048]{1,0:T(8,128)(2,1)S(1)}, bf16[2048,128]{1,0:T(8,128)(2,1)S(1)}, bf16[2048,128]{1,0:T(8,128)(2,1)S(1)}) custom-call(bf16[2048,128]{1,0:T(8,128)(2,1)S(1)} %bitcast.125, bf16[2048,128]{1,0:T(8,128)(2,1)S(1)} %bitcast.103, bf16[128,2048]{1,0:T(8,128)(2,1)S(1)} %bitcast.137, bf16[2048,128]{1,0:T(8,128)(2,1)S(1)} %bitcast.124, ...), custom_call_target="tpu_custom_call" | custom-call | tf_op jit(solution)/shard_map/pallas_call | solution.py:83
  330.9 3.4 collective-permute-start.17
  335.4 12.3 %collective-permute-done.47 = bf16[1,3,2,128,128]{4,3,2,1,0:T(8,128)(2,1)S(1)} collective-permute-done((bf16[1,3,2,128,128]{4,3,2,1,0:T(8,128)(2,1)S(1)}, bf16[1,3,2,128,128]{4,3,2,1,0:T(8,128)(2,1)S(1)}, u32[]{:S(2)}, u32[]{:S(2)}) %collective-permute-start.47) | collective-permute-done | bytes 196640 | tf_op jit(solution)/shard_map/ppermute | solution.py:158
  347.8 3.7 collective-permute-done.48
  351.5 7.3 %collective-permute-start.50 = (bf16[1,3,2,128,128]{4,3,2,1,0:T(8,128)(2,1)S(1)}, bf16[1,3,2,128,128]{4,3,2,1,0:T(8,128)(2,1)S(1)}, u32[]{:S(2)}, u32[]{:S(2)}) collective-permute-start(bf16[1,3,2,128,128]{4,3,2,1,0:T(8,128)(2,1)S(1)} %get-tuple-element.88), channel_id=1, source_target_pairs={{0,6},{1,7},{2,8},{3,9},{4,10},{5,11},{6,12},{7,13},{8,14},{9,15},... | collective-permute-start | bytes 589832 | tf_op jit(solution)/shard_map/ppermute | solution.py:158
  359.4 11.7 %collective-permute-done.50 = bf16[1,3,2,128,128]{4,3,2,1,0:T(8,128)(2,1)S(1)} collective-permute-done((bf16[1,3,2,128,128]{4,3,2,1,0:T(8,128)(2,1)S(1)}, bf16[1,3,2,128,128]{4,3,2,1,0:T(8,128)(2,1)S(1)}, u32[]{:S(2)}, u32[]{:S(2)}) %collective-permute-start.50) | collective-permute-done | bytes 196640 | tf_op jit(solution)/shard_map/ppermute | solution.py:158
  371.1 11.8 %collective-permute-done.51 = bf16[1,3,2,128,128]{4,3,2,1,0:T(8,128)(2,1)S(1)} collective-permute-done((bf16[1,3,2,128,128]{4,3,2,1,0:T(8,128)(2,1)S(1)}, bf16[1,3,2,128,128]{4,3,2,1,0:T(8,128)(2,1)S(1)}, u32[]{:S(2)}, u32[]{:S(2)}) %collective-permute-start.51) | collective-permute-done | bytes 196640 | tf_op jit(solution)/shard_map/ppermute | solution.py:158
  383.0 7.1 %collective-permute-start.53 = (bf16[1,3,2,128,128]{4,3,2,1,0:T(8,128)(2,1)S(1)}, bf16[1,3,2,128,128]{4,3,2,1,0:T(8,128)(2,1)S(1)}, u32[]{:S(2)}, u32[]{:S(2)}) collective-permute-start(bf16[1,3,2,128,128]{4,3,2,1,0:T(8,128)(2,1)S(1)} %get-tuple-element.85), channel_id=1, source_target_pairs={{0,9},{1,10},{2,11},{3,12},{4,13},{5,14},{6,15},{7,0},{8,1},{9,2},... | collective-permute-start | bytes 589832 | tf_op jit(solution)/shard_map/ppermute | solution.py:158
  390.1 3.9 collective-permute-start.54
  395.1 9.8 %collective-permute-start.55 = (bf16[1,3,2,128,128]{4,3,2,1,0:T(8,128)(2,1)S(1)}, bf16[1,3,2,128,128]{4,3,2,1,0:T(8,128)(2,1)S(1)}, u32[]{:S(2)}, u32[]{:S(2)}) collective-permute-start(bf16[1,3,2,128,128]{4,3,2,1,0:T(8,128)(2,1)S(1)} %get-tuple-element.83), channel_id=1, source_target_pairs={{0,11},{1,12},{2,13},{3,14},{4,15},{5,0},{6,1},{7,2},{8,3},{9,4},{... | collective-permute-start | bytes 589832 | tf_op jit(solution)/shard_map/ppermute | solution.py:158
  404.9 3.7 collective-permute-start.56
  408.6 5.2 %collective-permute-start.57 = (bf16[1,3,2,128,128]{4,3,2,1,0:T(8,128)(2,1)S(1)}, bf16[1,3,2,128,128]{4,3,2,1,0:T(8,128)(2,1)S(1)}, u32[]{:S(2)}, u32[]{:S(2)}) collective-permute-start(bf16[1,3,2,128,128]{4,3,2,1,0:T(8,128)(2,1)S(1)} %get-tuple-element.81), channel_id=1, source_target_pairs={{0,13},{1,14},{2,15},{3,0},{4,1},{5,2},{6,3},{7,4},{8,5},{9,6},{10... | collective-permute-start | bytes 589832 | tf_op jit(solution)/shard_map/ppermute | solution.py:158
  413.8 3.5 collective-permute-start.58
  417.9 3.8 collective-permute-done.58
  421.7 3.2 collective-permute-done.59
  425.0 6.7 %collective-permute-start.19 = (bf16[1,3,2,128,128]{4,3,2,1,0:T(8,128)(2,1)}, bf16[1,3,2,128,128]{4,3,2,1,0:T(8,128)(2,1)}, u32[]{:S(2)}, u32[]{:S(2)}) collective-permute-start(bf16[1,3,2,128,128]{4,3,2,1,0:T(8,128)(2,1)} %get-tuple-element.104), channel_id=1, source_target_pairs={{0,5},{1,6},{2,7},{3,8},{4,9},{5,10},{6,11},{7,12},{8,13},{9,14},{... | collective-permute-start | bytes 589832 | tf_op jit(solution)/shard_map/ppermute | solution.py:158
  436.6 4.6 shard_map.73
  443.7 3.9 collective-permute-start.22
  452.5 3.0 collective-permute-start.24
  456.5 12.4 %collective-permute-done.20 = bf16[1,3,2,128,128]{4,3,2,1,0:T(8,128)(2,1)S(1)} collective-permute-done((bf16[1,3,2,128,128]{4,3,2,1,0:T(8,128)(2,1)}, bf16[1,3,2,128,128]{4,3,2,1,0:T(8,128)(2,1)S(1)}, u32[]{:S(2)}, u32[]{:S(2)}) %collective-permute-start.20) | collective-permute-done | bytes 196640 | tf_op jit(solution)/shard_map/ppermute | solution.py:158
  468.9 6.1 %collective-permute-done.21 = bf16[1,3,2,128,128]{4,3,2,1,0:T(8,128)(2,1)S(1)} collective-permute-done((bf16[1,3,2,128,128]{4,3,2,1,0:T(8,128)(2,1)}, bf16[1,3,2,128,128]{4,3,2,1,0:T(8,128)(2,1)S(1)}, u32[]{:S(2)}, u32[]{:S(2)}) %collective-permute-start.21) | collective-permute-done | bytes 196640 | tf_op jit(solution)/shard_map/ppermute | solution.py:158
  475.0 6.4 %collective-permute-done.22 = bf16[1,3,2,128,128]{4,3,2,1,0:T(8,128)(2,1)S(1)} collective-permute-done((bf16[1,3,2,128,128]{4,3,2,1,0:T(8,128)(2,1)}, bf16[1,3,2,128,128]{4,3,2,1,0:T(8,128)(2,1)S(1)}, u32[]{:S(2)}, u32[]{:S(2)}) %collective-permute-start.22) | collective-permute-done | bytes 196640 | tf_op jit(solution)/shard_map/ppermute | solution.py:158
  483.4 14.1 %collective-permute-start.29 = (bf16[1,3,2,128,128]{4,3,2,1,0:T(8,128)(2,1)S(1)}, bf16[1,3,2,128,128]{4,3,2,1,0:T(8,128)(2,1)S(1)}, u32[]{:S(2)}, u32[]{:S(2)}) collective-permute-start(bf16[1,3,2,128,128]{4,3,2,1,0:T(8,128)(2,1)S(1)} %get-tuple-element.94), channel_id=1, source_target_pairs={{0,15},{1,0},{2,1},{3,2},{4,3},{5,4},{6,5},{7,6},{8,7},{9,8},{10,9... | collective-permute-start | bytes 589832 | tf_op jit(solution)/shard_map/ppermute | solution.py:158
  503.0 4.5 shard_map.74
  (220 shorter events, 107.6 us)
Async XLA Ops:
  25.0 12.0 %collective-permute-start.32 = (bf16[1,4,2,128,128]{4,3,2,1,0:T(8,128)(2,1)}, bf16[1,4,2,128,128]{4,3,2,1,0:T(8,128)(2,1)}, u32[]{:S(2)}, u32[]{:S(2)}) collective-permute-start(bf16[1,4,2,128,128]{4,3,2,1,0:T(8,128)(2,1)} %get-tuple-element.53), channel_id=1, source_target_pairs={{0,3},{1,4},{2,5},{3,6},{4,7},{5,8},{6,9},{7,10},{8,11},{9,12},{10... | collective-permute-start | bytes 786440 | tf_op jit(solution)/shard_map/ppermute | solution.py:158
  26.7 36.3 %collective-permute-start.33 = (bf16[1,4,2,128,128]{4,3,2,1,0:T(8,128)(2,1)}, bf16[1,4,2,128,128]{4,3,2,1,0:T(8,128)(2,1)S(1)}, u32[]{:S(2)}, u32[]{:S(2)}) collective-permute-start(bf16[1,4,2,128,128]{4,3,2,1,0:T(8,128)(2,1)} %get-tuple-element.52), channel_id=1, source_target_pairs={{0,4},{1,5},{2,6},{3,7},{4,8},{5,9},{6,10},{7,11},{8,12},{9,13},{1... | collective-permute-start | bytes 786440 | tf_op jit(solution)/shard_map/ppermute | solution.py:158
  28.0 54.6 %collective-permute-start.34 = (bf16[1,4,2,128,128]{4,3,2,1,0:T(8,128)(2,1)}, bf16[1,4,2,128,128]{4,3,2,1,0:T(8,128)(2,1)S(1)}, u32[]{:S(2)}, u32[]{:S(2)}) collective-permute-start(bf16[1,4,2,128,128]{4,3,2,1,0:T(8,128)(2,1)} %get-tuple-element.51), channel_id=1, source_target_pairs={{0,5},{1,6},{2,7},{3,8},{4,9},{5,10},{6,11},{7,12},{8,13},{9,14},{... | collective-permute-start | bytes 786440 | tf_op jit(solution)/shard_map/ppermute | solution.py:158
  29.0 33.3 %collective-permute-start.2 = (bf16[1,4,2,128,128]{4,3,2,1,0:T(8,128)(2,1)}, bf16[1,4,2,128,128]{4,3,2,1,0:T(8,128)(2,1)S(1)}, u32[]{:S(2)}, u32[]{:S(2)}) collective-permute-start(bf16[1,4,2,128,128]{4,3,2,1,0:T(8,128)(2,1)} %get-tuple-element.76), channel_id=1, source_target_pairs={{0,3},{1,4},{2,5},{3,6},{4,7},{5,8},{6,9},{7,10},{8,11},{9,12},{10... | collective-permute-start | bytes 786440 | tf_op jit(solution)/shard_map/ppermute | solution.py:158
  32.4 91.2 %collective-permute-start.35 = (bf16[1,4,2,128,128]{4,3,2,1,0:T(8,128)(2,1)}, bf16[1,4,2,128,128]{4,3,2,1,0:T(8,128)(2,1)S(1)}, u32[]{:S(2)}, u32[]{:S(2)}) collective-permute-start(bf16[1,4,2,128,128]{4,3,2,1,0:T(8,128)(2,1)} %get-tuple-element.50), channel_id=1, source_target_pairs={{0,6},{1,7},{2,8},{3,9},{4,10},{5,11},{6,12},{7,13},{8,14},{9,15},... | collective-permute-start | bytes 786440 | tf_op jit(solution)/shard_map/ppermute | solution.py:158
  37.0 44.9 %collective-permute-start.3 = (bf16[1,4,2,128,128]{4,3,2,1,0:T(8,128)(2,1)}, bf16[1,4,2,128,128]{4,3,2,1,0:T(8,128)(2,1)S(1)}, u32[]{:S(2)}, u32[]{:S(2)}) collective-permute-start(bf16[1,4,2,128,128]{4,3,2,1,0:T(8,128)(2,1)} %get-tuple-element.75), channel_id=1, source_target_pairs={{0,4},{1,5},{2,6},{3,7},{4,8},{5,9},{6,10},{7,11},{8,12},{9,13},{1... | collective-permute-start | bytes 786440 | tf_op jit(solution)/shard_map/ppermute | solution.py:158
  62.3 72.0 %collective-permute-start.36 = (bf16[1,4,2,128,128]{4,3,2,1,0:T(8,128)(2,1)}, bf16[1,4,2,128,128]{4,3,2,1,0:T(8,128)(2,1)S(1)}, u32[]{:S(2)}, u32[]{:S(2)}) collective-permute-start(bf16[1,4,2,128,128]{4,3,2,1,0:T(8,128)(2,1)} %get-tuple-element.49), channel_id=1, source_target_pairs={{0,7},{1,8},{2,9},{3,10},{4,11},{5,12},{6,13},{7,14},{8,15},{9,0},... | collective-permute-start | bytes 786440 | tf_op jit(solution)/shard_map/ppermute | solution.py:158
  63.0 41.4 %collective-permute-start.4 = (bf16[1,4,2,128,128]{4,3,2,1,0:T(8,128)(2,1)}, bf16[1,4,2,128,128]{4,3,2,1,0:T(8,128)(2,1)S(1)}, u32[]{:S(2)}, u32[]{:S(2)}) collective-permute-start(bf16[1,4,2,128,128]{4,3,2,1,0:T(8,128)(2,1)} %get-tuple-element.74), channel_id=1, source_target_pairs={{0,5},{1,6},{2,7},{3,8},{4,9},{5,10},{6,11},{7,12},{8,13},{9,14},{... | collective-permute-start | bytes 786440 | tf_op jit(solution)/shard_map/ppermute | solution.py:158
  82.0 68.8 %collective-permute-start.37 = (bf16[1,4,2,128,128]{4,3,2,1,0:T(8,128)(2,1)}, bf16[1,4,2,128,128]{4,3,2,1,0:T(8,128)(2,1)S(1)}, u32[]{:S(2)}, u32[]{:S(2)}) collective-permute-start(bf16[1,4,2,128,128]{4,3,2,1,0:T(8,128)(2,1)} %get-tuple-element.48), channel_id=1, source_target_pairs={{0,8},{1,9},{2,10},{3,11},{4,12},{5,13},{6,14},{7,15},{8,0},{9,1},... | collective-permute-start | bytes 786440 | tf_op jit(solution)/shard_map/ppermute | solution.py:158
  82.7 41.6 %collective-permute-start.5 = (bf16[1,4,2,128,128]{4,3,2,1,0:T(8,128)(2,1)S(1)}, bf16[1,4,2,128,128]{4,3,2,1,0:T(8,128)(2,1)S(1)}, u32[]{:S(2)}, u32[]{:S(2)}) collective-permute-start(bf16[1,4,2,128,128]{4,3,2,1,0:T(8,128)(2,1)S(1)} %copy-done.29), channel_id=1, source_target_pairs={{0,6},{1,7},{2,8},{3,9},{4,10},{5,11},{6,12},{7,13},{8,14},{9,15},... | collective-permute-start | bytes 786440 | tf_op jit(solution)/shard_map/ppermute | solution.py:158
  104.4 59.9 %collective-permute-start.38 = (bf16[1,4,2,128,128]{4,3,2,1,0:T(8,128)(2,1)S(1)}, bf16[1,4,2,128,128]{4,3,2,1,0:T(8,128)(2,1)S(1)}, u32[]{:S(2)}, u32[]{:S(2)}) collective-permute-start(bf16[1,4,2,128,128]{4,3,2,1,0:T(8,128)(2,1)S(1)} %get-tuple-element.47), channel_id=1, source_target_pairs={{0,9},{1,10},{2,11},{3,12},{4,13},{5,14},{6,15},{7,0},{8,1},{9,2},... | collective-permute-start | bytes 786440 | tf_op jit(solution)/shard_map/ppermute | solution.py:158
  123.6 20.8 %collective-permute-start.6 = (bf16[1,4,2,128,128]{4,3,2,1,0:T(8,128)(2,1)S(1)}, bf16[1,4,2,128,128]{4,3,2,1,0:T(8,128)(2,1)S(1)}, u32[]{:S(2)}, u32[]{:S(2)}) collective-permute-start(bf16[1,4,2,128,128]{4,3,2,1,0:T(8,128)(2,1)S(1)} %copy-done.28), channel_id=1, source_target_pairs={{0,7},{1,8},{2,9},{3,10},{4,11},{5,12},{6,13},{7,14},{8,15},{9,0},... | collective-permute-start | bytes 786440 | tf_op jit(solution)/shard_map/ppermute | solution.py:158
  124.3 67.0 %collective-permute-start.39 = (bf16[1,4,2,128,128]{4,3,2,1,0:T(8,128)(2,1)S(1)}, bf16[1,4,2,128,128]{4,3,2,1,0:T(8,128)(2,1)S(1)}, u32[]{:S(2)}, u32[]{:S(2)}) collective-permute-start(bf16[1,4,2,128,128]{4,3,2,1,0:T(8,128)(2,1)S(1)} %get-tuple-element.46), channel_id=1, source_target_pairs={{0,10},{1,11},{2,12},{3,13},{4,14},{5,15},{6,0},{7,1},{8,2},{9,3},... | collective-permute-start | bytes 786440 | tf_op jit(solution)/shard_map/ppermute | solution.py:158
  134.3 21.2 %collective-permute-start.7 = (bf16[1,4,2,128,128]{4,3,2,1,0:T(8,128)(2,1)S(1)}, bf16[1,4,2,128,128]{4,3,2,1,0:T(8,128)(2,1)S(1)}, u32[]{:S(2)}, u32[]{:S(2)}) collective-permute-start(bf16[1,4,2,128,128]{4,3,2,1,0:T(8,128)(2,1)S(1)} %copy-done.27), channel_id=1, source_target_pairs={{0,8},{1,9},{2,10},{3,11},{4,12},{5,13},{6,14},{7,15},{8,0},{9,1},... | collective-permute-start | bytes 786440 | tf_op jit(solution)/shard_map/ppermute | solution.py:158
  144.4 52.3 %collective-permute-start.40 = (bf16[1,4,2,128,128]{4,3,2,1,0:T(8,128)(2,1)S(1)}, bf16[1,4,2,128,128]{4,3,2,1,0:T(8,128)(2,1)S(1)}, u32[]{:S(2)}, u32[]{:S(2)}) collective-permute-start(bf16[1,4,2,128,128]{4,3,2,1,0:T(8,128)(2,1)S(1)} %get-tuple-element.45), channel_id=1, source_target_pairs={{0,11},{1,12},{2,13},{3,14},{4,15},{5,0},{6,1},{7,2},{8,3},{9,4},{... | collective-permute-start | bytes 786440 | tf_op jit(solution)/shard_map/ppermute | solution.py:158
  150.8 15.4 %collective-permute-start.8 = (bf16[1,4,2,128,128]{4,3,2,1,0:T(8,128)(2,1)S(1)}, bf16[1,4,2,128,128]{4,3,2,1,0:T(8,128)(2,1)S(1)}, u32[]{:S(2)}, u32[]{:S(2)}) collective-permute-start(bf16[1,4,2,128,128]{4,3,2,1,0:T(8,128)(2,1)S(1)} %copy-done.26), channel_id=1, source_target_pairs={{0,9},{1,10},{2,11},{3,12},{4,13},{5,14},{6,15},{7,0},{8,1},{9,2},... | collective-permute-start | bytes 786440 | tf_op jit(solution)/shard_map/ppermute | solution.py:158
  155.5 46.9 %collective-permute-start.41 = (bf16[1,4,2,128,128]{4,3,2,1,0:T(8,128)(2,1)S(1)}, bf16[1,4,2,128,128]{4,3,2,1,0:T(8,128)(2,1)S(1)}, u32[]{:S(2)}, u32[]{:S(2)}) collective-permute-start(bf16[1,4,2,128,128]{4,3,2,1,0:T(8,128)(2,1)S(1)} %get-tuple-element.44), channel_id=1, source_target_pairs={{0,12},{1,13},{2,14},{3,15},{4,0},{5,1},{6,2},{7,3},{8,4},{9,5},{1... | collective-permute-start | bytes 786440 | tf_op jit(solution)/shard_map/ppermute | solution.py:158
  164.4 27.6 %collective-permute-start.9 = (bf16[1,4,2,128,128]{4,3,2,1,0:T(8,128)(2,1)S(1)}, bf16[1,4,2,128,128]{4,3,2,1,0:T(8,128)(2,1)S(1)}, u32[]{:S(2)}, u32[]{:S(2)}) collective-permute-start(bf16[1,4,2,128,128]{4,3,2,1,0:T(8,128)(2,1)S(1)} %get-tuple-element.69), channel_id=1, source_target_pairs={{0,10},{1,11},{2,12},{3,13},{4,14},{5,15},{6,0},{7,1},{8,2},{9,3},... | collective-permute-start | bytes 786440 | tf_op jit(solution)/shard_map/ppermute | solution.py:158
  166.2 50.2 %collective-permute-start.42 = (bf16[1,4,2,128,128]{4,3,2,1,0:T(8,128)(2,1)S(1)}, bf16[1,4,2,128,128]{4,3,2,1,0:T(8,128)(2,1)S(1)}, u32[]{:S(2)}, u32[]{:S(2)}) collective-permute-start(bf16[1,4,2,128,128]{4,3,2,1,0:T(8,128)(2,1)S(1)} %get-tuple-element.43), channel_id=1, source_target_pairs={{0,13},{1,14},{2,15},{3,0},{4,1},{5,2},{6,3},{7,4},{8,5},{9,6},{10... | collective-permute-start | bytes 786440 | tf_op jit(solution)/shard_map/ppermute | solution.py:158
  192.0 25.8 %collective-permute-start.43 = (bf16[1,4,2,128,128]{4,3,2,1,0:T(8,128)(2,1)S(1)}, bf16[1,4,2,128,128]{4,3,2,1,0:T(8,128)(2,1)S(1)}, u32[]{:S(2)}, u32[]{:S(2)}) collective-permute-start(bf16[1,4,2,128,128]{4,3,2,1,0:T(8,128)(2,1)S(1)} %get-tuple-element.42), channel_id=1, source_target_pairs={{0,14},{1,15},{2,0},{3,1},{4,2},{5,3},{6,4},{7,5},{8,6},{9,7},{10,... | collective-permute-start | bytes 786440 | tf_op jit(solution)/shard_map/ppermute | solution.py:158
  201.7 25.6 %collective-permute-start.44 = (bf16[1,4,2,128,128]{4,3,2,1,0:T(8,128)(2,1)S(1)}, bf16[1,4,2,128,128]{4,3,2,1,0:T(8,128)(2,1)S(1)}, u32[]{:S(2)}, u32[]{:S(2)}) collective-permute-start(bf16[1,4,2,128,128]{4,3,2,1,0:T(8,128)(2,1)S(1)} %get-tuple-element.41), channel_id=1, source_target_pairs={{0,15},{1,0},{2,1},{3,2},{4,3},{5,4},{6,5},{7,6},{8,7},{9,8},{10,9... | collective-permute-start | bytes 786440 | tf_op jit(solution)/shard_map/ppermute | solution.py:158
  202.4 14.7 %collective-permute-start.12 = (bf16[1,4,2,128,128]{4,3,2,1,0:T(8,128)(2,1)S(1)}, bf16[1,4,2,128,128]{4,3,2,1,0:T(8,128)(2,1)S(1)}, u32[]{:S(2)}, u32[]{:S(2)}) collective-permute-start(bf16[1,4,2,128,128]{4,3,2,1,0:T(8,128)(2,1)S(1)} %get-tuple-element.66), channel_id=1, source_target_pairs={{0,13},{1,14},{2,15},{3,0},{4,1},{5,2},{6,3},{7,4},{8,5},{9,6},{10... | collective-permute-start | bytes 786440 | tf_op jit(solution)/shard_map/ppermute | solution.py:158
  206.1 20.5 %collective-permute-start.13 = (bf16[1,4,2,128,128]{4,3,2,1,0:T(8,128)(2,1)S(1)}, bf16[1,4,2,128,128]{4,3,2,1,0:T(8,128)(2,1)S(1)}, u32[]{:S(2)}, u32[]{:S(2)}) collective-permute-start(bf16[1,4,2,128,128]{4,3,2,1,0:T(8,128)(2,1)S(1)} %get-tuple-element.65), channel_id=1, source_target_pairs={{0,14},{1,15},{2,0},{3,1},{4,2},{5,3},{6,4},{7,5},{8,6},{9,7},{10,... | collective-permute-start | bytes 786440 | tf_op jit(solution)/shard_map/ppermute | solution.py:158
  216.4 13.4 %collective-permute-start.14 = (bf16[1,4,2,128,128]{4,3,2,1,0:T(8,128)(2,1)S(1)}, bf16[1,4,2,128,128]{4,3,2,1,0:T(8,128)(2,1)S(1)}, u32[]{:S(2)}, u32[]{:S(2)}) collective-permute-start(bf16[1,4,2,128,128]{4,3,2,1,0:T(8,128)(2,1)S(1)} %get-tuple-element.64), channel_id=1, source_target_pairs={{0,15},{1,0},{2,1},{3,2},{4,3},{5,4},{6,5},{7,6},{8,7},{9,8},{10,9... | collective-permute-start | bytes 786440 | tf_op jit(solution)/shard_map/ppermute | solution.py:158
  328.7 112.5 %collective-permute-start.15 = (bf16[1,3,2,128,128]{4,3,2,1,0:T(8,128)(2,1)}, bf16[1,3,2,128,128]{4,3,2,1,0:T(8,128)(2,1)}, u32[]{:S(2)}, u32[]{:S(2)}) collective-permute-start(bf16[1,3,2,128,128]{4,3,2,1,0:T(8,128)(2,1)} %get-tuple-element.108), channel_id=1, source_target_pairs={{0,1},{1,2},{2,3},{3,4},{4,5},{5,6},{6,7},{7,8},{8,9},{9,10},{10,1... | collective-permute-start | bytes 589832 | tf_op jit(solution)/shard_map/ppermute | solution.py:158
  330.9 111.3 %collective-permute-start.16 = (bf16[1,3,2,128,128]{4,3,2,1,0:T(8,128)(2,1)}, bf16[1,3,2,128,128]{4,3,2,1,0:T(8,128)(2,1)}, u32[]{:S(2)}, u32[]{:S(2)}) collective-permute-start(bf16[1,3,2,128,128]{4,3,2,1,0:T(8,128)(2,1)} %get-tuple-element.107), channel_id=1, source_target_pairs={{0,2},{1,3},{2,4},{3,5},{4,6},{5,7},{6,8},{7,9},{8,10},{9,11},{10,... | collective-permute-start | bytes 589832 | tf_op jit(solution)/shard_map/ppermute | solution.py:158
  330.9 112.8 %collective-permute-start.17 = (bf16[1,3,2,128,128]{4,3,2,1,0:T(8,128)(2,1)}, bf16[1,3,2,128,128]{4,3,2,1,0:T(8,128)(2,1)}, u32[]{:S(2)}, u32[]{:S(2)}) collective-permute-start(bf16[1,3,2,128,128]{4,3,2,1,0:T(8,128)(2,1)} %get-tuple-element.106), channel_id=1, source_target_pairs={{0,3},{1,4},{2,5},{3,6},{4,7},{5,8},{6,9},{7,10},{8,11},{9,12},{10... | collective-permute-start | bytes 589832 | tf_op jit(solution)/shard_map/ppermute | solution.py:158
  334.3 13.4 %collective-permute-start.47 = (bf16[1,3,2,128,128]{4,3,2,1,0:T(8,128)(2,1)S(1)}, bf16[1,3,2,128,128]{4,3,2,1,0:T(8,128)(2,1)S(1)}, u32[]{:S(2)}, u32[]{:S(2)}) collective-permute-start(bf16[1,3,2,128,128]{4,3,2,1,0:T(8,128)(2,1)S(1)} %get-tuple-element.91), channel_id=1, source_target_pairs={{0,3},{1,4},{2,5},{3,6},{4,7},{5,8},{6,9},{7,10},{8,11},{9,12},{10... | collective-permute-start | bytes 589832 | tf_op jit(solution)/shard_map/ppermute | solution.py:158
  335.1 16.4 %collective-permute-start.48 = (bf16[1,3,2,128,128]{4,3,2,1,0:T(8,128)(2,1)S(1)}, bf16[1,3,2,128,128]{4,3,2,1,0:T(8,128)(2,1)S(1)}, u32[]{:S(2)}, u32[]{:S(2)}) collective-permute-start(bf16[1,3,2,128,128]{4,3,2,1,0:T(8,128)(2,1)S(1)} %get-tuple-element.90), channel_id=1, source_target_pairs={{0,4},{1,5},{2,6},{3,7},{4,8},{5,9},{6,10},{7,11},{8,12},{9,13},{1... | collective-permute-start | bytes 589832 | tf_op jit(solution)/shard_map/ppermute | solution.py:158
  347.7 11.7 %collective-permute-start.49 = (bf16[1,3,2,128,128]{4,3,2,1,0:T(8,128)(2,1)S(1)}, bf16[1,3,2,128,128]{4,3,2,1,0:T(8,128)(2,1)S(1)}, u32[]{:S(2)}, u32[]{:S(2)}) collective-permute-start(bf16[1,3,2,128,128]{4,3,2,1,0:T(8,128)(2,1)S(1)} %get-tuple-element.89), channel_id=1, source_target_pairs={{0,5},{1,6},{2,7},{3,8},{4,9},{5,10},{6,11},{7,12},{8,13},{9,14},{... | collective-permute-start | bytes 589832 | tf_op jit(solution)/shard_map/ppermute | solution.py:158
  351.5 19.6 %collective-permute-start.50 = (bf16[1,3,2,128,128]{4,3,2,1,0:T(8,128)(2,1)S(1)}, bf16[1,3,2,128,128]{4,3,2,1,0:T(8,128)(2,1)S(1)}, u32[]{:S(2)}, u32[]{:S(2)}) collective-permute-start(bf16[1,3,2,128,128]{4,3,2,1,0:T(8,128)(2,1)S(1)} %get-tuple-element.88), channel_id=1, source_target_pairs={{0,6},{1,7},{2,8},{3,9},{4,10},{5,11},{6,12},{7,13},{8,14},{9,15},... | collective-permute-start | bytes 589832 | tf_op jit(solution)/shard_map/ppermute | solution.py:158
  359.4 23.6 %collective-permute-start.51 = (bf16[1,3,2,128,128]{4,3,2,1,0:T(8,128)(2,1)S(1)}, bf16[1,3,2,128,128]{4,3,2,1,0:T(8,128)(2,1)S(1)}, u32[]{:S(2)}, u32[]{:S(2)}) collective-permute-start(bf16[1,3,2,128,128]{4,3,2,1,0:T(8,128)(2,1)S(1)} %get-tuple-element.87), channel_id=1, source_target_pairs={{0,7},{1,8},{2,9},{3,10},{4,11},{5,12},{6,13},{7,14},{8,15},{9,0},... | collective-permute-start | bytes 589832 | tf_op jit(solution)/shard_map/ppermute | solution.py:158
  371.1 19.0 %collective-permute-start.52 = (bf16[1,3,2,128,128]{4,3,2,1,0:T(8,128)(2,1)S(1)}, bf16[1,3,2,128,128]{4,3,2,1,0:T(8,128)(2,1)S(1)}, u32[]{:S(2)}, u32[]{:S(2)}) collective-permute-start(bf16[1,3,2,128,128]{4,3,2,1,0:T(8,128)(2,1)S(1)} %get-tuple-element.86), channel_id=1, source_target_pairs={{0,8},{1,9},{2,10},{3,11},{4,12},{5,13},{6,14},{7,15},{8,0},{9,1},... | collective-permute-start | bytes 589832 | tf_op jit(solution)/shard_map/ppermute | solution.py:158
  383.0 12.1 %collective-permute-start.53 = (bf16[1,3,2,128,128]{4,3,2,1,0:T(8,128)(2,1)S(1)}, bf16[1,3,2,128,128]{4,3,2,1,0:T(8,128)(2,1)S(1)}, u32[]{:S(2)}, u32[]{:S(2)}) collective-permute-start(bf16[1,3,2,128,128]{4,3,2,1,0:T(8,128)(2,1)S(1)} %get-tuple-element.85), channel_id=1, source_target_pairs={{0,9},{1,10},{2,11},{3,12},{4,13},{5,14},{6,15},{7,0},{8,1},{9,2},... | collective-permute-start | bytes 589832 | tf_op jit(solution)/shard_map/ppermute | solution.py:158
  390.1 14.7 %collective-permute-start.54 = (bf16[1,3,2,128,128]{4,3,2,1,0:T(8,128)(2,1)S(1)}, bf16[1,3,2,128,128]{4,3,2,1,0:T(8,128)(2,1)S(1)}, u32[]{:S(2)}, u32[]{:S(2)}) collective-permute-start(bf16[1,3,2,128,128]{4,3,2,1,0:T(8,128)(2,1)S(1)} %get-tuple-element.84), channel_id=1, source_target_pairs={{0,10},{1,11},{2,12},{3,13},{4,14},{5,15},{6,0},{7,1},{8,2},{9,3},... | collective-permute-start | bytes 589832 | tf_op jit(solution)/shard_map/ppermute | solution.py:158
  395.1 13.5 %collective-permute-start.55 = (bf16[1,3,2,128,128]{4,3,2,1,0:T(8,128)(2,1)S(1)}, bf16[1,3,2,128,128]{4,3,2,1,0:T(8,128)(2,1)S(1)}, u32[]{:S(2)}, u32[]{:S(2)}) collective-permute-start(bf16[1,3,2,128,128]{4,3,2,1,0:T(8,128)(2,1)S(1)} %get-tuple-element.83), channel_id=1, source_target_pairs={{0,11},{1,12},{2,13},{3,14},{4,15},{5,0},{6,1},{7,2},{8,3},{9,4},{... | collective-permute-start | bytes 589832 | tf_op jit(solution)/shard_map/ppermute | solution.py:158
  421.7 26.8 %collective-permute-start.18 = (bf16[1,3,2,128,128]{4,3,2,1,0:T(8,128)(2,1)}, bf16[1,3,2,128,128]{4,3,2,1,0:T(8,128)(2,1)}, u32[]{:S(2)}, u32[]{:S(2)}) collective-permute-start(bf16[1,3,2,128,128]{4,3,2,1,0:T(8,128)(2,1)} %get-tuple-element.105), channel_id=1, source_target_pairs={{0,4},{1,5},{2,6},{3,7},{4,8},{5,9},{6,10},{7,11},{8,12},{9,13},{1... | collective-permute-start | bytes 589832 | tf_op jit(solution)/shard_map/ppermute | solution.py:158
  425.0 27.5 %collective-permute-start.19 = (bf16[1,3,2,128,128]{4,3,2,1,0:T(8,128)(2,1)}, bf16[1,3,2,128,128]{4,3,2,1,0:T(8,128)(2,1)}, u32[]{:S(2)}, u32[]{:S(2)}) collective-permute-start(bf16[1,3,2,128,128]{4,3,2,1,0:T(8,128)(2,1)} %get-tuple-element.104), channel_id=1, source_target_pairs={{0,5},{1,6},{2,7},{3,8},{4,9},{5,10},{6,11},{7,12},{8,13},{9,14},{... | collective-permute-start | bytes 589832 | tf_op jit(solution)/shard_map/ppermute | solution.py:158
  441.2 27.6 %collective-permute-start.20 = (bf16[1,3,2,128,128]{4,3,2,1,0:T(8,128)(2,1)}, bf16[1,3,2,128,128]{4,3,2,1,0:T(8,128)(2,1)S(1)}, u32[]{:S(2)}, u32[]{:S(2)}) collective-permute-start(bf16[1,3,2,128,128]{4,3,2,1,0:T(8,128)(2,1)} %get-tuple-element.103), channel_id=1, source_target_pairs={{0,6},{1,7},{2,8},{3,9},{4,10},{5,11},{6,12},{7,13},{8,14},{9,15},... | collective-permute-start | bytes 589832 | tf_op jit(solution)/shard_map/ppermute | solution.py:158
  442.2 32.8 %collective-permute-start.21 = (bf16[1,3,2,128,128]{4,3,2,1,0:T(8,128)(2,1)}, bf16[1,3,2,128,128]{4,3,2,1,0:T(8,128)(2,1)S(1)}, u32[]{:S(2)}, u32[]{:S(2)}) collective-permute-start(bf16[1,3,2,128,128]{4,3,2,1,0:T(8,128)(2,1)} %get-tuple-element.102), channel_id=1, source_target_pairs={{0,7},{1,8},{2,9},{3,10},{4,11},{5,12},{6,13},{7,14},{8,15},{9,0},... | collective-permute-start | bytes 589832 | tf_op jit(solution)/shard_map/ppermute | solution.py:158
  443.7 37.8 %collective-permute-start.22 = (bf16[1,3,2,128,128]{4,3,2,1,0:T(8,128)(2,1)}, bf16[1,3,2,128,128]{4,3,2,1,0:T(8,128)(2,1)S(1)}, u32[]{:S(2)}, u32[]{:S(2)}) collective-permute-start(bf16[1,3,2,128,128]{4,3,2,1,0:T(8,128)(2,1)} %get-tuple-element.101), channel_id=1, source_target_pairs={{0,8},{1,9},{2,10},{3,11},{4,12},{5,13},{6,14},{7,15},{8,0},{9,1},... | collective-permute-start | bytes 589832 | tf_op jit(solution)/shard_map/ppermute | solution.py:158
  448.5 33.8 %collective-permute-start.23 = (bf16[1,3,2,128,128]{4,3,2,1,0:T(8,128)(2,1)}, bf16[1,3,2,128,128]{4,3,2,1,0:T(8,128)(2,1)S(1)}, u32[]{:S(2)}, u32[]{:S(2)}) collective-permute-start(bf16[1,3,2,128,128]{4,3,2,1,0:T(8,128)(2,1)} %get-tuple-element.100), channel_id=1, source_target_pairs={{0,9},{1,10},{2,11},{3,12},{4,13},{5,14},{6,15},{7,0},{8,1},{9,2},... | collective-permute-start | bytes 589832 | tf_op jit(solution)/shard_map/ppermute | solution.py:158
  452.5 30.9 %collective-permute-start.24 = (bf16[1,3,2,128,128]{4,3,2,1,0:T(8,128)(2,1)}, bf16[1,3,2,128,128]{4,3,2,1,0:T(8,128)(2,1)S(1)}, u32[]{:S(2)}, u32[]{:S(2)}) collective-permute-start(bf16[1,3,2,128,128]{4,3,2,1,0:T(8,128)(2,1)} %get-tuple-element.99), channel_id=1, source_target_pairs={{0,10},{1,11},{2,12},{3,13},{4,14},{5,15},{6,0},{7,1},{8,2},{9,3},... | collective-permute-start | bytes 589832 | tf_op jit(solution)/shard_map/ppermute | solution.py:158
  468.8 28.7 %collective-permute-start.25 = (bf16[1,3,2,128,128]{4,3,2,1,0:T(8,128)(2,1)}, bf16[1,3,2,128,128]{4,3,2,1,0:T(8,128)(2,1)S(1)}, u32[]{:S(2)}, u32[]{:S(2)}) collective-permute-start(bf16[1,3,2,128,128]{4,3,2,1,0:T(8,128)(2,1)} %get-tuple-element.98), channel_id=1, source_target_pairs={{0,11},{1,12},{2,13},{3,14},{4,15},{5,0},{6,1},{7,2},{8,3},{9,4},{... | collective-permute-start | bytes 589832 | tf_op jit(solution)/shard_map/ppermute | solution.py:158
  475.0 22.6 %collective-permute-start.26 = (bf16[1,3,2,128,128]{4,3,2,1,0:T(8,128)(2,1)}, bf16[1,3,2,128,128]{4,3,2,1,0:T(8,128)(2,1)S(1)}, u32[]{:S(2)}, u32[]{:S(2)}) collective-permute-start(bf16[1,3,2,128,128]{4,3,2,1,0:T(8,128)(2,1)} %get-tuple-element.97), channel_id=1, source_target_pairs={{0,12},{1,13},{2,14},{3,15},{4,0},{5,1},{6,2},{7,3},{8,4},{9,5},{1... | collective-permute-start | bytes 589832 | tf_op jit(solution)/shard_map/ppermute | solution.py:158
  481.5 16.1 %collective-permute-start.27 = (bf16[1,3,2,128,128]{4,3,2,1,0:T(8,128)(2,1)}, bf16[1,3,2,128,128]{4,3,2,1,0:T(8,128)(2,1)S(1)}, u32[]{:S(2)}, u32[]{:S(2)}) collective-permute-start(bf16[1,3,2,128,128]{4,3,2,1,0:T(8,128)(2,1)} %get-tuple-element.96), channel_id=1, source_target_pairs={{0,13},{1,14},{2,15},{3,0},{4,1},{5,2},{6,3},{7,4},{8,5},{9,6},{10... | collective-permute-start | bytes 589832 | tf_op jit(solution)/shard_map/ppermute | solution.py:158
  482.4 17.7 %collective-permute-start.28 = (bf16[1,3,2,128,128]{4,3,2,1,0:T(8,128)(2,1)S(1)}, bf16[1,3,2,128,128]{4,3,2,1,0:T(8,128)(2,1)S(1)}, u32[]{:S(2)}, u32[]{:S(2)}) collective-permute-start(bf16[1,3,2,128,128]{4,3,2,1,0:T(8,128)(2,1)S(1)} %get-tuple-element.95), channel_id=1, source_target_pairs={{0,14},{1,15},{2,0},{3,1},{4,2},{5,3},{6,4},{7,5},{8,6},{9,7},{10,... | collective-permute-start | bytes 589832 | tf_op jit(solution)/shard_map/ppermute | solution.py:158
  483.4 17.9 %collective-permute-start.29 = (bf16[1,3,2,128,128]{4,3,2,1,0:T(8,128)(2,1)S(1)}, bf16[1,3,2,128,128]{4,3,2,1,0:T(8,128)(2,1)S(1)}, u32[]{:S(2)}, u32[]{:S(2)}) collective-permute-start(bf16[1,3,2,128,128]{4,3,2,1,0:T(8,128)(2,1)S(1)} %get-tuple-element.94), channel_id=1, source_target_pairs={{0,15},{1,0},{2,1},{3,2},{4,3},{5,4},{6,5},{7,6},{8,7},{9,8},{10,9... | collective-permute-start | bytes 589832 | tf_op jit(solution)/shard_map/ppermute | solution.py:158
  (42 other events, 527.1 us)

commit v10 on v8

--- a/solution.py
+++ b/solution.py
@@ -104,7 +104,7 @@
 
 def to_owners(inputs, page, seq_size, per_dev, head_width):
     page_count, tok_rows, feature_width = inputs[0].shape
-    groups = max(1, 8 // per_dev)
+    groups = max(1, seq_size // 2)
     while seq_size % groups:
         groups //= 2
     width = groups * per_dev * head_width
@@ -131,7 +131,7 @@
 def from_owners(returned, results, page, per_dev, head_width):
     seq_size = returned.shape[0]
     page_count, tok_rows, feature_width = results[0].shape
-    groups = max(1, 8 // per_dev)
+    groups = max(1, seq_size // 2)
     while seq_size % groups:
         groups //= 2
     width = groups * per_dev * head_width

time: 359 us -> 356 us (level)
  Pallas kernels: 71.3 us -> 67.2 us
where the time goes in v10:
time: 356 us; the launch traced here: 355 us
  waiting for transfers between devices  222 us (62%)
  Pallas kernels  67.2 us (19%)
  local copies, waits for them, and re-layouts  38.5 us (11%)
  starting transfers between devices  20.9 us (6%)
  other arithmetic  6.02 us (2%)
    all_to_all x2, waiting for transfers between devices, body(): lax.all_to_all(part, 'seq', split_axis=0, concat_axis=0, tiled=True)  136 us
    all_to_all x2, waiting for transfers between devices, body(): lax.all_to_all(grads, 'seq', split_axis=0, concat_axis=0, tiled=True)  86.4 us
    pallas_call x4, Pallas kernels, item_gradients(): pl.pallas_call(_kernel, out_shape=(out_t, out, out), scratch_shapes=[pltp...  52.4 us
    unnamed x42, local copies, waits for them, and re-layouts  17.5 us
    all_to_all x2, starting transfers between devices, body(): lax.all_to_all(part, 'seq', split_axis=0, concat_axis=0, tiled=True)  11.3 us
    all_to_all x2, starting transfers between devices, body(): lax.all_to_all(grads, 'seq', split_axis=0, concat_axis=0, tiled=True)  9.56 us
    pallas_call x2, Pallas kernels, to_owners(): pl.pallas_call(functools.partial(_gather_kernel, groups=groups, per_dev=p...  7.78 us
  transfers between devices with their start and end apart: 4, of which 4 were waited for; matrix products, arithmetic and copies ran while one was open for 8% of the time, Pallas kernels for 17%

profile of v10, /device:TPU:13, one launch (start us, length us, event | category | flops | bytes accessed | tf_op | source)
XLA Modules:
  0.0 355.3 jit_solution(3993010440580423529)
XLA Ops:
  0.6 3.9 %shard_map.70 = bf16[16,4,2,128,128]{4,3,2,1,0:T(8,128)(2,1)} custom-call(bf16[2,128,4096]{2,1,0:T(8,128)(2,1)} %refs_0_.3, bf16[2,128,4096]{2,1,0:T(8,128)(2,1)} %refs_1_.3, bf16[2,128,4096]{2,1,0:T(8,128)(2,1)} %refs_2_.3, bf16[2,128,4096]{2,1,0:T(8,128)(2,1)} %refs_3_.3), custom_call_target="tpu_custom_call" | custom-call | tf_op jit(solution)/shard_map/pallas_call | solution.py:113
  4.5 6.5 %all-to-all-start.2 = ((bf16[16,4,2,128,128]{4,3,2,1,0:T(8,128)(2,1)}), bf16[16,4,2,128,128]{4,3,2,1,0:T(8,128)(2,1)}, u32[]{:S(2)}, u32[]{:S(2)}) async-start(bf16[16,4,2,128,128]{4,3,2,1,0:T(8,128)(2,1)} %shard_map.70), calls=%async_computation.2 | async-start | bytes 8388608 | tf_op jit(solution)/shard_map/all_to_all | solution.py:161
  11.0 3.9 %shard_map.67 = bf16[16,4,2,128,128]{4,3,2,1,0:T(8,128)(2,1)} custom-call(bf16[2,128,4096]{2,1,0:T(8,128)(2,1)} %refs_0_.3, bf16[2,128,4096]{2,1,0:T(8,128)(2,1)} %refs_1_.3, bf16[2,128,4096]{2,1,0:T(8,128)(2,1)} %refs_2_.3, bf16[2,128,4096]{2,1,0:T(8,128)(2,1)} %refs_3_.3), custom_call_target="tpu_custom_call" | custom-call | tf_op jit(solution)/shard_map/pallas_call | solution.py:113
  14.9 88.5 %all-to-all-done.2 = bf16[16,4,2,128,128]{4,3,2,1,0:T(8,128)(2,1)} async-done(((bf16[16,4,2,128,128]{4,3,2,1,0:T(8,128)(2,1)}), bf16[16,4,2,128,128]{4,3,2,1,0:T(8,128)(2,1)}, u32[]{:S(2)}, u32[]{:S(2)}) %all-to-all-start.2) | async-done | bytes 4194336 | tf_op jit(solution)/shard_map/all_to_all | solution.py:161
  103.5 4.8 %all-to-all-start = ((bf16[16,4,2,128,128]{4,3,2,1,0:T(8,128)(2,1)}), bf16[16,4,2,128,128]{4,3,2,1,0:T(8,128)(2,1)}, u32[]{:S(2)}, u32[]{:S(2)}) async-start(bf16[16,4,2,128,128]{4,3,2,1,0:T(8,128)(2,1)} %shard_map.67), calls=%async_computation | async-start | bytes 8388608 | tf_op jit(solution)/shard_map/all_to_all | solution.py:161
  108.3 3.5 fusion
  111.8 1.0 copy.28
  112.8 1.0 copy-done
  113.9 1.0 copy-done.1
  114.9 1.0 copy-done.4
  115.9 13.1 %shard_map.72 = (bf16[128,2048]{1,0:T(8,128)(2,1)S(1)}, bf16[2048,128]{1,0:T(8,128)(2,1)S(1)}, bf16[2048,128]{1,0:T(8,128)(2,1)S(1)}) custom-call(bf16[2048,128]{1,0:T(8,128)(2,1)S(1)} %bitcast.56, bf16[2048,128]{1,0:T(8,128)(2,1)S(1)} %bitcast.45, bf16[128,2048]{1,0:T(8,128)(2,1)S(1)} %bitcast.62, bf16[2048,128]{1,0:T(8,128)(2,1)S(1)} %bitcast.55, ...), custom_call_target="tpu_custom_call" | custom-call | tf_op jit(solution)/shard_map/pallas_call | solution.py:82
  129.1 0.8 copy-done.6
  129.9 0.8 copy-done.8
  130.7 0.8 copy-done.16
  131.4 2.1 copy.24
  133.8 13.1 %shard_map.71 = (bf16[128,2048]{1,0:T(8,128)(2,1)S(1)}, bf16[2048,128]{1,0:T(8,128)(2,1)S(1)}, bf16[2048,128]{1,0:T(8,128)(2,1)S(1)}) custom-call(bf16[2048,128]{1,0:T(8,128)(2,1)S(1)} %bitcast.50, bf16[2048,128]{1,0:T(8,128)(2,1)S(1)} %bitcast.41, bf16[128,2048]{1,0:T(8,128)(2,1)S(1)} %bitcast.60, bf16[2048,128]{1,0:T(8,128)(2,1)S(1)} %bitcast.49, ...), custom_call_target="tpu_custom_call" | custom-call | tf_op jit(solution)/shard_map/pallas_call | solution.py:82
  146.9 0.8 copy-done.12
  147.7 0.8 copy-done.13
  148.5 0.8 copy-done.17
  149.3 1.3 copy.21
  150.7 3.0 maximum_bitcast_fusion.1
  153.7 47.1 %all-to-all-done = bf16[16,4,2,128,128]{4,3,2,1,0:T(8,128)(2,1)} async-done(((bf16[16,4,2,128,128]{4,3,2,1,0:T(8,128)(2,1)}), bf16[16,4,2,128,128]{4,3,2,1,0:T(8,128)(2,1)}, u32[]{:S(2)}, u32[]{:S(2)}) %all-to-all-start) | async-done | bytes 4194336 | tf_op jit(solution)/shard_map/all_to_all | solution.py:161
  200.7 4.8 %all-to-all-start.3 = ((bf16[16,3,2,128,128]{4,3,2,1,0:T(8,128)(2,1)}), bf16[16,3,2,128,128]{4,3,2,1,0:T(8,128)(2,1)}, u32[]{:S(2)}, u32[]{:S(2)}) async-start(bf16[16,3,2,128,128]{4,3,2,1,0:T(8,128)(2,1)} %maximum_bitcast_fusion.1), calls=%async_computation.3 | async-start | bytes 6291456 | tf_op jit(solution)/shard_map/all_to_all | solution.py:168
  205.5 3.5 fusion.1
  209.1 1.0 copy.26
  210.1 1.0 copy-done.2
  211.1 1.0 copy-done.3
  212.1 1.0 copy-done.5
  213.2 13.1 %shard_map.69 = (bf16[128,2048]{1,0:T(8,128)(2,1)S(1)}, bf16[2048,128]{1,0:T(8,128)(2,1)S(1)}, bf16[2048,128]{1,0:T(8,128)(2,1)S(1)}) custom-call(bf16[2048,128]{1,0:T(8,128)(2,1)S(1)} %bitcast.59, bf16[2048,128]{1,0:T(8,128)(2,1)S(1)} %bitcast.47, bf16[128,2048]{1,0:T(8,128)(2,1)S(1)} %bitcast.63, bf16[2048,128]{1,0:T(8,128)(2,1)S(1)} %bitcast.58, ...), custom_call_target="tpu_custom_call" | custom-call | tf_op jit(solution)/shard_map/pallas_call | solution.py:82
  226.3 0.8 copy-done.9
  227.1 0.8 copy-done.11
  227.9 0.8 copy-done.18
  228.7 2.1 copy.18
  231.0 13.1 %shard_map.68 = (bf16[128,2048]{1,0:T(8,128)(2,1)S(1)}, bf16[2048,128]{1,0:T(8,128)(2,1)S(1)}, bf16[2048,128]{1,0:T(8,128)(2,1)S(1)}) custom-call(bf16[2048,128]{1,0:T(8,128)(2,1)S(1)} %bitcast.53, bf16[2048,128]{1,0:T(8,128)(2,1)S(1)} %bitcast.43, bf16[128,2048]{1,0:T(8,128)(2,1)S(1)} %bitcast.61, bf16[2048,128]{1,0:T(8,128)(2,1)S(1)} %bitcast.52, ...), custom_call_target="tpu_custom_call" | custom-call | tf_op jit(solution)/shard_map/pallas_call | solution.py:82
  244.1 0.8 copy-done.14
  244.9 0.8 copy-done.15
  245.7 0.8 copy-done.19
  246.5 1.3 copy.15
  247.9 3.0 maximum_bitcast_fusion
  250.9 24.6 %all-to-all-done.3.ret_ref = bf16[16,3,2,128,128]{4,3,2,1,0:T(8,128)(2,1)} async-done(((bf16[16,3,2,128,128]{4,3,2,1,0:T(8,128)(2,1)}), bf16[16,3,2,128,128]{4,3,2,1,0:T(8,128)(2,1)}, u32[]{:S(2)}, u32[]{:S(2)}) %all-to-all-start.3) | async-done | bytes 3145760 | tf_op jit(solution)/shard_map/all_to_all | solution.py:168
  275.5 4.8 %all-to-all-start.1 = ((bf16[16,3,2,128,128]{4,3,2,1,0:T(8,128)(2,1)}), bf16[16,3,2,128,128]{4,3,2,1,0:T(8,128)(2,1)S(1)}, u32[]{:S(2)}, u32[]{:S(2)}) async-start(bf16[16,3,2,128,128]{4,3,2,1,0:T(8,128)(2,1)} %maximum_bitcast_fusion), calls=%async_computation.1 | async-start | bytes 6291456 | tf_op jit(solution)/shard_map/all_to_all | solution.py:168
  280.3 1.6 broadcast_1_a_in_b_in_c_in.2.clone.1.c_in
  281.8 1.6 broadcast_1_a_in_b_in_c_in.2.clone.b_in
  283.4 1.6 broadcast_1_a_in_b_in_c_in.2.a_in
  285.0 3.5 shard_map.73
  288.4 61.7 %all-to-all-done.1.ret_ref = bf16[16,3,2,128,128]{4,3,2,1,0:T(8,128)(2,1)S(1)} async-done(((bf16[16,3,2,128,128]{4,3,2,1,0:T(8,128)(2,1)}), bf16[16,3,2,128,128]{4,3,2,1,0:T(8,128)(2,1)S(1)}, u32[]{:S(2)}, u32[]{:S(2)}) %all-to-all-start.1) | async-done | bytes 3145760 | tf_op jit(solution)/shard_map/all_to_all | solution.py:168
  350.2 1.6 copy-done.20
  351.8 3.5 shard_map.74
  (25 shorter events, 0.5 us)
Async XLA Ops:
  4.5 99.0 %all-to-all-start.2 = ((bf16[16,4,2,128,128]{4,3,2,1,0:T(8,128)(2,1)}), bf16[16,4,2,128,128]{4,3,2,1,0:T(8,128)(2,1)}, u32[]{:S(2)}, u32[]{:S(2)}) async-start(bf16[16,4,2,128,128]{4,3,2,1,0:T(8,128)(2,1)} %shard_map.70), calls=%async_computation.2 | async-start | bytes 8388608 | tf_op jit(solution)/shard_map/all_to_all | solution.py:161
  103.5 97.2 %all-to-all-start = ((bf16[16,4,2,128,128]{4,3,2,1,0:T(8,128)(2,1)}), bf16[16,4,2,128,128]{4,3,2,1,0:T(8,128)(2,1)}, u32[]{:S(2)}, u32[]{:S(2)}) async-start(bf16[16,4,2,128,128]{4,3,2,1,0:T(8,128)(2,1)} %shard_map.67), calls=%async_computation | async-start | bytes 8388608 | tf_op jit(solution)/shard_map/all_to_all | solution.py:161
  112.8 1.0 copy-start
  113.9 1.0 copy-start.1
  114.9 1.0 copy-start.4
  129.1 0.8 copy-start.6
  129.9 0.8 copy-start.8
  130.7 0.8 copy-start.16
  131.4 19.2 %copy-start.7 = (bf16[2048,128]{1,0:T(8,128)(2,1)S(1)}, bf16[2048,128]{1,0:T(8,128)(2,1)}, u32[]{:S(2)}) copy-start(bf16[2048,128]{1,0:T(8,128)(2,1)} %copy-done.6) | copy-start | bytes 1572868
  146.9 0.8 copy-start.12
  147.7 0.8 copy-start.13
  148.5 0.8 copy-start.17
  200.7 74.8 %all-to-all-start.3 = ((bf16[16,3,2,128,128]{4,3,2,1,0:T(8,128)(2,1)}), bf16[16,3,2,128,128]{4,3,2,1,0:T(8,128)(2,1)}, u32[]{:S(2)}, u32[]{:S(2)}) async-start(bf16[16,3,2,128,128]{4,3,2,1,0:T(8,128)(2,1)} %maximum_bitcast_fusion.1), calls=%async_computation.3 | async-start | bytes 6291456 | tf_op jit(solution)/shard_map/all_to_all | solution.py:168
  210.1 1.0 copy-start.2
  211.1 1.0 copy-start.3
  212.1 1.0 copy-start.5
  226.3 0.8 copy-start.9
  227.1 0.8 copy-start.11
  227.9 0.8 copy-start.18
  228.7 19.2 %copy-start.10 = (bf16[2048,128]{1,0:T(8,128)(2,1)S(1)}, bf16[2048,128]{1,0:T(8,128)(2,1)}, u32[]{:S(2)}) copy-start(bf16[2048,128]{1,0:T(8,128)(2,1)} %copy-done.9) | copy-start | bytes 1572868
  244.1 0.8 copy-start.14
  244.9 0.8 copy-start.15
  245.7 0.8 copy-start.19
  275.5 74.7 %all-to-all-start.1 = ((bf16[16,3,2,128,128]{4,3,2,1,0:T(8,128)(2,1)}), bf16[16,3,2,128,128]{4,3,2,1,0:T(8,128)(2,1)S(1)}, u32[]{:S(2)}, u32[]{:S(2)}) async-start(bf16[16,3,2,128,128]{4,3,2,1,0:T(8,128)(2,1)} %maximum_bitcast_fusion), calls=%async_computation.1 | async-start | bytes 6291456 | tf_op jit(solution)/shard_map/all_to_all | solution.py:168
  350.2 1.6 copy-start.20

commit v11 on v10

--- a/solution.py
+++ b/solution.py
@@ -11,9 +11,11 @@
 BLOCK = 512
 
 
-def _kernel(q_ref, k_ref, kt_ref, v_ref, do_ref, dqt_ref, dk_ref, dv_ref, s_scr, dp_scr, dk_acc, dv_acc):
-    tokens_all, head_width = q_ref.shape
+def _kernel(q_ref, k_ref, v_ref, do_ref, dq_ref, dk_ref, dv_ref, s_scr, dp_scr, dk_acc, dv_acc, kt_scr):
+    owners, tok_rows, head_width = q_ref.shape
+    tokens_all = owners * tok_rows
     blk = BLOCK
+    per_blk = blk // tok_rows
     scale = head_width ** (-0.5)
     dk_acc[...] = jnp.zeros_like(dk_acc)
     dv_acc[...] = jnp.zeros_like(dv_acc)
@@ -21,14 +23,24 @@
     key_ids = lax.broadcasted_iota(jnp.int32, (blk, blk), 0)
     query_ids = lax.broadcasted_iota(jnp.int32, (blk, blk), 1)
 
+    def rows(ref, j):
+        o0 = pl.multiple_of(j * per_blk, per_blk)
+        return ref[pl.ds(o0, per_blk)].reshape(blk, head_width)
+
+    def fill_kt(j, carry):
+        c0 = pl.multiple_of(j * blk, blk)
+        kt_scr[:, pl.ds(c0, blk)] = rows(k_ref, j).T
+        return carry
+
+    lax.fori_loop(0, tokens_all // blk, fill_kt, 0)
+
     def query_block(i, carry):
-        r0 = pl.multiple_of(i * blk, blk)
-        q = q_ref[pl.ds(r0, blk), :]
-        do = do_ref[pl.ds(r0, blk), :]
+        q = rows(q_ref, i)
+        do = rows(do_ref, i)
 
         def scores(j, masked):
             c0 = pl.multiple_of(j * blk, blk)
-            s = lax.dot_general(k_ref[pl.ds(c0, blk), :], q, contract_cols,
+            s = lax.dot_general(rows(k_ref, j), q, contract_cols,
                                 preferred_element_type=jnp.float32) * scale
             if masked:
                 s = jnp.where(query_ids >= key_ids, s, -jnp.inf)
@@ -44,7 +56,7 @@
             total, weighted = sums
             c0 = pl.multiple_of(j * blk, blk)
             w = jnp.exp(s_scr[pl.ds(c0, blk), :] - top)
-            dp = lax.dot_general(v_ref[pl.ds(c0, blk), :], do, contract_cols,
+            dp = lax.dot_general(rows(v_ref, j), do, contract_cols,
                                  preferred_element_type=jnp.float32)
             s_scr[pl.ds(c0, blk), :] = w
             dp_scr[pl.ds(c0, blk), :] = dp
@@ -60,14 +72,15 @@
             c0 = pl.multiple_of(j * blk, blk)
             p = s_scr[pl.ds(c0, blk), :] * inv_total
             ds = (p * (dp_scr[pl.ds(c0, blk), :] - delta)).astype(jnp.bfloat16)
-            dqt = dqt + jnp.dot(kt_ref[:, pl.ds(c0, blk)], ds, preferred_element_type=jnp.float32)
+            dqt = dqt + jnp.dot(kt_scr[:, pl.ds(c0, blk)], ds, preferred_element_type=jnp.float32)
             dk_acc[pl.ds(c0, blk), :] += jnp.dot(ds, q, preferred_element_type=jnp.float32)
             dv_acc[pl.ds(c0, blk), :] += jnp.dot(
                 p.astype(jnp.bfloat16), do, preferred_element_type=jnp.float32)
             return dqt
 
         dqt = lax.fori_loop(0, i + 1, grads_pass, jnp.zeros((head_width, blk), jnp.float32))
-        dqt_ref[:, pl.ds(r0, blk)] = (dqt * scale).astype(dqt_ref.dtype)
+        r0 = pl.multiple_of(i * blk, blk)
+        dq_ref[pl.ds(r0, blk), :] = (dqt * scale).T.astype(dq_ref.dtype)
         return carry
 
     lax.fori_loop(0, tokens_all // blk, query_block, 0)
@@ -75,22 +88,30 @@
     dv_ref[...] = dv_acc[...].astype(dv_ref.dtype)
 
 
-def item_gradients(queries, key_vectors, value_vectors, out_grad):
-    tokens_all, head_width = queries.shape
+def item_gradients(arrived, head):
+    owners, _, _, tok_rows, head_width = arrived.shape
+    tokens_all = owners * tok_rows
     out = jax.ShapeDtypeStruct((tokens_all, head_width), jnp.bfloat16)
-    out_t = jax.ShapeDtypeStruct((head_width, tokens_all), jnp.bfloat16)
-    dqt, dk, dv = pl.pallas_call(
+    specs = [
+        pl.BlockSpec((owners, None, None, tok_rows, head_width),
+                     functools.partial(lambda a, i: (0, a, head, 0, 0), a))
+        for a in range(4)
+    ]
+    return pl.pallas_call(
         _kernel,
-        out_shape=(out_t, out, out),
+        grid=(1,),
+        in_specs=specs,
+        out_specs=[pl.BlockSpec((tokens_all, head_width), lambda i: (0, 0))] * 3,
+        out_shape=(out, out, out),
         scratch_shapes=[
             pltpu.VMEM((tokens_all, BLOCK), jnp.float32),
             pltpu.VMEM((tokens_all, BLOCK), jnp.float32),
             pltpu.VMEM((tokens_all, head_width), jnp.float32),
             pltpu.VMEM((tokens_all, head_width), jnp.float32),
+            pltpu.VMEM((head_width, tokens_all), jnp.bfloat16),
         ],
-        compiler_params=pltpu.CompilerParams(vmem_limit_bytes=32 * 1024 * 1024),
-    )(queries, key_vectors, key_vectors.T, value_vectors, out_grad)
-    return dqt.T, dk, dv
+        compiler_params=pltpu.CompilerParams(vmem_limit_bytes=40 * 1024 * 1024),
+    )(arrived, arrived, arrived, arrived)
 
 
 def _gather_kernel(*refs, groups, per_dev, head_width):
@@ -161,8 +182,7 @@
         arrived = lax.all_to_all(part, "seq", split_axis=0, concat_axis=0, tiled=True)
         grads = []
         for head in range(per_dev):
-            items = [arrived[:, a, head].reshape(tokens_all, head_width) for a in range(4)]
-            grads.append(jnp.stack(item_gradients(*items)))
+            grads.append(jnp.stack(item_gradients(arrived, head)))
         grads = jnp.stack(grads).reshape(per_dev, 3, seq_size, tok_rows, head_width)
         grads = grads.transpose(2, 1, 0, 3, 4)
         returned = lax.all_to_all(grads, "seq", split_axis=0, concat_axis=0, tiled=True)

time: 356 us -> 356 us (level)
  local copies, waits for them, and re-layouts: 38.5 us -> 6.39 us
  waiting for transfers between devices: 222 us -> 248 us
  Pallas kernels: 67.2 us -> 76 us
    unnamed x42 -> x2, local copies, waits for them, and re-layouts: 17.5 us -> 1.72 us
    all_to_all x2, waiting for transfers between devices: 136 us -> 148 us  [body(): lax.all_to_all(part, 'seq', split_axis=0, concat_axis=0, tiled=True)]
    all_to_all x2, waiting for transfers between devices: 86.4 us -> 99.2 us  [body(): lax.all_to_all(grads, 'seq', split_axis=0, concat_axis=0, tiled=True)]
    pallas_call x4, Pallas kernels: 52.4 us -> 61.4 us  [item_gradients(): pl.pallas_call(_kernel, grid=(1,), in_specs=specs, out_specs=[pl.BlockSpe...]
    slice x2 -> x0, local copies, waits for them, and re-layouts: 7.09 us -> none  [body(): arrived[:, a, head].reshape(tokens_all, head_width)]
    transpose x4 -> x0, local copies, waits for them, and re-layouts: 6.8 us -> none  [item_gradients(): return (dqt.T, dk, dv)]
  transfers between devices with their start and end apart: 4 -> 4, of which waited for: 4 -> 4; matrix products, arithmetic and copies ran while one was open for 8% -> 2% of each run, Pallas kernels for 17% -> 19%
where the time goes in v11:
time: 356 us; the launch traced here: 355 us
  waiting for transfers between devices  248 us (70%)
  Pallas kernels  76 us (21%)
  starting transfers between devices  20.9 us (6%)
  local copies, waits for them, and re-layouts  6.39 us (2%)
  other arithmetic  3.73 us (1%)
    all_to_all x2, waiting for transfers between devices, body(): lax.all_to_all(part, 'seq', split_axis=0, concat_axis=0, tiled=True)  148 us
    all_to_all x2, waiting for transfers between devices, body(): lax.all_to_all(grads, 'seq', split_axis=0, concat_axis=0, tiled=True)  99.2 us
    pallas_call x4, Pallas kernels, item_gradients(): pl.pallas_call(_kernel, grid=(1,), in_specs=specs, out_specs=[pl.BlockSpe...  61.4 us
    all_to_all x2, starting transfers between devices, body(): lax.all_to_all(part, 'seq', split_axis=0, concat_axis=0, tiled=True)  11.3 us
    all_to_all x2, starting transfers between devices, body(): lax.all_to_all(grads, 'seq', split_axis=0, concat_axis=0, tiled=True)  9.56 us
    pallas_call x2, Pallas kernels, to_owners(): pl.pallas_call(functools.partial(_gather_kernel, groups=groups, per_dev=p...  7.72 us
  transfers between devices with their start and end apart: 4, of which 4 were waited for; matrix products, arithmetic and copies ran while one was open for 2% of the time, Pallas kernels for 19%

profile of v11, /device:TPU:13, one launch (start us, length us, event | category | flops | bytes accessed | tf_op | source)
XLA Modules:
  0.0 355.4 jit_solution(7463619996631430773)
XLA Ops:
  0.6 3.9 %shard_map.70 = bf16[16,4,2,128,128]{4,3,2,1,0:T(8,128)(2,1)} custom-call(bf16[2,128,4096]{2,1,0:T(8,128)(2,1)} %refs_0_.3, bf16[2,128,4096]{2,1,0:T(8,128)(2,1)} %refs_1_.3, bf16[2,128,4096]{2,1,0:T(8,128)(2,1)} %refs_2_.3, bf16[2,128,4096]{2,1,0:T(8,128)(2,1)} %refs_3_.3), custom_call_target="tpu_custom_call" | custom-call | tf_op jit(solution)/shard_map/pallas_call | solution.py:134
  4.5 6.5 %all-to-all-start.2 = ((bf16[16,4,2,128,128]{4,3,2,1,0:T(8,128)(2,1)}), bf16[16,4,2,128,128]{4,3,2,1,0:T(8,128)(2,1)}, u32[]{:S(2)}, u32[]{:S(2)}) async-start(bf16[16,4,2,128,128]{4,3,2,1,0:T(8,128)(2,1)} %shard_map.70), calls=%async_computation.2 | async-start | bytes 8388608 | tf_op jit(solution)/shard_map/all_to_all | solution.py:182
  11.0 3.8 %shard_map.67 = bf16[16,4,2,128,128]{4,3,2,1,0:T(8,128)(2,1)} custom-call(bf16[2,128,4096]{2,1,0:T(8,128)(2,1)} %refs_0_.3, bf16[2,128,4096]{2,1,0:T(8,128)(2,1)} %refs_1_.3, bf16[2,128,4096]{2,1,0:T(8,128)(2,1)} %refs_2_.3, bf16[2,128,4096]{2,1,0:T(8,128)(2,1)} %refs_3_.3), custom_call_target="tpu_custom_call" | custom-call | tf_op jit(solution)/shard_map/pallas_call | solution.py:134
  14.9 88.6 %all-to-all-done.2.q_ref.k_ref.v_ref.do_ref = bf16[16,4,2,128,128]{4,3,2,1,0:T(8,128)(2,1)} async-done(((bf16[16,4,2,128,128]{4,3,2,1,0:T(8,128)(2,1)}), bf16[16,4,2,128,128]{4,3,2,1,0:T(8,128)(2,1)}, u32[]{:S(2)}, u32[]{:S(2)}) %all-to-all-start.2) | async-done | bytes 4194336 | tf_op jit(solution)/shard_map/all_to_all | solution.py:182
  103.5 4.8 %all-to-all-start = ((bf16[16,4,2,128,128]{4,3,2,1,0:T(8,128)(2,1)}), bf16[16,4,2,128,128]{4,3,2,1,0:T(8,128)(2,1)}, u32[]{:S(2)}, u32[]{:S(2)}) async-start(bf16[16,4,2,128,128]{4,3,2,1,0:T(8,128)(2,1)} %shard_map.67), calls=%async_computation | async-start | bytes 8388608 | tf_op jit(solution)/shard_map/all_to_all | solution.py:182
  108.3 15.3 %shard_map.72 = (bf16[2048,128]{1,0:T(8,128)(2,1)S(1)}, bf16[2048,128]{1,0:T(8,128)(2,1)S(1)}, bf16[2048,128]{1,0:T(8,128)(2,1)S(1)}) custom-call(bf16[16,4,2,128,128]{4,3,2,1,0:T(8,128)(2,1)} %all-to-all-done.2.q_ref.k_ref.v_ref.do_ref, bf16[16,4,2,128,128]{4,3,2,1,0:T(8,128)(2,1)} %all-to-all-done.2.q_ref.k_ref.v_ref.do_ref, ...), custom_call_target="tpu_custom_call" | custom-call | tf_op jit(solution)/shard_map/pallas_call | solution.py:100
  123.6 15.4 %shard_map.71 = (bf16[2048,128]{1,0:T(8,128)(2,1)S(1)}, bf16[2048,128]{1,0:T(8,128)(2,1)S(1)}, bf16[2048,128]{1,0:T(8,128)(2,1)S(1)}) custom-call(bf16[16,4,2,128,128]{4,3,2,1,0:T(8,128)(2,1)} %all-to-all-done.2.q_ref.k_ref.v_ref.do_ref, bf16[16,4,2,128,128]{4,3,2,1,0:T(8,128)(2,1)} %all-to-all-done.2.q_ref.k_ref.v_ref.do_ref, ...), custom_call_target="tpu_custom_call" | custom-call | tf_op jit(solution)/shard_map/pallas_call | solution.py:100
  139.0 1.9 maximum_bitcast_fusion.1
  140.9 59.9 %all-to-all-done.q_ref.k_ref.v_ref.do_ref = bf16[16,4,2,128,128]{4,3,2,1,0:T(8,128)(2,1)} async-done(((bf16[16,4,2,128,128]{4,3,2,1,0:T(8,128)(2,1)}), bf16[16,4,2,128,128]{4,3,2,1,0:T(8,128)(2,1)}, u32[]{:S(2)}, u32[]{:S(2)}) %all-to-all-start) | async-done | bytes 4194336 | tf_op jit(solution)/shard_map/all_to_all | solution.py:182
  200.7 4.8 %all-to-all-start.3 = ((bf16[16,3,2,128,128]{4,3,2,1,0:T(8,128)(2,1)}), bf16[16,3,2,128,128]{4,3,2,1,0:T(8,128)(2,1)S(1)}, u32[]{:S(2)}, u32[]{:S(2)}) async-start(bf16[16,3,2,128,128]{4,3,2,1,0:T(8,128)(2,1)} %maximum_bitcast_fusion.1), calls=%async_computation.3 | async-start | bytes 6291456 | tf_op jit(solution)/shard_map/all_to_all | solution.py:188
  205.5 15.3 %shard_map.69 = (bf16[2048,128]{1,0:T(8,128)(2,1)S(1)}, bf16[2048,128]{1,0:T(8,128)(2,1)S(1)}, bf16[2048,128]{1,0:T(8,128)(2,1)S(1)}) custom-call(bf16[16,4,2,128,128]{4,3,2,1,0:T(8,128)(2,1)} %all-to-all-done.q_ref.k_ref.v_ref.do_ref, bf16[16,4,2,128,128]{4,3,2,1,0:T(8,128)(2,1)} %all-to-all-done.q_ref.k_ref.v_ref.do_ref, ...), custom_call_target="tpu_custom_call" | custom-call | tf_op jit(solution)/shard_map/pallas_call | solution.py:100
  220.9 15.4 %shard_map.68 = (bf16[2048,128]{1,0:T(8,128)(2,1)S(1)}, bf16[2048,128]{1,0:T(8,128)(2,1)S(1)}, bf16[2048,128]{1,0:T(8,128)(2,1)S(1)}) custom-call(bf16[16,4,2,128,128]{4,3,2,1,0:T(8,128)(2,1)} %all-to-all-done.q_ref.k_ref.v_ref.do_ref, bf16[16,4,2,128,128]{4,3,2,1,0:T(8,128)(2,1)} %all-to-all-done.q_ref.k_ref.v_ref.do_ref, ...), custom_call_target="tpu_custom_call" | custom-call | tf_op jit(solution)/shard_map/pallas_call | solution.py:100
  236.2 1.8 maximum_bitcast_fusion
  238.1 37.3 %all-to-all-done.3.ret_ref = bf16[16,3,2,128,128]{4,3,2,1,0:T(8,128)(2,1)S(1)} async-done(((bf16[16,3,2,128,128]{4,3,2,1,0:T(8,128)(2,1)}), bf16[16,3,2,128,128]{4,3,2,1,0:T(8,128)(2,1)S(1)}, u32[]{:S(2)}, u32[]{:S(2)}) %all-to-all-start.3) | async-done | bytes 3145760 | tf_op jit(solution)/shard_map/all_to_all | solution.py:188
  275.4 0.0 copy-start
  275.4 1.7 copy-done
  277.1 4.8 %all-to-all-start.1 = ((bf16[16,3,2,128,128]{4,3,2,1,0:T(8,128)(2,1)}), bf16[16,3,2,128,128]{4,3,2,1,0:T(8,128)(2,1)}, u32[]{:S(2)}, u32[]{:S(2)}) async-start(bf16[16,3,2,128,128]{4,3,2,1,0:T(8,128)(2,1)} %maximum_bitcast_fusion), calls=%async_computation.1 | async-start | bytes 6291456 | tf_op jit(solution)/shard_map/all_to_all | solution.py:188
  281.9 1.6 broadcast_1_a_in_b_in_c_in.2.clone.1.c_in
  283.5 1.6 broadcast_1_a_in_b_in_c_in.2.clone.b_in
  285.0 1.6 broadcast_1_a_in_b_in_c_in.2.a_in
  286.6 3.5 shard_map.73
  290.1 61.9 %all-to-all-done.1.ret_ref = bf16[16,3,2,128,128]{4,3,2,1,0:T(8,128)(2,1)} async-done(((bf16[16,3,2,128,128]{4,3,2,1,0:T(8,128)(2,1)}), bf16[16,3,2,128,128]{4,3,2,1,0:T(8,128)(2,1)}, u32[]{:S(2)}, u32[]{:S(2)}) %all-to-all-start.1) | async-done | bytes 3145760 | tf_op jit(solution)/shard_map/all_to_all | solution.py:188
  351.9 3.5 shard_map.74
Async XLA Ops:
  4.5 99.0 %all-to-all-start.2 = ((bf16[16,4,2,128,128]{4,3,2,1,0:T(8,128)(2,1)}), bf16[16,4,2,128,128]{4,3,2,1,0:T(8,128)(2,1)}, u32[]{:S(2)}, u32[]{:S(2)}) async-start(bf16[16,4,2,128,128]{4,3,2,1,0:T(8,128)(2,1)} %shard_map.70), calls=%async_computation.2 | async-start | bytes 8388608 | tf_op jit(solution)/shard_map/all_to_all | solution.py:182
  103.5 97.2 %all-to-all-start = ((bf16[16,4,2,128,128]{4,3,2,1,0:T(8,128)(2,1)}), bf16[16,4,2,128,128]{4,3,2,1,0:T(8,128)(2,1)}, u32[]{:S(2)}, u32[]{:S(2)}) async-start(bf16[16,4,2,128,128]{4,3,2,1,0:T(8,128)(2,1)} %shard_map.67), calls=%async_computation | async-start | bytes 8388608 | tf_op jit(solution)/shard_map/all_to_all | solution.py:182
  200.7 74.7 %all-to-all-start.3 = ((bf16[16,3,2,128,128]{4,3,2,1,0:T(8,128)(2,1)}), bf16[16,3,2,128,128]{4,3,2,1,0:T(8,128)(2,1)S(1)}, u32[]{:S(2)}, u32[]{:S(2)}) async-start(bf16[16,3,2,128,128]{4,3,2,1,0:T(8,128)(2,1)} %maximum_bitcast_fusion.1), calls=%async_computation.3 | async-start | bytes 6291456 | tf_op jit(solution)/shard_map/all_to_all | solution.py:188
  275.4 1.7 copy-start
  277.1 74.8 %all-to-all-start.1 = ((bf16[16,3,2,128,128]{4,3,2,1,0:T(8,128)(2,1)}), bf16[16,3,2,128,128]{4,3,2,1,0:T(8,128)(2,1)}, u32[]{:S(2)}, u32[]{:S(2)}) async-start(bf16[16,3,2,128,128]{4,3,2,1,0:T(8,128)(2,1)} %maximum_bitcast_fusion), calls=%async_computation.1 | async-start | bytes 6291456 | tf_op jit(solution)/shard_map/all_to_all | solution.py:188
